TPU v7x, 512 devices: a whole 4x8x8 slice. The times are simulated.
512 devices in a mesh: ctx: 128 (over y, z, core), tp: 4 (over x).
Axes of the slice: x: 4, y: 8, z: 8, core: 2. Of those that a mesh axis runs over, the one named last changes fastest.
Arguments:
- hidden_in: bfloat16 [16384, 1536], P('ctx', 'tp'), may hold values from -60 to 60
- queries: bfloat16 [16384, 2048], P('ctx', 'tp'), may hold values from -200 to 200
- rotated_key_value: bfloat16 [16384, 4, 128], P('ctx', 'tp'), may hold values from -5 to 5
- sink_logit_table: float32 [32], P('tp'), may hold values from -2 to 2
- out_proj: bfloat16 [2048, 1536], P('tp', 'ctx'), may hold values from -0.125 to 0.125
- norm_gain: float32 [1536], P('tp'), may hold values from 0.1 to 1.9
- expert_in: bfloat16 [128, 2, 1536, 1536], P('ctx', None, None, 'tp'), may hold values from -0.15625 to 0.15625
- expert_out: bfloat16 [128, 1536, 1536], P('ctx', 'tp'), may hold values from -0.15625 to 0.15625
- routes: int32 [16384, 4], P('ctx'), may hold values from 0 to 127, all different within a row; in each aligned block of 128 rows (0 to 127, 128 to 255, ...) at most 12 rows name the same one
- route_scores: float32 [16384, 4], P('ctx'), may hold values from 0.05 to 1
Outputs:
- layer_out: bfloat16 [16384, 1536], P('ctx', 'tp')
Inputs may be any that keep to these rules, and one draw needn't show every extreme that they name: `routes`: each token names 4 different experts. In every aligned block of 128 tokens (the tokens of one device) no expert is named by more than 12 tokens, a bound that some block reaches.
All inputs are finite; a program needn't handle non-finite values.
Results may differ from a plain program's by a relative error of at most 0.008.
Values may be sent and summed in bfloat16 or wider, within the bound.
No kernel may reach another device: no remote copies, remote signals or barrier semaphores. Data moves between devices by JAX's collectives and lax.ppermute only.
A program may use at most 64 MiB of HBM per device.

v0:
```python
import jax
import jax.numpy as jnp
from jax import lax
from jax.sharding import PartitionSpec as P

WINDOW_KEYS = 128


def shifted(value, axis, steps):
    count = lax.axis_size(axis)
    first, last = (max(0, -steps), min(count, count - steps))
    return lax.ppermute(value, axis, [(source, source + steps) for source in range(first, last)])


def attend(query_block, key_blk, value_blk, inside, sink_row_block, factor):
    score = (
        jnp.einsum("rgqd,sgd->gqrs", query_block, key_blk, preferred_element_type=jnp.float32)
        * factor
    )
    masked = jnp.where(inside, score, -1e30)
    top_score = jnp.maximum(jnp.max(masked, -1), sink_row_block[:, :, None])
    expvals = jnp.where(inside, jnp.exp(score - top_score[..., None]), 0.0)
    denominator = jnp.sum(expvals, -1) + jnp.exp(sink_row_block[:, :, None] - top_score)
    probs = (expvals / denominator[..., None]).astype(jnp.bfloat16)
    mixed = jnp.einsum("gqrs,sgd->rgqd", probs, value_blk, preferred_element_type=jnp.float32)
    return mixed.astype(jnp.bfloat16)


def body(
    hidden_in,
    queries,
    rotated_key_value,
    sink_logit_table,
    out_proj,
    norm_gain,
    expert_in,
    expert_out,
    routes,
    route_scores,
):
    tok_rows = hidden_in.shape[0]
    kv_heads = rotated_key_value.shape[1]
    head_dim = rotated_key_value.shape[2] // 2
    q_heads = sink_logit_table.shape[0]
    queries_per_group = q_heads // kv_heads
    factor = head_dim ** (-0.5)
    sink_row_block = sink_logit_table.reshape(kv_heads, queries_per_group)
    earlier = shifted(rotated_key_value, "ctx", 1)
    keys_all = jnp.concatenate([earlier, rotated_key_value], 0)
    first_pos = lax.axis_index("ctx") * tok_rows
    block_row_count = min(512, tok_rows)
    query_block = queries.reshape(block_row_count, kv_heads, queries_per_group, head_dim)
    query_pos = first_pos + 0 + jnp.arange(block_row_count, dtype=jnp.int32)[:, None]
    key_pos = (
        first_pos
        + 0
        - WINDOW_KEYS
        + jnp.arange(block_row_count + WINDOW_KEYS, dtype=jnp.int32)[None, :]
    )
    inside = (key_pos <= query_pos) & (key_pos > query_pos - WINDOW_KEYS) & (key_pos >= 0)
    mixed = attend(
        query_block,
        keys_all[..., :head_dim],
        keys_all[..., head_dim:],
        inside,
        sink_row_block,
        factor,
    )
    outputs = mixed.reshape(block_row_count, q_heads * head_dim)
    head_partial = jnp.dot(
        outputs,
        lax.all_gather(out_proj, "ctx", axis=1, tiled=True),
        preferred_element_type=jnp.float32,
    )
    d_model = head_partial.shape[1]
    residual = hidden_in.astype(jnp.float32) + lax.psum_scatter(
        head_partial.astype(jnp.bfloat16), "tp", scatter_dimension=1, tiled=True
    ).astype(jnp.float32)
    square_total = lax.psum(jnp.sum(residual * residual, -1), "tp")
    normed = (residual * lax.rsqrt(square_total[:, None] / d_model + 1e-05) * norm_gain).astype(
        jnp.bfloat16
    )
    ctx_count = lax.axis_size("ctx")
    tp_count = lax.axis_size("tp")
    top_count = routes.shape[1]
    experts = ctx_count * expert_in.shape[0]
    capacity = max(2, min(tok_rows, 3 * top_count * tok_rows // experts))
    quarter_w = d_model // tp_count
    onehot = (routes[:, :, None] == jnp.arange(experts, dtype=jnp.int32)).astype(jnp.int32)
    per_tok = jnp.sum(onehot, 1)
    before = jnp.cumsum(per_tok, axis=0) - per_tok
    slot_ids = jnp.sum(onehot * before[:, None, :], -1)
    flat_index = (routes * capacity + slot_ids).reshape(-1)
    weights = route_scores / jnp.sum(route_scores, -1, keepdims=True)
    full_data = lax.all_gather(normed, "tp", axis=1, tiled=True)
    row_width = full_data.shape[1]
    spread = jnp.broadcast_to(full_data[:, None, :], (tok_rows, top_count, row_width)).reshape(
        -1, row_width
    )
    outbox = jnp.zeros((experts * capacity, row_width), jnp.bfloat16).at[flat_index].set(spread)
    arrived = lax.all_to_all(
        outbox.reshape(ctx_count, 1, capacity, row_width),
        "ctx",
        split_axis=0,
        concat_axis=1,
        tiled=True,
    )
    leading = arrived.shape[:3]
    row_data = arrived.reshape(-1, d_model)
    gate_vals = jnp.dot(row_data, expert_in[0, 0], preferred_element_type=jnp.float32)
    up_vals = jnp.dot(row_data, expert_in[0, 1], preferred_element_type=jnp.float32)
    activated = ((up_vals + 1.0) * gate_vals * jax.nn.sigmoid(1.702 * gate_vals)).astype(
        jnp.bfloat16
    )
    partial_value = jnp.dot(activated, expert_out[0], preferred_element_type=jnp.float32).astype(
        jnp.bfloat16
    )
    result = partial_value.reshape(leading + (d_model,))
    returned = lax.all_to_all(result, "ctx", split_axis=1, concat_axis=0, tiled=True)
    picked = returned.reshape(-1, d_model)[flat_index].reshape(tok_rows, top_count, d_model)
    expert_result = lax.psum_scatter(
        picked.astype(jnp.float32).astype(jnp.bfloat16), "tp", scatter_dimension=2, tiled=True
    )
    moe_sum = jnp.zeros((tok_rows, quarter_w), jnp.float32)
    for member in range(top_count):
        moe_sum = moe_sum + weights[:, member : member + 1] * expert_result[:, member].astype(
            jnp.float32
        )
    return (residual + moe_sum).astype(jnp.bfloat16)


def solution(mesh):
    in_specs = (
        P("ctx", "tp"),
        P("ctx", "tp"),
        P("ctx", "tp", None),
        P("tp"),
        P("tp", "ctx"),
        P("tp"),
        P("ctx", None, None, "tp"),
        P("ctx", "tp", None),
        P("ctx", None),
        P("ctx", None),
    )
    out_specs = P("ctx", "tp")
    return jax.shard_map(body, mesh=mesh, in_specs=in_specs, out_specs=out_specs, check_vma=False)
```

profile of v0, /device:TPU:1, one launch (start us, length us, event | category | flops | bytes accessed | tf_op | source)
XLA Modules:
  0.0 596.0 jit_solution(12314358451730001000)
XLA Ops:
  6.5 0.0 copy-start
  6.5 0.0 all-gather.3.cloned.1.call-start
  6.5 0.7 all-gather.3.cloned.1.call-update
  7.3 0.0 reduce-scatter.7.cloned.1.call-start
  7.3 0.9 copy.32
  8.2 5.4 collective-permute-start
  13.6 0.1 and_and_fusion
  13.7 1.0 copy.34
  14.8 2.2 collective-permute-done
  17.0 0.3 select_reduce_fusion
  17.3 0.7 broadcast_maximum_fusion
  18.1 0.2 fusion.14
  18.3 0.0 copy-done.6
  18.3 0.1 exponential_add_fusion
  18.3 0.4 convolution_convert_fusion.2
  18.7 80.7 %all-gather.3.cloned.1.call-done = bf16[128,12,512]{2,1,0:T(8,128)(2,1)} async-done(((bf16[1,12,512]{2,1,0:T(8,128)(2,1)}), bf16[128,12,512]{2,1,0:T(8,128)(2,1)}) %all-gather.3.cloned.1.call-update) | async-done | bytes 1572880 | tf_op jit(solution)/shard_map/all_gather | solution.py:72
  99.4 2.5 reshape.218
  101.9 0.0 copy-start.3
  101.9 0.0 copy-start.2
  101.9 0.0 copy-start.5
  102.0 0.7 convolution_convert_fusion.1
  102.6 0.9 copy.41
  103.5 0.0 reduce-scatter.7.cloned.1.call-update
  103.6 0.0 copy-done.3
  103.6 0.1 convert_reduce_fusion
  103.7 0.2 reduce_window_sum.11
  103.9 0.2 select_reduce_fusion.1
  104.1 0.1 copy.36
  104.3 0.1 reshape.190
  104.4 19.8 %reduce-scatter.7.cloned.1.call-done = bf16[384,128]{1,0:T(8,128)(2,1)} async-done(((bf16[1536,128]{1,0:T(8,128)(2,1)}), bf16[384,128]{1,0:T(8,128)(2,1)}) %reduce-scatter.7.cloned.1.call-update) | async-done | bytes 98320
  124.2 1.0 copy.42
  125.2 0.1 multiply_reduce_fusion
  125.4 6.9 %psum.7 = f32[128]{0:T(128)S(1)} all-reduce(f32[128]{0:T(128)S(1)} %multiply_reduce_fusion), channel_id=1, replica_groups=mesh['ctx'=128,'tp'=4] {'tp'}, use_global_device_ids=true, to_apply=%region_8.9 | all-reduce | flops 128 | bytes 1024 | tf_op jit(solution)/shard_map/psum | solution.py:79
  132.3 0.0 copy-done.5
  132.3 0.1 multiply_convert_fusion
  132.4 10.0 %all_gather.7 = bf16[128,1536]{1,0:T(8,128)(2,1)S(1)} all-gather(bf16[128,384]{1,0:T(8,128)(2,1)S(1)} %multiply_convert_fusion), channel_id=1, replica_groups=mesh['ctx'=128,'tp'=4] {'tp'}, dimensions={1}, use_global_device_ids=true | all-gather | bytes 491520 | tf_op jit(solution)/shard_map/all_gather | solution.py:95
  142.4 0.4 broadcast_in_dim.20
  142.8 1.4 reshape.213
  144.2 6.9 %scatter_custom_fusion = bf16[1536,1536]{1,0:T(8,128)(2,1)} fusion(s32[512]{0:T(512)S(1)} %bitcast.86, bf16[512,1536]{1,0:T(8,128)(2,1)} %reshape.213, bf16[]{:T(256)} %constant.14.clone.1), kind=kCustom, calls=%fused_computation.8 | custom fusion | bytes 4719104 | tf_op jit(solution)/shard_map/scatter | solution.py:100
  151.0 8.1 %reshape.192 = bf16[128,1,12,1536]{3,2,0,1:T(8,128)(2,1)} reshape(bf16[1536,1536]{1,0:T(8,128)(2,1)} %scatter_custom_fusion) | data formatting | bytes 9437184 | tf_op jit(solution)/shard_map/reshape | solution.py:102
  159.1 164.5 %all_to_all.8 = bf16[128,1,12,1536]{3,2,1,0:T(8,128)(2,1)} all-to-all(bf16[128,1,12,1536]{3,2,1,0:T(8,128)(2,1)} %bitcast.77), channel_id=1, replica_groups=mesh['ctx'=128,'tp'=4] {'ctx'}, dimensions={0} | all-to-all | bytes 9437184 | tf_op jit(solution)/shard_map/all_to_all | solution.py:101
  323.6 8.2 %reshape.193 = bf16[1536,1536]{1,0:T(8,128)(2,1)} reshape(bf16[128,1,12,1536]{3,2,1,0:T(8,128)(2,1)} %all_to_all.8) | data formatting | bytes 9437184 | tf_op jit(solution)/shard_map/reshape | solution.py:109
  331.8 6.7 %fusion.7 = f32[1536,384]{1,0:T(8,128)} fusion(bf16[1536,1536]{1,0:T(8,128)(2,1)} %reshape.193, bf16[1,2,1536,384]{3,2,1,0:T(8,128)(2,1)} %param.16), kind=kOutput, calls=%fused_computation.14 | convolution fusion | flops 1811939328 | bytes 8257536 | tf_op jit(solution)/shard_map/dot_general | solution.py:110
  338.5 0.0 copy-done
  338.5 9.1 %convolution_convert_fusion = bf16[1536,1536]{1,0:T(8,128)(2,1)} fusion(bf16[1,384,1536]{2,1,0:T(8,128)(2,1)S(1)} %copy-done, f32[1536,384]{1,0:T(8,128)} %fusion.7, bf16[1536,1536]{1,0:T(8,128)(2,1)} %reshape.193, bf16[1,2,1536,384]{3,2,1,0:T(8,128)(2,1)} %param.16), kind=kOutput, calls=%fused_computation.2 | convolution fusion | flops 3630956544 | bytes 14155776 | tf_op jit(solution)/shard_map/dot_general | solution.py:115
  347.6 8.1 %reshape.194 = bf16[1,128,12,1536]{3,2,1,0:T(8,128)(2,1)} reshape(bf16[1536,1536]{1,0:T(8,128)(2,1)} %convolution_convert_fusion) | data formatting | bytes 9437184 | tf_op jit(solution)/shard_map/reshape | solution.py:118
  355.6 17.5 %all-to-all-start.1 = ((bf16[1,128,12,1536]{3,2,0,1:T(8,128)(2,1)}), bf16[1,128,12,1536]{3,2,0,1:T(8,128)(2,1)}, u32[]{:S(2)}, u32[]{:S(2)}) async-start(bf16[1,128,12,1536]{3,2,0,1:T(8,128)(2,1)} %bitcast.76), calls=%async_computation.1 | async-start | bytes 12582912 | tf_op jit(solution)/shard_map/all_to_all | solution.py:119
  373.2 0.0 reduce-scatter.9.cloned.1.call-start
  373.3 153.9 %all-to-all-done.1 = bf16[1,128,12,1536]{3,2,0,1:T(8,128)(2,1)} async-done(((bf16[1,128,12,1536]{3,2,0,1:T(8,128)(2,1)}), bf16[1,128,12,1536]{3,2,0,1:T(8,128)(2,1)}, u32[]{:S(2)}, u32[]{:S(2)}) %all-to-all-start.1) | async-done | bytes 4718624 | tf_op jit(solution)/shard_map/all_to_all | solution.py:119
  527.2 8.2 %reshape.195 = bf16[1536,1536]{1,0:T(8,128)(2,1)} reshape(bf16[1,128,12,1536]{3,2,0,1:T(8,128)(2,1)} %all-to-all-done.1) | data formatting | bytes 9437184 | tf_op jit(solution)/shard_map/reshape | solution.py:120
  535.4 7.4 %gather_fusion = bf16[512,1536]{1,0:T(8,128)(2,1)} fusion(bf16[1536,1536]{1,0:T(8,128)(2,1)} %reshape.195, s32[1024]{0:T(1024)S(1)} %pad_clamp_fusion), kind=kCustom, calls=%fused_computation | custom fusion | bytes 3147776 | tf_op jit(solution)/shard_map/gather | solution.py:120
  542.7 2.9 reshape.196
  545.6 2.4 copy.43
  548.1 2.8 copy.52
  550.9 0.0 reduce-scatter.9.cloned.1.call-update
  550.9 0.0 copy-start.1
  551.0 35.4 %reduce-scatter.9.cloned.1.call-done = bf16[384,512]{1,0:T(8,128)(2,1)} async-done(((bf16[1536,512]{1,0:T(8,128)(2,1)}), bf16[384,512]{1,0:T(8,128)(2,1)}) %reduce-scatter.9.cloned.1.call-update) | async-done | bytes 393232
  586.4 1.1 reshape.224
  587.5 0.6 fusion.32
  588.1 0.1 copy.46
  588.2 0.1 copy.47
  588.4 0.1 copy.48
  588.5 0.1 copy.49
  588.7 0.8 fusion.18
  (16 shorter events, 0.1 us)
Async XLA Ops:
  6.5 332.0 %copy-start = (bf16[1,384,1536]{2,1,0:T(8,128)(2,1)S(1)}, bf16[1,384,1536]{2,1,0:T(8,128)(2,1)}, u32[]{:S(2)}) copy-start(bf16[1,384,1536]{2,1,0:T(8,128)(2,1)} %param.17) | copy-start | bytes 3538948
  6.5 11.7 %copy-start.6 = (f32[8]{0:T(128)S(1)}, f32[8]{0:T(128)}, u32[]{:S(2)}) copy-start(f32[8]{0:T(128)} %param.13) | copy-start | bytes 100
  6.5 92.9 %all-gather.3.cloned.1.call-start = ((), (), s32[]{:S(2)}) async-start(), calls=%async_computation.4 | async-start | bytes 2113536 | tf_op jit(solution)/shard_map/all_gather | solution.py:72
  7.3 117.0 %reduce-scatter.7.cloned.1.call-start = ((), (), s32[]{:S(2)}) async-start(), calls=%async_computation.5 | async-start | bytes 491520
  8.2 8.8 %collective-permute-start = (bf16[128,1,128]{0,2,1:T(8,128)(2,1)S(1)}, bf16[128,1,128]{0,2,1:T(8,128)(2,1)S(1)}, u32[]{:S(2)}, u32[]{:S(2)}) collective-permute-start(bf16[128,1,128]{0,2,1:T(8,128)(2,1)S(1)} %copy.32), channel_id=1, source_target_pairs={{0,4},{4,8},{8,12},{12,16},{16,20},{20,24},{24,28},{28,32},{32,36}... | collective-permute-start | bytes 98312 | tf_op jit(solution)/shard_map/ppermute | solution.py:12
  101.9 1.6 copy-start.3
  101.9 23.3 %copy-start.2 = (bf16[128,384]{1,0:T(8,128)(2,1)S(1)}, bf16[128,384]{1,0:T(8,128)(2,1)}, u32[]{:S(2)}) copy-start(bf16[128,384]{1,0:T(8,128)(2,1)} %param.10) | copy-start | bytes 294916
  101.9 30.3 %copy-start.5 = (f32[384]{0:T(512)S(1)}, f32[384]{0:T(512)}, u32[]{:S(2)}) copy-start(f32[384]{0:T(512)} %param.15) | copy-start | bytes 4612
  355.6 171.5 %all-to-all-start.1 = ((bf16[1,128,12,1536]{3,2,0,1:T(8,128)(2,1)}), bf16[1,128,12,1536]{3,2,0,1:T(8,128)(2,1)}, u32[]{:S(2)}, u32[]{:S(2)}) async-start(bf16[1,128,12,1536]{3,2,0,1:T(8,128)(2,1)} %bitcast.76), calls=%async_computation.1 | async-start | bytes 12582912 | tf_op jit(solution)/shard_map/all_to_all | solution.py:119
  373.2 213.2 %reduce-scatter.9.cloned.1.call-start = ((), (), s32[]{:S(2)}) async-start(), calls=%async_computation.6 | async-start | bytes 1966080
  548.1 2.9 copy-start.4
  550.9 38.5 %copy-start.1 = (bf16[1,384,1536]{2,1,0:T(8,128)(2,1)S(1)}, bf16[1,384,1536]{2,1,0:T(8,128)(2,1)}, u32[]{:S(2)}) copy-start(bf16[1,384,1536]{2,1,0:T(8,128)(2,1)} %param.17) | copy-start | bytes 3538948
Sparse Core Ops, SparseCore 0:
  10.5 88.9 all-gather.2
  103.7 20.4 reduce-scatter.6
  551.1 35.3 reduce-scatter.8
where the time goes:
time: 597 us; the launch traced here: 596 us
  waiting for transfers between devices  293 us (49%)
  blocking collectives  181 us (30%)
  local copies, waits for them, and re-layouts  65.4 us (11%)
  starting transfers between devices  23 us (4%)
  matrix products  17.1 us (3%)
  between operations  13.4 us (2%)
    all_to_all x1, blocking collectives, body(): lax.all_to_all(outbox.reshape(ctx_count, 1, capacity, row_width), 'ctx',...  165 us
    all_to_all x1, waiting for transfers between devices, body(): lax.all_to_all(result, 'ctx', split_axis=1, concat_axis=0, tiled=True)  154 us
    all_gather x1, waiting for transfers between devices, body(): lax.all_gather(out_proj, 'ctx', axis=1, tiled=True)  80.7 us
    unnamed x5, waiting for transfers between devices  56 us
    all_to_all x1, starting transfers between devices, body(): lax.all_to_all(result, 'ctx', split_axis=1, concat_axis=0, tiled=True)  17.5 us
    unnamed x26, local copies, waits for them, and re-layouts  13.2 us
  transfers between devices with their start and end apart: 5, of which 5 were waited for; matrix products, arithmetic and copies ran while one was open for 1% of the time, Pallas kernels for 0%

commit v1 on v0

--- a/solution.py
+++ b/solution.py
@@ -92,35 +92,40 @@
     slot_ids = jnp.sum(onehot * before[:, None, :], -1)
     flat_index = (routes * capacity + slot_ids).reshape(-1)
     weights = route_scores / jnp.sum(route_scores, -1, keepdims=True)
-    full_data = lax.all_gather(normed, "tp", axis=1, tiled=True)
-    row_width = full_data.shape[1]
-    spread = jnp.broadcast_to(full_data[:, None, :], (tok_rows, top_count, row_width)).reshape(
-        -1, row_width
+    tp_index = lax.axis_index("tp")
+    spread = jnp.broadcast_to(normed[:, None, :], (tok_rows, top_count, quarter_w)).reshape(
+        -1, quarter_w
     )
-    outbox = jnp.zeros((experts * capacity, row_width), jnp.bfloat16).at[flat_index].set(spread)
+    outbox = jnp.zeros((experts * capacity, quarter_w), jnp.bfloat16).at[flat_index].set(spread)
     arrived = lax.all_to_all(
-        outbox.reshape(ctx_count, 1, capacity, row_width),
-        "ctx",
-        split_axis=0,
-        concat_axis=1,
-        tiled=True,
-    )
-    leading = arrived.shape[:3]
-    row_data = arrived.reshape(-1, d_model)
-    gate_vals = jnp.dot(row_data, expert_in[0, 0], preferred_element_type=jnp.float32)
-    up_vals = jnp.dot(row_data, expert_in[0, 1], preferred_element_type=jnp.float32)
+        outbox.reshape(ctx_count, capacity, quarter_w), "ctx", 0, 0, tiled=True
+    ).reshape(-1, quarter_w)
+    pieces = [arrived]
+    for step in range(1, tp_count):
+        pieces.append(lax.ppermute(arrived, "tp", [(i, (i + step) % tp_count) for i in range(tp_count)]))
+    row_data = jnp.concatenate(pieces, 1)
+    order = (tp_index - jnp.arange(tp_count, dtype=jnp.int32)) % tp_count
+    hidden_w = expert_in.shape[3]
+    w_gate = jnp.take(expert_in[0, 0].reshape(tp_count, quarter_w, hidden_w), order, axis=0).reshape(d_model, hidden_w)
+    w_up = jnp.take(expert_in[0, 1].reshape(tp_count, quarter_w, hidden_w), order, axis=0).reshape(d_model, hidden_w)
+    gate_vals = jnp.dot(row_data, w_gate, preferred_element_type=jnp.float32)
+    up_vals = jnp.dot(row_data, w_up, preferred_element_type=jnp.float32)
     activated = ((up_vals + 1.0) * gate_vals * jax.nn.sigmoid(1.702 * gate_vals)).astype(
         jnp.bfloat16
     )
-    partial_value = jnp.dot(activated, expert_out[0], preferred_element_type=jnp.float32).astype(
-        jnp.bfloat16
-    )
-    result = partial_value.reshape(leading + (d_model,))
-    returned = lax.all_to_all(result, "ctx", split_axis=1, concat_axis=0, tiled=True)
-    picked = returned.reshape(-1, d_model)[flat_index].reshape(tok_rows, top_count, d_model)
-    expert_result = lax.psum_scatter(
-        picked.astype(jnp.float32).astype(jnp.bfloat16), "tp", scatter_dimension=2, tiled=True
-    )
+    def partial_for(quarter_id):
+        cols = lax.dynamic_slice_in_dim(expert_out[0], quarter_id * quarter_w, quarter_w, 1)
+        return jnp.dot(activated, cols, preferred_element_type=jnp.float32).astype(jnp.bfloat16)
+
+    summed = partial_for(tp_index).astype(jnp.float32)
+    for step in range(1, tp_count):
+        piece = partial_for((tp_index + step) % tp_count)
+        summed = summed + lax.ppermute(
+            piece, "tp", [(i, (i + step) % tp_count) for i in range(tp_count)]
+        ).astype(jnp.float32)
+    result = summed.astype(jnp.bfloat16).reshape(ctx_count, capacity, quarter_w)
+    returned = lax.all_to_all(result, "ctx", 0, 0, tiled=True).reshape(-1, quarter_w)
+    expert_result = returned[flat_index].reshape(tok_rows, top_count, quarter_w)
     moe_sum = jnp.zeros((tok_rows, quarter_w), jnp.float32)
     for member in range(top_count):
         moe_sum = moe_sum + weights[:, member : member + 1] * expert_result[:, member].astype(

time: 597 us -> 400 us (0.67)
  blocking collectives: 181 us -> 66.2 us
  waiting for transfers between devices: 293 us -> 232 us
  local copies, waits for them, and re-layouts: 65.4 us -> 33.3 us
  starting transfers between devices: 23 us -> 34.3 us
    all_to_all x1, waiting for transfers between devices: 154 us -> 40.8 us  [body(): lax.all_to_all(result, 'ctx', 0, 0, tiled=True).reshape(-1, quarter_w)]
    all_to_all x1, blocking collectives: 165 us -> 59.3 us  [body(): lax.all_to_all(outbox.reshape(ctx_count, capacity, quarter_w), 'ctx', 0,...]
    ppermute x0 -> x6, waiting for transfers between devices: none -> 87.5 us  [the longest x3 46.6 us: body(): lax.ppermute(piece, 'tp', [(i, (i + step) % tp_count) for i in range(tp_c...]
    unnamed x5 -> x3, waiting for transfers between devices: 56 us -> 20.6 us
    reshape x6, local copies, waits for them, and re-layouts: 36.8 us -> 9.13 us  [the longest x1 3.21 us: body(): arrived = lax.all_to_all(outbox.reshape(ctx_count, capacity, quarter_w),...]
    ppermute x0 -> x6, starting transfers between devices: none -> 19.6 us  [the longest x3 10.3 us: body(): lax.ppermute(piece, 'tp', [(i, (i + step) % tp_count) for i in range(tp_c...]
    all_gather x1 -> x0, blocking collectives: 10 us -> none  [body(): full_data = lax.all_gather(normed, 'tp', axis=1, tiled=True)]
    all_to_all x1, starting transfers between devices: 17.5 us -> 9.22 us  [body(): lax.all_to_all(result, 'ctx', 0, 0, tiled=True).reshape(-1, quarter_w)]
  transfers between devices with their start and end apart: 5 -> 10, of which waited for: 5 -> 10; matrix products, arithmetic and copies ran while one was open for 1% -> 5% of each run, Pallas kernels for 0% -> 0%
where the time goes in v1:
time: 400 us; the launch traced here: 399 us
  waiting for transfers between devices  232 us (58%)
  blocking collectives  66.2 us (17%)
  starting transfers between devices  34.3 us (9%)
  local copies, waits for them, and re-layouts  33.3 us (8%)
  matrix products  15.8 us (4%)
  between operations  13.9 us (3%)
    all_gather x1, waiting for transfers between devices, body(): lax.all_gather(out_proj, 'ctx', axis=1, tiled=True)  81.4 us
    all_to_all x1, blocking collectives, body(): lax.all_to_all(outbox.reshape(ctx_count, capacity, quarter_w), 'ctx', 0,...  59.3 us
    ppermute x3, waiting for transfers between devices, body(): lax.ppermute(piece, 'tp', [(i, (i + step) % tp_count) for i in range(tp_c...  46.6 us
    ppermute x3, waiting for transfers between devices, body(): lax.ppermute(arrived, 'tp', [(i, (i + step) % tp_count) for i in range(tp...  40.9 us
    all_to_all x1, waiting for transfers between devices, body(): lax.all_to_all(result, 'ctx', 0, 0, tiled=True).reshape(-1, quarter_w)  40.8 us
    unnamed x3, waiting for transfers between devices  20.6 us
    unnamed x28, local copies, waits for them, and re-layouts  11 us
    ppermute x3, starting transfers between devices, body(): lax.ppermute(piece, 'tp', [(i, (i + step) % tp_count) for i in range(tp_c...  10.3 us
  transfers between devices with their start and end apart: 10, of which 10 were waited for; matrix products, arithmetic and copies ran while one was open for 5% of the time, Pallas kernels for 0%

profile of v1, /device:TPU:1, one launch (start us, length us, event | category | flops | bytes accessed | tf_op | source)
XLA Modules:
  0.0 398.9 jit_solution(11350336013368773157)
XLA Ops:
  6.5 0.7 all-gather.3.cloned.1.call-update
  7.3 0.9 copy.35
  8.2 5.4 %collective-permute-start = (bf16[128,1,128]{0,2,1:T(8,128)(2,1)S(1)}, bf16[128,1,128]{0,2,1:T(8,128)(2,1)S(1)}, u32[]{:S(2)}, u32[]{:S(2)}) collective-permute-start(bf16[128,1,128]{0,2,1:T(8,128)(2,1)S(1)} %copy.35), channel_id=1, source_target_pairs={{0,4},{4,8},{8,12},{12,16},{16,20},{20,24},{24,28},{28,32},{32,36}... | collective-permute-start | bytes 98312 | tf_op jit(solution)/shard_map/ppermute | solution.py:12
  13.6 0.1 and_and_fusion
  13.7 1.0 copy.37
  14.8 2.2 collective-permute-done
  17.0 0.3 select_reduce_fusion
  17.4 0.2 fusion.5
  17.7 0.4 convolution_convert_fusion.5
  18.0 81.4 %all-gather.3.cloned.1.call-done = bf16[128,12,512]{2,1,0:T(8,128)(2,1)} async-done(((bf16[1,12,512]{2,1,0:T(8,128)(2,1)}), bf16[128,12,512]{2,1,0:T(8,128)(2,1)}) %all-gather.3.cloned.1.call-update) | async-done | bytes 1572880 | tf_op jit(solution)/shard_map/all_gather | solution.py:72
  99.4 2.5 reshape.245
  101.9 0.7 convolution_convert_fusion.4
  102.6 0.9 copy.44
  103.6 0.1 convert_reduce_fusion
  103.7 0.2 reduce_window_sum.11
  103.9 0.2 select_reduce_fusion.1
  104.2 0.1 copy.39
  104.3 0.1 reshape.197
  104.4 19.9 %reduce-scatter.4.cloned.1.call-done = bf16[384,128]{1,0:T(8,128)(2,1)} async-done(((bf16[1536,128]{1,0:T(8,128)(2,1)}), bf16[384,128]{1,0:T(8,128)(2,1)}) %reduce-scatter.4.cloned.1.call-update) | async-done | bytes 98320
  124.3 1.0 copy.45
  125.3 0.1 multiply_reduce_fusion
  125.4 6.9 %psum.7 = f32[128]{0:T(128)S(1)} all-reduce(f32[128]{0:T(128)S(1)} %multiply_reduce_fusion), channel_id=1, replica_groups=mesh['ctx'=128,'tp'=4] {'tp'}, use_global_device_ids=true, to_apply=%region_8.9 | all-reduce | flops 128 | bytes 1024 | tf_op jit(solution)/shard_map/psum | solution.py:79
  132.3 0.1 multiply_convert_fusion
  132.4 0.1 broadcast_in_dim.46
  132.5 0.1 reshape.238
  132.6 3.5 scatter_custom_fusion
  136.1 2.2 reshape.199
  138.3 59.3 %all_to_all.10 = bf16[128,12,384]{2,1,0:T(8,128)(2,1)} all-to-all(bf16[128,12,384]{2,1,0:T(8,128)(2,1)S(1)} %reshape.199), channel_id=1, replica_groups=mesh['ctx'=128,'tp'=4] {'ctx'}, dimensions={0} | all-to-all | bytes 2359296 | tf_op jit(solution)/shard_map/all_to_all | solution.py:100
  197.6 3.2 reshape.200
  200.9 2.9 collective-permute-start.1
  203.8 2.9 fusion.38
  206.7 3.1 collective-permute-start.2
  209.8 3.3 collective-permute-start.3
  213.2 0.8 gather_fusion.1
  214.0 2.1 gather_fusion.2
  216.1 0.3 broadcast_select_fusion.1
  216.5 1.4 constant_dynamic-update-slice_fusion.3
  217.9 13.0 %collective-permute-done.1 = bf16[1536,384]{1,0:T(8,128)(2,1)} collective-permute-done((bf16[1536,384]{1,0:T(8,128)(2,1)}, bf16[1536,384]{1,0:T(8,128)(2,1)}, u32[]{:S(2)}, u32[]{:S(2)}) %collective-permute-start.1) | collective-permute-done | bytes 1179680 | tf_op jit(solution)/shard_map/ppermute | solution.py:105
  230.9 1.5 constant_dynamic-update-slice_fusion.2
  232.4 22.9 %collective-permute-done.2 = bf16[1536,384]{1,0:T(8,128)(2,1)} collective-permute-done((bf16[1536,384]{1,0:T(8,128)(2,1)}, bf16[1536,384]{1,0:T(8,128)(2,1)}, u32[]{:S(2)}, u32[]{:S(2)}) %collective-permute-start.2) | collective-permute-done | bytes 1179680 | tf_op jit(solution)/shard_map/ppermute | solution.py:105
  255.3 1.5 constant_dynamic-update-slice_fusion.1
  256.8 5.0 %collective-permute-done.3 = bf16[1536,384]{1,0:T(8,128)(2,1)} collective-permute-done((bf16[1536,384]{1,0:T(8,128)(2,1)}, bf16[1536,384]{1,0:T(8,128)(2,1)}, u32[]{:S(2)}, u32[]{:S(2)}) %collective-permute-start.3) | collective-permute-done | bytes 1179680 | tf_op jit(solution)/shard_map/ppermute | solution.py:105
  261.8 1.5 constant_dynamic-update-slice_fusion
  263.3 2.6 fusion.40
  266.0 3.1 fusion.2
  269.0 1.9 convolution_convert_fusion.2
  271.0 3.7 collective-permute-start.4
  274.7 1.9 convolution_convert_fusion.1
  276.6 4.7 %collective-permute-start.5 = (bf16[1536,384]{1,0:T(8,128)(2,1)}, bf16[1536,384]{1,0:T(8,128)(2,1)}, u32[]{:S(2)}, u32[]{:S(2)}) collective-permute-start(bf16[1536,384]{1,0:T(8,128)(2,1)} %convolution_convert_fusion.1), channel_id=1, source_target_pairs={{0,2},{1,3},{2,0},{3,1},{4,6},{5,7},{6,4},{7,5},{8,10},{9,11},{10,... | collective-permute-start | bytes 3538952 | tf_op jit(solution)/shard_map/ppermute | solution.py:123
  281.3 1.9 convolution_convert_fusion
  283.2 1.9 collective-permute-start.6
  285.1 16.6 %collective-permute-done.4 = bf16[1536,384]{1,0:T(8,128)(2,1)S(1)} collective-permute-done((bf16[1536,384]{1,0:T(8,128)(2,1)}, bf16[1536,384]{1,0:T(8,128)(2,1)S(1)}, u32[]{:S(2)}, u32[]{:S(2)}) %collective-permute-start.4) | collective-permute-done | bytes 1179680 | tf_op jit(solution)/shard_map/ppermute | solution.py:123
  301.8 26.9 %collective-permute-done.5 = bf16[1536,384]{1,0:T(8,128)(2,1)} collective-permute-done((bf16[1536,384]{1,0:T(8,128)(2,1)}, bf16[1536,384]{1,0:T(8,128)(2,1)}, u32[]{:S(2)}, u32[]{:S(2)}) %collective-permute-start.5) | collective-permute-done | bytes 1179680 | tf_op jit(solution)/shard_map/ppermute | solution.py:123
  328.6 3.0 collective-permute-done.6
  331.7 3.1 add_convert_fusion
  334.8 1.3 reshape.203
  336.1 9.2 %all-to-all-start.1 = ((bf16[128,12,384]{2,1,0:T(8,128)(2,1)}), bf16[128,12,384]{2,1,0:T(8,128)(2,1)}, u32[]{:S(2)}, u32[]{:S(2)}) async-start(bf16[128,12,384]{2,1,0:T(8,128)(2,1)} %reshape.203), calls=%async_computation.1 | async-start | bytes 3145728 | tf_op jit(solution)/shard_map/all_to_all | solution.py:127
  345.4 40.8 %all-to-all-done.1 = bf16[128,12,384]{2,1,0:T(8,128)(2,1)} async-done(((bf16[128,12,384]{2,1,0:T(8,128)(2,1)}), bf16[128,12,384]{2,1,0:T(8,128)(2,1)}, u32[]{:S(2)}, u32[]{:S(2)}) %all-to-all-start.1) | async-done | bytes 1179680 | tf_op jit(solution)/shard_map/all_to_all | solution.py:127
  386.1 2.3 reshape.204
  388.4 1.9 gather_fusion
  390.4 0.1 reshape.205
  390.5 0.6 fusion.39
  391.0 0.2 copy-done.2
  391.3 0.8 fusion.21
  (38 shorter events, 0.4 us)
Async XLA Ops:
  6.5 262.5 %copy-start = (bf16[1,384,1536]{2,1,0:T(8,128)(2,1)S(1)}, bf16[1,384,1536]{2,1,0:T(8,128)(2,1)}, u32[]{:S(2)}) copy-start(bf16[1,384,1536]{2,1,0:T(8,128)(2,1)} %param.19) | copy-start | bytes 3538948
  6.5 10.8 %copy-start.9 = (f32[8]{0:T(128)S(1)}, f32[8]{0:T(128)}, u32[]{:S(2)}) copy-start(f32[8]{0:T(128)} %param.15) | copy-start | bytes 100
  6.5 92.9 %all-gather.3.cloned.1.call-start = ((), (), s32[]{:S(2)}) async-start(), calls=%async_computation.3 | async-start | bytes 2113536 | tf_op jit(solution)/shard_map/all_gather | solution.py:72
  7.3 117.0 %reduce-scatter.4.cloned.1.call-start = ((), (), s32[]{:S(2)}) async-start(), calls=%async_computation.4 | async-start | bytes 491520
  8.2 8.8 %collective-permute-start = (bf16[128,1,128]{0,2,1:T(8,128)(2,1)S(1)}, bf16[128,1,128]{0,2,1:T(8,128)(2,1)S(1)}, u32[]{:S(2)}, u32[]{:S(2)}) collective-permute-start(bf16[128,1,128]{0,2,1:T(8,128)(2,1)S(1)} %copy.35), channel_id=1, source_target_pairs={{0,4},{4,8},{8,12},{12,16},{16,20},{20,24},{24,28},{28,32},{32,36}... | collective-permute-start | bytes 98312 | tf_op jit(solution)/shard_map/ppermute | solution.py:12
  101.9 1.7 copy-start.6
  102.6 22.7 %copy-start.4 = (bf16[128,384]{1,0:T(8,128)(2,1)S(1)}, bf16[128,384]{1,0:T(8,128)(2,1)}, u32[]{:S(2)}) copy-start(bf16[128,384]{1,0:T(8,128)(2,1)} %param.12) | copy-start | bytes 294916
  102.6 29.7 %copy-start.8 = (f32[384]{0:T(512)S(1)}, f32[384]{0:T(512)}, u32[]{:S(2)}) copy-start(f32[384]{0:T(512)} %param.17) | copy-start | bytes 4612
  125.3 7.3 %copy-start.1 = (bf16[128,384]{1,0:T(8,128)(2,1)}, bf16[128,384]{1,0:T(8,128)(2,1)S(1)}, u32[]{:S(2)}) copy-start(bf16[128,384]{1,0:T(8,128)(2,1)S(1)} %copy.45) | copy-start | bytes 294916
  200.9 30.0 %collective-permute-start.1 = (bf16[1536,384]{1,0:T(8,128)(2,1)}, bf16[1536,384]{1,0:T(8,128)(2,1)}, u32[]{:S(2)}, u32[]{:S(2)}) collective-permute-start(bf16[1536,384]{1,0:T(8,128)(2,1)} %reshape.200), channel_id=1, source_target_pairs={{0,1},{1,2},{2,3},{3,0},{4,5},{5,6},{6,7},{7,4},{8,9},{9,10},{10,1... | collective-permute-start | bytes 3538952 | tf_op jit(solution)/shard_map/ppermute | solution.py:105
  206.7 48.6 %collective-permute-start.2 = (bf16[1536,384]{1,0:T(8,128)(2,1)}, bf16[1536,384]{1,0:T(8,128)(2,1)}, u32[]{:S(2)}, u32[]{:S(2)}) collective-permute-start(bf16[1536,384]{1,0:T(8,128)(2,1)} %reshape.200), channel_id=1, source_target_pairs={{0,2},{1,3},{2,0},{3,1},{4,6},{5,7},{6,4},{7,5},{8,10},{9,11},{10,... | collective-permute-start | bytes 3538952 | tf_op jit(solution)/shard_map/ppermute | solution.py:105
  209.8 52.0 %collective-permute-start.3 = (bf16[1536,384]{1,0:T(8,128)(2,1)}, bf16[1536,384]{1,0:T(8,128)(2,1)}, u32[]{:S(2)}, u32[]{:S(2)}) collective-permute-start(bf16[1536,384]{1,0:T(8,128)(2,1)} %reshape.200), channel_id=1, source_target_pairs={{0,3},{1,0},{2,1},{3,2},{4,7},{5,4},{6,5},{7,6},{8,11},{9,8},{10,9... | collective-permute-start | bytes 3538952 | tf_op jit(solution)/shard_map/ppermute | solution.py:105
  271.0 30.8 %collective-permute-start.4 = (bf16[1536,384]{1,0:T(8,128)(2,1)}, bf16[1536,384]{1,0:T(8,128)(2,1)S(1)}, u32[]{:S(2)}, u32[]{:S(2)}) collective-permute-start(bf16[1536,384]{1,0:T(8,128)(2,1)} %convolution_convert_fusion.2), channel_id=1, source_target_pairs={{0,1},{1,2},{2,3},{3,0},{4,5},{5,6},{6,7},{7,4},{8,9},{9,10},{10,1... | collective-permute-start | bytes 3538952 | tf_op jit(solution)/shard_map/ppermute | solution.py:123
  276.6 52.1 %collective-permute-start.5 = (bf16[1536,384]{1,0:T(8,128)(2,1)}, bf16[1536,384]{1,0:T(8,128)(2,1)}, u32[]{:S(2)}, u32[]{:S(2)}) collective-permute-start(bf16[1536,384]{1,0:T(8,128)(2,1)} %convolution_convert_fusion.1), channel_id=1, source_target_pairs={{0,2},{1,3},{2,0},{3,1},{4,6},{5,7},{6,4},{7,5},{8,10},{9,11},{10,... | collective-permute-start | bytes 3538952 | tf_op jit(solution)/shard_map/ppermute | solution.py:123
  283.2 48.5 %collective-permute-start.6 = (bf16[1536,384]{1,0:T(8,128)(2,1)}, bf16[1536,384]{1,0:T(8,128)(2,1)}, u32[]{:S(2)}, u32[]{:S(2)}) collective-permute-start(bf16[1536,384]{1,0:T(8,128)(2,1)} %convolution_convert_fusion), channel_id=1, source_target_pairs={{0,3},{1,0},{2,1},{3,2},{4,7},{5,4},{6,5},{7,6},{8,11},{9,8},{10,9... | collective-permute-start | bytes 3538952 | tf_op jit(solution)/shard_map/ppermute | solution.py:123
  301.8 26.9 %copy-start.3 = (bf16[1536,384]{1,0:T(8,128)(2,1)}, bf16[1536,384]{1,0:T(8,128)(2,1)S(1)}, u32[]{:S(2)}) copy-start(bf16[1536,384]{1,0:T(8,128)(2,1)S(1)} %collective-permute-done.4) | copy-start | bytes 3538948
  336.1 9.2 %copy-start.7 = (f32[128,4]{0,1:T(4,128)S(1)}, f32[128,4]{0,1:T(4,128)}, u32[]{:S(2)}) copy-start(f32[128,4]{0,1:T(4,128)} %param.21) | copy-start | bytes 6148
  336.1 50.1 %all-to-all-start.1 = ((bf16[128,12,384]{2,1,0:T(8,128)(2,1)}), bf16[128,12,384]{2,1,0:T(8,128)(2,1)}, u32[]{:S(2)}, u32[]{:S(2)}) async-start(bf16[128,12,384]{2,1,0:T(8,128)(2,1)} %reshape.203), calls=%async_computation.1 | async-start | bytes 3145728 | tf_op jit(solution)/shard_map/all_to_all | solution.py:127
  390.3 0.9 copy-start.2
  390.3 0.9 copy-start.5
Sparse Core Ops, SparseCore 0:
  10.5 88.9 all-gather.2
  103.7 20.5 reduce-scatter.3

commit v2 on v1

--- a/solution.py
+++ b/solution.py
@@ -10,6 +10,31 @@
     count = lax.axis_size(axis)
     first, last = (max(0, -steps), min(count, count - steps))
     return lax.ppermute(value, axis, [(source, source + steps) for source in range(first, last)])
+
+
+def gathered_columns(block):
+    count = lax.axis_size("ctx")
+    bits = count.bit_length() - 1
+    me = lax.axis_index("ctx")
+    order = []
+    half = (bits - 1) // 2
+    y_bits, z_bits = list(range(bits - 1, half, -1)), list(range(half, 0, -1))
+    for pair in range(max(len(y_bits), len(z_bits))):
+        if pair < len(y_bits):
+            order.append(y_bits[pair])
+        if pair < len(z_bits):
+            order.append(z_bits[pair])
+    order.append(0)
+    held = block.T
+    for bit in order:
+        theirs = lax.ppermute(held, "ctx", [(i, i ^ (1 << bit)) for i in range(count)])
+        upper = ((me >> bit) & 1) == 1
+        lo = jnp.where(upper, theirs, held)
+        hi = jnp.where(upper, held, theirs)
+        held = jnp.stack([lo, hi], 0)
+    axis_of = {bit: place for place, bit in enumerate(reversed(order))}
+    perm = [axis_of[bit] for bit in range(bits - 1, -1, -1)] + [bits, bits + 1]
+    return held.transpose(perm).reshape(count * block.shape[1], block.shape[0])
 
 
 def attend(query_block, key_blk, value_blk, inside, sink_row_block, factor):
@@ -67,9 +92,10 @@
         factor,
     )
     outputs = mixed.reshape(block_row_count, q_heads * head_dim)
-    head_partial = jnp.dot(
+    head_partial = lax.dot_general(
         outputs,
-        lax.all_gather(out_proj, "ctx", axis=1, tiled=True),
+        gathered_columns(out_proj),
+        (((1,), (1,)), ((), ())),
         preferred_element_type=jnp.float32,
     )
     d_model = head_partial.shape[1]

time: 400 us -> 385 us (0.963)
  waiting for transfers between devices: 232 us -> 174 us
  starting transfers between devices: 34.3 us -> 75.2 us
    all_gather x1 -> x0, waiting for transfers between devices: 81.4 us -> none  [body(): lax.all_gather(out_proj, 'ctx', axis=1, tiled=True)]
    ppermute x0 -> x7, starting transfers between devices: none -> 39.8 us  [gathered_columns(): lax.ppermute(held, 'ctx', [(i, i ^ 1 << bit) for i in range(count)])]
    ppermute x0 -> x7, waiting for transfers between devices: none -> 21.2 us  [gathered_columns(): lax.ppermute(held, 'ctx', [(i, i ^ 1 << bit) for i in range(count)])]
    unnamed x3 -> x2, waiting for transfers between devices: 20.6 us -> 24.4 us
    unnamed x28 -> x29, local copies, waits for them, and re-layouts: 11 us -> 7.63 us
  transfers between devices with their start and end apart: 10 -> 16, of which waited for: 10 -> 14; matrix products, arithmetic and copies ran while one was open for 5% -> 5% of each run, Pallas kernels for 0% -> 0%
where the time goes in v2:
time: 385 us; the launch traced here: 384 us
  waiting for transfers between devices  174 us (45%)
  starting transfers between devices  75.2 us (20%)
  blocking collectives  66.2 us (17%)
  local copies, waits for them, and re-layouts  32.3 us (8%)
  matrix products  17.3 us (4%)
  between operations  14.1 us (4%)
  other arithmetic  4.83 us (1%)
    all_to_all x1, blocking collectives, body(): lax.all_to_all(outbox.reshape(ctx_count, capacity, quarter_w), 'ctx', 0,...  59.4 us
    ppermute x3, waiting for transfers between devices, body(): lax.ppermute(piece, 'tp', [(i, (i + step) % tp_count) for i in range(tp_c...  46.5 us
    ppermute x3, waiting for transfers between devices, body(): lax.ppermute(arrived, 'tp', [(i, (i + step) % tp_count) for i in range(tp...  40.9 us
    all_to_all x1, waiting for transfers between devices, body(): lax.all_to_all(result, 'ctx', 0, 0, tiled=True).reshape(-1, quarter_w)  40.8 us
    ppermute x7, starting transfers between devices, gathered_columns(): lax.ppermute(held, 'ctx', [(i, i ^ 1 << bit) for i in range(count)])  39.8 us
    unnamed x2, waiting for transfers between devices  24.4 us
    ppermute x7, waiting for transfers between devices, gathered_columns(): lax.ppermute(held, 'ctx', [(i, i ^ 1 << bit) for i in range(count)])  21.2 us
    ppermute x3, starting transfers between devices, body(): lax.ppermute(piece, 'tp', [(i, (i + step) % tp_count) for i in range(tp_c...  10.3 us
  transfers between devices with their start and end apart: 16, of which 14 were waited for; matrix products, arithmetic and copies ran while one was open for 5% of the time, Pallas kernels for 0%

profile of v2, /device:TPU:1, one launch (start us, length us, event | category | flops | bytes accessed | tf_op | source)
XLA Modules:
  0.0 383.6 jit_solution(9923590117875483595)
XLA Ops:
  6.5 8.4 %collective-permute-start.1 = (bf16[12,512]{1,0:T(8,128)(2,1)}, bf16[12,512]{1,0:T(8,128)(2,1)S(1)}, u32[]{:S(2)}, u32[]{:S(2)}) collective-permute-start(bf16[12,512]{1,0:T(8,128)(2,1)} %bitcast.127), channel_id=1, source_target_pairs={{0,256},{4,260},{8,264},{12,268},{16,272},{20,276},{24,280},{28,28... | collective-permute-start | bytes 36872 | tf_op jit(solution)/shard_map/ppermute | solution.py:30
  14.9 1.3 collective-permute-done.1
  16.3 0.7 select_bitcast_fusion.11
  17.0 10.6 %collective-permute-start.2 = (bf16[2,12,512]{2,1,0:T(8,128)(2,1)S(1)}, bf16[2,12,512]{2,1,0:T(8,128)(2,1)S(1)}, u32[]{:S(2)}, u32[]{:S(2)}) collective-permute-start(bf16[2,12,512]{2,1,0:T(8,128)(2,1)S(1)} %pad_maximum_fusion.6), channel_id=1, source_target_pairs={{0,32},{4,36},{8,40},{12,44},{16,48},{20,52},{24,56},{28,60},{32,0... | collective-permute-start | bytes 73736 | tf_op jit(solution)/shard_map/ppermute | solution.py:30
  27.7 1.3 collective-permute-done.2
  29.0 4.2 %collective-permute-start.3 = (bf16[2,2,12,512]{3,2,1,0:T(8,128)(2,1)S(1)}, bf16[2,2,12,512]{3,2,1,0:T(8,128)(2,1)S(1)}, u32[]{:S(2)}, u32[]{:S(2)}) collective-permute-start(bf16[2,2,12,512]{3,2,1,0:T(8,128)(2,1)S(1)} %pad_maximum_fusion.4), channel_id=1, source_target_pairs={{0,128},{4,132},{8,136},{12,140},{16,144},{20,148},{24,152},{28,15... | collective-permute-start | bytes 147464 | tf_op jit(solution)/shard_map/ppermute | solution.py:30
  33.2 1.7 collective-permute-done.3
  35.0 4.4 %collective-permute-start.4 = (bf16[2,2,2,12,512]{4,3,2,1,0:T(8,128)(2,1)S(1)}, bf16[2,2,2,12,512]{4,3,2,1,0:T(8,128)(2,1)S(1)}, u32[]{:S(2)}, u32[]{:S(2)}) collective-permute-start(bf16[2,2,2,12,512]{4,3,2,1,0:T(8,128)(2,1)S(1)} %pad_maximum_fusion.3), channel_id=1, source_target_pairs={{0,16},{4,20},{8,24},{12,28},{16,0},{20,4},{24,8},{28,12},{32,48},... | collective-permute-start | bytes 294920 | tf_op jit(solution)/shard_map/ppermute | solution.py:30
  39.4 0.9 copy.51
  40.3 6.5 %collective-permute-start = (bf16[128,1,128]{0,2,1:T(8,128)(2,1)S(1)}, bf16[128,1,128]{0,2,1:T(8,128)(2,1)S(1)}, u32[]{:S(2)}, u32[]{:S(2)}) collective-permute-start(bf16[128,1,128]{0,2,1:T(8,128)(2,1)S(1)} %copy.51), channel_id=1, source_target_pairs={{0,4},{4,8},{8,12},{12,16},{16,20},{20,24},{24,28},{28,32},{32,36}... | collective-permute-start | bytes 98312 | tf_op jit(solution)/shard_map/ppermute | solution.py:12
  46.9 3.3 collective-permute-start.5
  50.2 4.6 %collective-permute-done.5 = bf16[2,2,2,2,12,512]{5,4,3,2,1,0:T(8,128)(2,1)S(1)} collective-permute-done((bf16[2,2,2,2,12,512]{5,4,3,2,1,0:T(8,128)(2,1)S(1)}, bf16[2,2,2,2,12,512]{5,4,3,2,1,0:T(8,128)(2,1)S(1)}, u32[]{:S(2)}, u32[]{:S(2)}) %collective-permute-start.5) | collective-permute-done | bytes 196640 | tf_op jit(solution)/shard_map/ppermute | solution.py:30
  55.0 5.8 %collective-permute-start.6 = (bf16[2,2,2,2,2,12,512]{6,5,4,3,2,1,0:T(8,128)(2,1)S(1)}, bf16[2,2,2,2,2,12,512]{6,5,4,3,2,1,0:T(8,128)(2,1)S(1)}, u32[]{:S(2)}, u32[]{:S(2)}) collective-permute-start(bf16[2,2,2,2,2,12,512]{6,5,4,3,2,1,0:T(8,128)(2,1)S(1)} %pad_maximum_fusion.1), channel_id=1, source_target_pairs={{0,8},{4,12},{8,0},{12,4},{16,24},{20,28},{24,16},{28,20},{32,40},... | collective-permute-start | bytes 1179656 | tf_op jit(solution)/shard_map/ppermute | solution.py:30
  61.0 0.3 select_reduce_fusion
  61.4 11.0 %collective-permute-done.6 = bf16[2,2,2,2,2,12,512]{6,5,4,3,2,1,0:T(8,128)(2,1)S(1)} collective-permute-done((bf16[2,2,2,2,2,12,512]{6,5,4,3,2,1,0:T(8,128)(2,1)S(1)}, bf16[2,2,2,2,2,12,512]{6,5,4,3,2,1,0:T(8,128)(2,1)S(1)}, u32[]{:S(2)}, u32[]{:S(2)}) %collective-permute-start.6) | collective-permute-done | bytes 393248 | tf_op jit(solution)/shard_map/ppermute | solution.py:30
  72.6 0.8 copy.55
  73.5 3.1 collective-permute-start.7
  77.0 0.4 convolution_convert_fusion.5
  77.3 1.2 collective-permute-done.7
  78.5 0.3 fusion.5
  78.8 0.3 maximum_bitcast_fusion
  79.3 1.4 reshape.200
  80.6 2.1 convolution_convert_fusion.4
  82.7 0.9 copy.64
  84.5 24.4 %reduce-scatter.4.cloned.1.call-done = bf16[384,128]{1,0:T(8,128)(2,1)} async-done(((bf16[1536,128]{1,0:T(8,128)(2,1)}), bf16[384,128]{1,0:T(8,128)(2,1)}) %reduce-scatter.4.cloned.1.call-update) | async-done | bytes 98320
  108.9 1.0 copy.65
  110.1 6.8 %psum.7 = f32[128]{0:T(128)S(1)} all-reduce(f32[128]{0:T(128)S(1)} %multiply_reduce_fusion), channel_id=1, replica_groups=mesh['ctx'=128,'tp'=4] {'tp'}, use_global_device_ids=true, to_apply=%region_8.9 | all-reduce | flops 128 | bytes 1024 | tf_op jit(solution)/shard_map/psum | solution.py:105
  117.3 3.6 scatter_custom_fusion
  120.8 2.2 reshape.203
  123.0 59.4 %all_to_all.10 = bf16[128,12,384]{2,1,0:T(8,128)(2,1)} all-to-all(bf16[128,12,384]{2,1,0:T(8,128)(2,1)S(1)} %reshape.203), channel_id=1, replica_groups=mesh['ctx'=128,'tp'=4] {'ctx'}, dimensions={0} | all-to-all | bytes 2359296 | tf_op jit(solution)/shard_map/all_to_all | solution.py:126
  182.3 3.2 reshape.204
  185.6 2.9 collective-permute-start.8
  188.5 2.9 fusion.40
  191.4 3.1 collective-permute-start.9
  194.5 3.3 collective-permute-start.10
  197.9 0.8 gather_fusion.1
  198.7 2.1 gather_fusion.2
  200.8 0.3 broadcast_select_fusion.1
  201.2 1.4 constant_dynamic-update-slice_fusion.3
  202.6 13.0 %collective-permute-done.8 = bf16[1536,384]{1,0:T(8,128)(2,1)} collective-permute-done((bf16[1536,384]{1,0:T(8,128)(2,1)}, bf16[1536,384]{1,0:T(8,128)(2,1)}, u32[]{:S(2)}, u32[]{:S(2)}) %collective-permute-start.8) | collective-permute-done | bytes 1179680 | tf_op jit(solution)/shard_map/ppermute | solution.py:131
  215.6 1.5 constant_dynamic-update-slice_fusion.2
  217.1 22.9 %collective-permute-done.9 = bf16[1536,384]{1,0:T(8,128)(2,1)} collective-permute-done((bf16[1536,384]{1,0:T(8,128)(2,1)}, bf16[1536,384]{1,0:T(8,128)(2,1)}, u32[]{:S(2)}, u32[]{:S(2)}) %collective-permute-start.9) | collective-permute-done | bytes 1179680 | tf_op jit(solution)/shard_map/ppermute | solution.py:131
  240.0 1.5 constant_dynamic-update-slice_fusion.1
  241.5 5.0 %collective-permute-done.10 = bf16[1536,384]{1,0:T(8,128)(2,1)} collective-permute-done((bf16[1536,384]{1,0:T(8,128)(2,1)}, bf16[1536,384]{1,0:T(8,128)(2,1)}, u32[]{:S(2)}, u32[]{:S(2)}) %collective-permute-start.10) | collective-permute-done | bytes 1179680 | tf_op jit(solution)/shard_map/ppermute | solution.py:131
  246.5 1.5 constant_dynamic-update-slice_fusion
  248.0 2.6 fusion.42
  250.7 3.1 fusion.2
  253.7 1.9 convolution_convert_fusion.2
  255.7 3.7 collective-permute-start.11
  259.4 1.9 convolution_convert_fusion.1
  261.3 4.7 %collective-permute-start.12 = (bf16[1536,384]{1,0:T(8,128)(2,1)}, bf16[1536,384]{1,0:T(8,128)(2,1)}, u32[]{:S(2)}, u32[]{:S(2)}) collective-permute-start(bf16[1536,384]{1,0:T(8,128)(2,1)} %convolution_convert_fusion.1), channel_id=1, source_target_pairs={{0,2},{1,3},{2,0},{3,1},{4,6},{5,7},{6,4},{7,5},{8,10},{9,11},{10,... | collective-permute-start | bytes 3538952 | tf_op jit(solution)/shard_map/ppermute | solution.py:149
  266.0 1.9 convolution_convert_fusion
  267.9 1.9 collective-permute-start.13
  269.8 16.6 %collective-permute-done.11 = bf16[1536,384]{1,0:T(8,128)(2,1)S(1)} collective-permute-done((bf16[1536,384]{1,0:T(8,128)(2,1)}, bf16[1536,384]{1,0:T(8,128)(2,1)S(1)}, u32[]{:S(2)}, u32[]{:S(2)}) %collective-permute-start.11) | collective-permute-done | bytes 1179680 | tf_op jit(solution)/shard_map/ppermute | solution.py:149
  286.4 26.9 %collective-permute-done.12 = bf16[1536,384]{1,0:T(8,128)(2,1)} collective-permute-done((bf16[1536,384]{1,0:T(8,128)(2,1)}, bf16[1536,384]{1,0:T(8,128)(2,1)}, u32[]{:S(2)}, u32[]{:S(2)}) %collective-permute-start.12) | collective-permute-done | bytes 1179680 | tf_op jit(solution)/shard_map/ppermute | solution.py:149
  313.3 3.1 collective-permute-done.13
  316.4 3.1 add_convert_fusion
  319.5 1.3 reshape.207
  320.7 9.2 %all-to-all-start.1 = ((bf16[128,12,384]{2,1,0:T(8,128)(2,1)}), bf16[128,12,384]{2,1,0:T(8,128)(2,1)}, u32[]{:S(2)}, u32[]{:S(2)}) async-start(bf16[128,12,384]{2,1,0:T(8,128)(2,1)} %reshape.207), calls=%async_computation.1 | async-start | bytes 3145728 | tf_op jit(solution)/shard_map/all_to_all | solution.py:153
  330.0 40.8 %all-to-all-done.1 = bf16[128,12,384]{2,1,0:T(8,128)(2,1)} async-done(((bf16[128,12,384]{2,1,0:T(8,128)(2,1)}), bf16[128,12,384]{2,1,0:T(8,128)(2,1)}, u32[]{:S(2)}, u32[]{:S(2)}) %all-to-all-start.1) | async-done | bytes 1179680 | tf_op jit(solution)/shard_map/all_to_all | solution.py:153
  370.8 2.3 reshape.208
  373.1 1.9 gather_fusion
  375.1 0.6 fusion.41
  376.0 0.8 fusion.23
  (67 shorter events, 3.0 us)
Async XLA Ops:
  6.5 247.2 %copy-start = (bf16[1,384,1536]{2,1,0:T(8,128)(2,1)S(1)}, bf16[1,384,1536]{2,1,0:T(8,128)(2,1)}, u32[]{:S(2)}) copy-start(bf16[1,384,1536]{2,1,0:T(8,128)(2,1)} %param.19) | copy-start | bytes 3538948
  6.5 102.4 %reduce-scatter.4.cloned.1.call-start = ((), (), s32[]{:S(2)}) async-start(), calls=%async_computation.3 | async-start | bytes 491520
  6.5 9.7 %collective-permute-start.1 = (bf16[12,512]{1,0:T(8,128)(2,1)}, bf16[12,512]{1,0:T(8,128)(2,1)S(1)}, u32[]{:S(2)}, u32[]{:S(2)}) collective-permute-start(bf16[12,512]{1,0:T(8,128)(2,1)} %bitcast.127), channel_id=1, source_target_pairs={{0,256},{4,260},{8,264},{12,268},{16,272},{20,276},{24,280},{28,28... | collective-permute-start | bytes 36872 | tf_op jit(solution)/shard_map/ppermute | solution.py:30
  17.0 12.0 %collective-permute-start.2 = (bf16[2,12,512]{2,1,0:T(8,128)(2,1)S(1)}, bf16[2,12,512]{2,1,0:T(8,128)(2,1)S(1)}, u32[]{:S(2)}, u32[]{:S(2)}) collective-permute-start(bf16[2,12,512]{2,1,0:T(8,128)(2,1)S(1)} %pad_maximum_fusion.6), channel_id=1, source_target_pairs={{0,32},{4,36},{8,40},{12,44},{16,48},{20,52},{24,56},{28,60},{32,0... | collective-permute-start | bytes 73736 | tf_op jit(solution)/shard_map/ppermute | solution.py:30
  29.0 5.9 %collective-permute-start.3 = (bf16[2,2,12,512]{3,2,1,0:T(8,128)(2,1)S(1)}, bf16[2,2,12,512]{3,2,1,0:T(8,128)(2,1)S(1)}, u32[]{:S(2)}, u32[]{:S(2)}) collective-permute-start(bf16[2,2,12,512]{3,2,1,0:T(8,128)(2,1)S(1)} %pad_maximum_fusion.4), channel_id=1, source_target_pairs={{0,128},{4,132},{8,136},{12,140},{16,144},{20,148},{24,152},{28,15... | collective-permute-start | bytes 147464 | tf_op jit(solution)/shard_map/ppermute | solution.py:30
  35.0 11.8 %collective-permute-start.4 = (bf16[2,2,2,12,512]{4,3,2,1,0:T(8,128)(2,1)S(1)}, bf16[2,2,2,12,512]{4,3,2,1,0:T(8,128)(2,1)S(1)}, u32[]{:S(2)}, u32[]{:S(2)}) collective-permute-start(bf16[2,2,2,12,512]{4,3,2,1,0:T(8,128)(2,1)S(1)} %pad_maximum_fusion.3), channel_id=1, source_target_pairs={{0,16},{4,20},{8,24},{12,28},{16,0},{20,4},{24,8},{28,12},{32,48},... | collective-permute-start | bytes 294920 | tf_op jit(solution)/shard_map/ppermute | solution.py:30
  40.3 20.8 %collective-permute-start = (bf16[128,1,128]{0,2,1:T(8,128)(2,1)S(1)}, bf16[128,1,128]{0,2,1:T(8,128)(2,1)S(1)}, u32[]{:S(2)}, u32[]{:S(2)}) collective-permute-start(bf16[128,1,128]{0,2,1:T(8,128)(2,1)S(1)} %copy.51), channel_id=1, source_target_pairs={{0,4},{4,8},{8,12},{12,16},{16,20},{20,24},{24,28},{28,32},{32,36}... | collective-permute-start | bytes 98312 | tf_op jit(solution)/shard_map/ppermute | solution.py:12
  46.8 14.1 %copy-start.6 = (bf16[128,512]{1,0:T(8,128)(2,1)S(1)}, bf16[128,512]{1,0:T(8,128)(2,1)}, u32[]{:S(2)}) copy-start(bf16[128,512]{1,0:T(8,128)(2,1)} %param.13) | copy-start | bytes 393220
  46.9 8.0 %collective-permute-start.5 = (bf16[2,2,2,2,12,512]{5,4,3,2,1,0:T(8,128)(2,1)S(1)}, bf16[2,2,2,2,12,512]{5,4,3,2,1,0:T(8,128)(2,1)S(1)}, u32[]{:S(2)}, u32[]{:S(2)}) collective-permute-start(bf16[2,2,2,2,12,512]{5,4,3,2,1,0:T(8,128)(2,1)S(1)} %pad_maximum_fusion.2), channel_id=1, source_target_pairs={{0,64},{4,68},{8,72},{12,76},{16,80},{20,84},{24,88},{28,92},{32,9... | collective-permute-start | bytes 589832 | tf_op jit(solution)/shard_map/ppermute | solution.py:30
  55.0 17.4 %collective-permute-start.6 = (bf16[2,2,2,2,2,12,512]{6,5,4,3,2,1,0:T(8,128)(2,1)S(1)}, bf16[2,2,2,2,2,12,512]{6,5,4,3,2,1,0:T(8,128)(2,1)S(1)}, u32[]{:S(2)}, u32[]{:S(2)}) collective-permute-start(bf16[2,2,2,2,2,12,512]{6,5,4,3,2,1,0:T(8,128)(2,1)S(1)} %pad_maximum_fusion.1), channel_id=1, source_target_pairs={{0,8},{4,12},{8,0},{12,4},{16,24},{20,28},{24,16},{28,20},{32,40},... | collective-permute-start | bytes 1179656 | tf_op jit(solution)/shard_map/ppermute | solution.py:30
  72.6 4.0 %copy-start.10 = (f32[8]{0:T(128)S(1)}, f32[8]{0:T(128)}, u32[]{:S(2)}) copy-start(f32[8]{0:T(128)} %param.15) | copy-start | bytes 100
  73.5 5.0 %collective-permute-start.7 = (bf16[2,2,2,2,2,2,12,512]{7,5,6,4,3,2,1,0:T(2,128)(2,1)S(1)}, bf16[2,2,2,2,2,2,12,512]{7,5,6,4,3,2,1,0:T(2,128)(2,1)S(1)}, u32[]{:S(2)}, u32[]{:S(2)}) collective-permute-start(bf16[2,2,2,2,2,2,12,512]{7,5,6,4,3,2,1,0:T(2,128)(2,1)S(1)} %copy.55), channel_id=1, source_target_pairs={{0,4},{4,0},{8,12},{12,8},{16,20},{20,16},{24,28},{28,24},{32,36},... | collective-permute-start | bytes 2359304 | tf_op jit(solution)/shard_map/ppermute | solution.py:30
  80.6 3.0 copy-start.7
  82.7 27.2 %copy-start.4 = (bf16[128,384]{1,0:T(8,128)(2,1)S(1)}, bf16[128,384]{1,0:T(8,128)(2,1)}, u32[]{:S(2)}) copy-start(bf16[128,384]{1,0:T(8,128)(2,1)} %param.12) | copy-start | bytes 294916
  82.7 34.2 %copy-start.9 = (f32[384]{0:T(512)S(1)}, f32[384]{0:T(512)}, u32[]{:S(2)}) copy-start(f32[384]{0:T(512)} %param.17) | copy-start | bytes 4612
  109.9 7.3 %copy-start.1 = (bf16[128,384]{1,0:T(8,128)(2,1)}, bf16[128,384]{1,0:T(8,128)(2,1)S(1)}, u32[]{:S(2)}) copy-start(bf16[128,384]{1,0:T(8,128)(2,1)S(1)} %copy.65) | copy-start | bytes 294916
  185.6 30.0 %collective-permute-start.8 = (bf16[1536,384]{1,0:T(8,128)(2,1)}, bf16[1536,384]{1,0:T(8,128)(2,1)}, u32[]{:S(2)}, u32[]{:S(2)}) collective-permute-start(bf16[1536,384]{1,0:T(8,128)(2,1)} %reshape.204), channel_id=1, source_target_pairs={{0,1},{1,2},{2,3},{3,0},{4,5},{5,6},{6,7},{7,4},{8,9},{9,10},{10,1... | collective-permute-start | bytes 3538952 | tf_op jit(solution)/shard_map/ppermute | solution.py:131
  191.4 48.6 %collective-permute-start.9 = (bf16[1536,384]{1,0:T(8,128)(2,1)}, bf16[1536,384]{1,0:T(8,128)(2,1)}, u32[]{:S(2)}, u32[]{:S(2)}) collective-permute-start(bf16[1536,384]{1,0:T(8,128)(2,1)} %reshape.204), channel_id=1, source_target_pairs={{0,2},{1,3},{2,0},{3,1},{4,6},{5,7},{6,4},{7,5},{8,10},{9,11},{10,... | collective-permute-start | bytes 3538952 | tf_op jit(solution)/shard_map/ppermute | solution.py:131
  194.5 52.0 %collective-permute-start.10 = (bf16[1536,384]{1,0:T(8,128)(2,1)}, bf16[1536,384]{1,0:T(8,128)(2,1)}, u32[]{:S(2)}, u32[]{:S(2)}) collective-permute-start(bf16[1536,384]{1,0:T(8,128)(2,1)} %reshape.204), channel_id=1, source_target_pairs={{0,3},{1,0},{2,1},{3,2},{4,7},{5,4},{6,5},{7,6},{8,11},{9,8},{10,9... | collective-permute-start | bytes 3538952 | tf_op jit(solution)/shard_map/ppermute | solution.py:131
  255.7 30.8 %collective-permute-start.11 = (bf16[1536,384]{1,0:T(8,128)(2,1)}, bf16[1536,384]{1,0:T(8,128)(2,1)S(1)}, u32[]{:S(2)}, u32[]{:S(2)}) collective-permute-start(bf16[1536,384]{1,0:T(8,128)(2,1)} %convolution_convert_fusion.2), channel_id=1, source_target_pairs={{0,1},{1,2},{2,3},{3,0},{4,5},{5,6},{6,7},{7,4},{8,9},{9,10},{10,1... | collective-permute-start | bytes 3538952 | tf_op jit(solution)/shard_map/ppermute | solution.py:149
  261.3 52.0 %collective-permute-start.12 = (bf16[1536,384]{1,0:T(8,128)(2,1)}, bf16[1536,384]{1,0:T(8,128)(2,1)}, u32[]{:S(2)}, u32[]{:S(2)}) collective-permute-start(bf16[1536,384]{1,0:T(8,128)(2,1)} %convolution_convert_fusion.1), channel_id=1, source_target_pairs={{0,2},{1,3},{2,0},{3,1},{4,6},{5,7},{6,4},{7,5},{8,10},{9,11},{10,... | collective-permute-start | bytes 3538952 | tf_op jit(solution)/shard_map/ppermute | solution.py:149
  267.9 48.5 %collective-permute-start.13 = (bf16[1536,384]{1,0:T(8,128)(2,1)}, bf16[1536,384]{1,0:T(8,128)(2,1)}, u32[]{:S(2)}, u32[]{:S(2)}) collective-permute-start(bf16[1536,384]{1,0:T(8,128)(2,1)} %convolution_convert_fusion), channel_id=1, source_target_pairs={{0,3},{1,0},{2,1},{3,2},{4,7},{5,4},{6,5},{7,6},{8,11},{9,8},{10,9... | collective-permute-start | bytes 3538952 | tf_op jit(solution)/shard_map/ppermute | solution.py:149
  286.4 26.9 %copy-start.3 = (bf16[1536,384]{1,0:T(8,128)(2,1)}, bf16[1536,384]{1,0:T(8,128)(2,1)S(1)}, u32[]{:S(2)}) copy-start(bf16[1536,384]{1,0:T(8,128)(2,1)S(1)} %collective-permute-done.11) | copy-start | bytes 3538948
  320.7 9.2 %copy-start.8 = (f32[128,4]{0,1:T(4,128)S(1)}, f32[128,4]{0,1:T(4,128)}, u32[]{:S(2)}) copy-start(f32[128,4]{0,1:T(4,128)} %param.21) | copy-start | bytes 6148
  320.7 50.1 %all-to-all-start.1 = ((bf16[128,12,384]{2,1,0:T(8,128)(2,1)}), bf16[128,12,384]{2,1,0:T(8,128)(2,1)}, u32[]{:S(2)}, u32[]{:S(2)}) async-start(bf16[128,12,384]{2,1,0:T(8,128)(2,1)} %reshape.207), calls=%async_computation.1 | async-start | bytes 3145728 | tf_op jit(solution)/shard_map/all_to_all | solution.py:153
  375.0 0.9 copy-start.2
  375.0 0.9 copy-start.5
Sparse Core Ops, SparseCore 0:
  83.8 25.0 reduce-scatter.3

commit v3 on v2

--- a/solution.py
+++ b/solution.py
@@ -99,26 +99,39 @@
         preferred_element_type=jnp.float32,
     )
     d_model = head_partial.shape[1]
-    residual = hidden_in.astype(jnp.float32) + lax.psum_scatter(
-        head_partial.astype(jnp.bfloat16), "tp", scatter_dimension=1, tiled=True
-    ).astype(jnp.float32)
-    square_total = lax.psum(jnp.sum(residual * residual, -1), "tp")
+    tp_count = lax.axis_size("tp")
+    tp_index = lax.axis_index("tp")
+    quarter_w = d_model // tp_count
+    sent = jnp.concatenate([head_partial.astype(jnp.bfloat16), hidden_in], 1)
+    held = [(sent, tp_index)]
+    for step in range(1, tp_count):
+        got = lax.ppermute(sent, "tp", [(i, (i + step) % tp_count) for i in range(tp_count)])
+        held.append((got, (tp_index - step) % tp_count))
+    head_sum = held[0][0][:, :d_model].astype(jnp.float32)
+    for got, _ in held[1:]:
+        head_sum = head_sum + got[:, :d_model].astype(jnp.float32)
+    square_total = jnp.zeros((tok_rows,), jnp.float32)
+    residual = None
+    for got, quarter_id in held:
+        part = got[:, d_model:].astype(jnp.float32) + lax.dynamic_slice_in_dim(
+            head_sum, quarter_id * quarter_w, quarter_w, 1
+        )
+        square_total = square_total + jnp.sum(part * part, -1)
+        if residual is None:
+            residual = part
     normed = (residual * lax.rsqrt(square_total[:, None] / d_model + 1e-05) * norm_gain).astype(
         jnp.bfloat16
     )
     ctx_count = lax.axis_size("ctx")
-    tp_count = lax.axis_size("tp")
     top_count = routes.shape[1]
     experts = ctx_count * expert_in.shape[0]
     capacity = max(2, min(tok_rows, 3 * top_count * tok_rows // experts))
-    quarter_w = d_model // tp_count
     onehot = (routes[:, :, None] == jnp.arange(experts, dtype=jnp.int32)).astype(jnp.int32)
     per_tok = jnp.sum(onehot, 1)
     before = jnp.cumsum(per_tok, axis=0) - per_tok
     slot_ids = jnp.sum(onehot * before[:, None, :], -1)
     flat_index = (routes * capacity + slot_ids).reshape(-1)
     weights = route_scores / jnp.sum(route_scores, -1, keepdims=True)
-    tp_index = lax.axis_index("tp")
     spread = jnp.broadcast_to(normed[:, None, :], (tok_rows, top_count, quarter_w)).reshape(
         -1, quarter_w
     )
@@ -126,16 +139,18 @@
     arrived = lax.all_to_all(
         outbox.reshape(ctx_count, capacity, quarter_w), "ctx", 0, 0, tiled=True
     ).reshape(-1, quarter_w)
-    pieces = [arrived]
+    pieces = [(arrived, tp_index)]
     for step in range(1, tp_count):
-        pieces.append(lax.ppermute(arrived, "tp", [(i, (i + step) % tp_count) for i in range(tp_count)]))
-    row_data = jnp.concatenate(pieces, 1)
-    order = (tp_index - jnp.arange(tp_count, dtype=jnp.int32)) % tp_count
-    hidden_w = expert_in.shape[3]
-    w_gate = jnp.take(expert_in[0, 0].reshape(tp_count, quarter_w, hidden_w), order, axis=0).reshape(d_model, hidden_w)
-    w_up = jnp.take(expert_in[0, 1].reshape(tp_count, quarter_w, hidden_w), order, axis=0).reshape(d_model, hidden_w)
-    gate_vals = jnp.dot(row_data, w_gate, preferred_element_type=jnp.float32)
-    up_vals = jnp.dot(row_data, w_up, preferred_element_type=jnp.float32)
+        got = lax.ppermute(arrived, "tp", [(i, (i + step) % tp_count) for i in range(tp_count)])
+        pieces.append((got, (tp_index - step) % tp_count))
+    gate_vals = None
+    up_vals = None
+    for piece, quarter_id in pieces:
+        rows_of = lambda w: lax.dynamic_slice_in_dim(w, quarter_id * quarter_w, quarter_w, 0)
+        gate_part = jnp.dot(piece, rows_of(expert_in[0, 0]), preferred_element_type=jnp.float32)
+        up_part = jnp.dot(piece, rows_of(expert_in[0, 1]), preferred_element_type=jnp.float32)
+        gate_vals = gate_part if gate_vals is None else gate_vals + gate_part
+        up_vals = up_part if up_vals is None else up_vals + up_part
     activated = ((up_vals + 1.0) * gate_vals * jax.nn.sigmoid(1.702 * gate_vals)).astype(
         jnp.bfloat16
     )
@@ -143,12 +158,15 @@
         cols = lax.dynamic_slice_in_dim(expert_out[0], quarter_id * quarter_w, quarter_w, 1)
         return jnp.dot(activated, cols, preferred_element_type=jnp.float32).astype(jnp.bfloat16)
 
-    summed = partial_for(tp_index).astype(jnp.float32)
+    arriving = []
     for step in range(1, tp_count):
         piece = partial_for((tp_index + step) % tp_count)
-        summed = summed + lax.ppermute(
-            piece, "tp", [(i, (i + step) % tp_count) for i in range(tp_count)]
-        ).astype(jnp.float32)
+        arriving.append(
+            lax.ppermute(piece, "tp", [(i, (i + step) % tp_count) for i in range(tp_count)])
+        )
+    summed = partial_for(tp_index).astype(jnp.float32)
+    for got in arriving:
+        summed = summed + got.astype(jnp.float32)
     result = summed.astype(jnp.bfloat16).reshape(ctx_count, capacity, quarter_w)
     returned = lax.all_to_all(result, "ctx", 0, 0, tiled=True).reshape(-1, quarter_w)
     expert_result = returned[flat_index].reshape(tok_rows, top_count, quarter_w)

time: 385 us -> 357 us (0.927)
  blocking collectives: 66.2 us -> 0 us
  waiting for transfers between devices: 174 us -> 221 us
  starting transfers between devices: 75.2 us -> 93.8 us
  local copies, waits for them, and re-layouts: 32.3 us -> 18.9 us
  between operations: 14.1 us -> 0.79 us
    all_to_all x1 -> x0, blocking collectives: 59.4 us -> none  [body(): lax.all_to_all(outbox.reshape(ctx_count, capacity, quarter_w), 'ctx', 0,...]
    all_to_all x0 -> x1, waiting for transfers between devices: none -> 40.8 us  [body(): lax.all_to_all(outbox.reshape(ctx_count, capacity, quarter_w), 'ctx', 0,...]
    unnamed x2 -> x0, waiting for transfers between devices: 24.4 us -> none
    ppermute x0 -> x3, waiting for transfers between devices: none -> 21.6 us  [body(): lax.ppermute(sent, 'tp', [(i, (i + step) % tp_count) for i in range(tp_co...]
    all_to_all x0 -> x1, starting transfers between devices: none -> 12.4 us  [body(): lax.all_to_all(outbox.reshape(ctx_count, capacity, quarter_w), 'ctx', 0,...]
    ppermute x0 -> x3, starting transfers between devices: none -> 9.55 us  [body(): lax.ppermute(sent, 'tp', [(i, (i + step) % tp_count) for i in range(tp_co...]
    psum x1 -> x0, blocking collectives: 6.84 us -> none  [body(): square_total = lax.psum(jnp.sum(residual * residual, -1), 'tp')]
    ppermute x7, waiting for transfers between devices: 21.2 us -> 27.9 us  [gathered_columns(): lax.ppermute(held, 'ctx', [(i, i ^ 1 << bit) for i in range(count)])]
  transfers between devices with their start and end apart: 16 -> 19, of which waited for: 14 -> 16; matrix products, arithmetic and copies ran while one was open for 5% -> 4% of each run, Pallas kernels for 0% -> 0%
where the time goes in v3:
time: 357 us; the launch traced here: 355 us
  waiting for transfers between devices  221 us (62%)
  starting transfers between devices  93.8 us (26%)
  local copies, waits for them, and re-layouts  18.9 us (5%)
  matrix products  14.2 us (4%)
  other arithmetic  6.12 us (2%)
    ppermute x3, waiting for transfers between devices, body(): lax.ppermute(piece, 'tp', [(i, (i + step) % tp_count) for i in range(tp_c...  48.6 us
    ppermute x3, waiting for transfers between devices, body(): lax.ppermute(arrived, 'tp', [(i, (i + step) % tp_count) for i in range(tp...  42.3 us
    all_to_all x1, waiting for transfers between devices, body(): lax.all_to_all(outbox.reshape(ctx_count, capacity, quarter_w), 'ctx', 0,...  40.8 us
    all_to_all x1, waiting for transfers between devices, body(): lax.all_to_all(result, 'ctx', 0, 0, tiled=True).reshape(-1, quarter_w)  40.3 us
    ppermute x7, starting transfers between devices, gathered_columns(): lax.ppermute(held, 'ctx', [(i, i ^ 1 << bit) for i in range(count)])  35.9 us
    ppermute x7, waiting for transfers between devices, gathered_columns(): lax.ppermute(held, 'ctx', [(i, i ^ 1 << bit) for i in range(count)])  27.9 us
    ppermute x3, waiting for transfers between devices, body(): lax.ppermute(sent, 'tp', [(i, (i + step) % tp_count) for i in range(tp_co...  21.6 us
    all_to_all x1, starting transfers between devices, body(): lax.all_to_all(result, 'ctx', 0, 0, tiled=True).reshape(-1, quarter_w)  12.9 us
  transfers between devices with their start and end apart: 19, of which 16 were waited for; matrix products, arithmetic and copies ran while one was open for 4% of the time, Pallas kernels for 0%

profile of v3, /device:TPU:1, one launch (start us, length us, event | category | flops | bytes accessed | tf_op | source)
XLA Modules:
  0.0 355.3 jit_solution(14169783674531006089)
XLA Ops:
  0.0 8.4 %collective-permute-start.1 = (bf16[12,512]{1,0:T(8,128)(2,1)}, bf16[12,512]{1,0:T(8,128)(2,1)S(1)}, u32[]{:S(2)}, u32[]{:S(2)}) collective-permute-start(bf16[12,512]{1,0:T(8,128)(2,1)} %bitcast.140), channel_id=1, source_target_pairs={{0,256},{4,260},{8,264},{12,268},{16,272},{20,276},{24,280},{28,28... | collective-permute-start | bytes 36872 | tf_op jit(solution)/shard_map/ppermute | solution.py:30
  8.4 1.3 collective-permute-done.1
  9.7 0.7 select_bitcast_fusion.11
  10.5 10.6 %collective-permute-start.2 = (bf16[2,12,512]{2,1,0:T(8,128)(2,1)S(1)}, bf16[2,12,512]{2,1,0:T(8,128)(2,1)S(1)}, u32[]{:S(2)}, u32[]{:S(2)}) collective-permute-start(bf16[2,12,512]{2,1,0:T(8,128)(2,1)S(1)} %pad_maximum_fusion.7), channel_id=1, source_target_pairs={{0,32},{4,36},{8,40},{12,44},{16,48},{20,52},{24,56},{28,60},{32,0... | collective-permute-start | bytes 73736 | tf_op jit(solution)/shard_map/ppermute | solution.py:30
  21.1 1.3 collective-permute-done.2
  22.5 4.2 %collective-permute-start.3 = (bf16[2,2,12,512]{3,2,1,0:T(8,128)(2,1)S(1)}, bf16[2,2,12,512]{3,2,1,0:T(8,128)(2,1)S(1)}, u32[]{:S(2)}, u32[]{:S(2)}) collective-permute-start(bf16[2,2,12,512]{3,2,1,0:T(8,128)(2,1)S(1)} %pad_maximum_fusion.5), channel_id=1, source_target_pairs={{0,128},{4,132},{8,136},{12,140},{16,144},{20,148},{24,152},{28,15... | collective-permute-start | bytes 147464 | tf_op jit(solution)/shard_map/ppermute | solution.py:30
  26.6 0.9 copy.53
  27.5 6.2 %collective-permute-start = (bf16[128,1,128]{0,2,1:T(8,128)(2,1)S(1)}, bf16[128,1,128]{0,2,1:T(8,128)(2,1)S(1)}, u32[]{:S(2)}, u32[]{:S(2)}) collective-permute-start(bf16[128,1,128]{0,2,1:T(8,128)(2,1)S(1)} %copy.53), channel_id=1, source_target_pairs={{0,4},{4,8},{8,12},{12,16},{16,20},{20,24},{24,28},{28,32},{32,36}... | collective-permute-start | bytes 98312 | tf_op jit(solution)/shard_map/ppermute | solution.py:12
  33.8 3.6 %collective-permute-start.4 = (bf16[2,2,2,12,512]{4,3,2,1,0:T(8,128)(2,1)S(1)}, bf16[2,2,2,12,512]{4,3,2,1,0:T(8,128)(2,1)S(1)}, u32[]{:S(2)}, u32[]{:S(2)}) collective-permute-start(bf16[2,2,2,12,512]{4,3,2,1,0:T(8,128)(2,1)S(1)} %pad_maximum_fusion.4), channel_id=1, source_target_pairs={{0,16},{4,20},{8,24},{12,28},{16,0},{20,4},{24,8},{28,12},{32,48},... | collective-permute-start | bytes 294920 | tf_op jit(solution)/shard_map/ppermute | solution.py:30
  37.4 7.1 %collective-permute-done.4 = bf16[2,2,2,12,512]{4,3,2,1,0:T(8,128)(2,1)S(1)} collective-permute-done((bf16[2,2,2,12,512]{4,3,2,1,0:T(8,128)(2,1)S(1)}, bf16[2,2,2,12,512]{4,3,2,1,0:T(8,128)(2,1)S(1)}, u32[]{:S(2)}, u32[]{:S(2)}) %collective-permute-start.4) | collective-permute-done | bytes 98336 | tf_op jit(solution)/shard_map/ppermute | solution.py:30
  44.6 2.3 collective-permute-start.5
  47.0 6.6 %collective-permute-done.5 = bf16[2,2,2,2,12,512]{5,4,3,2,1,0:T(8,128)(2,1)S(1)} collective-permute-done((bf16[2,2,2,2,12,512]{5,4,3,2,1,0:T(8,128)(2,1)S(1)}, bf16[2,2,2,2,12,512]{5,4,3,2,1,0:T(8,128)(2,1)S(1)}, u32[]{:S(2)}, u32[]{:S(2)}) %collective-permute-start.5) | collective-permute-done | bytes 196640 | tf_op jit(solution)/shard_map/ppermute | solution.py:30
  53.7 2.3 collective-permute-start.6
  57.0 10.4 %collective-permute-done.6 = bf16[2,2,2,2,2,12,512]{6,5,4,3,2,1,0:T(8,128)(2,1)S(1)} collective-permute-done((bf16[2,2,2,2,2,12,512]{6,5,4,3,2,1,0:T(8,128)(2,1)S(1)}, bf16[2,2,2,2,2,12,512]{6,5,4,3,2,1,0:T(8,128)(2,1)S(1)}, u32[]{:S(2)}, u32[]{:S(2)}) %collective-permute-start.6) | collective-permute-done | bytes 393248 | tf_op jit(solution)/shard_map/ppermute | solution.py:30
  67.6 0.8 copy.57
  68.5 4.4 %collective-permute-start.7 = (bf16[2,2,2,2,2,2,12,512]{7,5,6,4,3,2,1,0:T(2,128)(2,1)S(1)}, bf16[2,2,2,2,2,2,12,512]{7,5,6,4,3,2,1,0:T(2,128)(2,1)S(1)}, u32[]{:S(2)}, u32[]{:S(2)}) collective-permute-start(bf16[2,2,2,2,2,2,12,512]{7,5,6,4,3,2,1,0:T(2,128)(2,1)S(1)} %copy.57), channel_id=1, source_target_pairs={{0,4},{4,0},{8,12},{12,8},{16,20},{20,16},{24,28},{28,24},{32,36},... | collective-permute-start | bytes 2359304 | tf_op jit(solution)/shard_map/ppermute | solution.py:30
  73.6 1.2 collective-permute-done.7
  75.6 1.3 reshape.210
  76.9 2.1 convolution_convert_fusion.4
  79.1 4.6 %collective-permute-start.10 = (bf16[128,1920]{1,0:T(8,128)(2,1)S(1)}, bf16[128,1920]{1,0:T(8,128)(2,1)S(1)}, u32[]{:S(2)}, u32[]{:S(2)}) collective-permute-start(bf16[128,1920]{1,0:T(8,128)(2,1)S(1)} %pad_maximum_fusion.2), channel_id=1, source_target_pairs={{0,3},{1,0},{2,1},{3,2},{4,7},{5,4},{6,5},{7,6},{8,11},{9,8},{10,9... | collective-permute-start | bytes 1474568 | tf_op jit(solution)/shard_map/ppermute | solution.py:108
  83.7 2.4 collective-permute-start.9
  86.1 2.5 collective-permute-start.8
  89.2 15.0 %collective-permute-done.10 = bf16[128,1920]{1,0:T(8,128)(2,1)S(1)} collective-permute-done((bf16[128,1920]{1,0:T(8,128)(2,1)S(1)}, bf16[128,1920]{1,0:T(8,128)(2,1)S(1)}, u32[]{:S(2)}, u32[]{:S(2)}) %collective-permute-start.10) | collective-permute-done | bytes 491552 | tf_op jit(solution)/shard_map/ppermute | solution.py:108
  104.2 6.6 %collective-permute-done.8 = bf16[128,1920]{1,0:T(8,128)(2,1)} collective-permute-done((bf16[128,1920]{1,0:T(8,128)(2,1)S(1)}, bf16[128,1920]{1,0:T(8,128)(2,1)}, u32[]{:S(2)}, u32[]{:S(2)}) %collective-permute-start.8) | collective-permute-done | bytes 491552 | tf_op jit(solution)/shard_map/ppermute | solution.py:108
  110.9 1.2 convert_add_fusion
  112.0 1.1 multiply_reduce_fusion.2
  113.5 2.8 scatter_custom_fusion
  116.3 1.3 reshape.213
  117.6 12.4 %all-to-all-start = ((bf16[128,12,384]{2,1,0:T(8,128)(2,1)}), bf16[128,12,384]{2,1,0:T(8,128)(2,1)}, u32[]{:S(2)}, u32[]{:S(2)}) async-start(bf16[128,12,384]{2,1,0:T(8,128)(2,1)} %reshape.213), calls=%async_computation | async-start | bytes 3145728 | tf_op jit(solution)/shard_map/all_to_all | solution.py:139
  130.1 40.8 %all-to-all-done = bf16[128,12,384]{2,1,0:T(8,128)(2,1)} async-done(((bf16[128,12,384]{2,1,0:T(8,128)(2,1)}), bf16[128,12,384]{2,1,0:T(8,128)(2,1)}, u32[]{:S(2)}, u32[]{:S(2)}) %all-to-all-start) | async-done | bytes 1179680 | tf_op jit(solution)/shard_map/all_to_all | solution.py:139
  170.9 2.3 reshape.214
  173.1 2.2 collective-permute-start.13
  175.4 1.9 fusion.70
  177.2 3.0 collective-permute-start.11
  180.3 2.6 collective-permute-start.12
  182.9 0.9 fusion.24
  183.8 0.9 fusion.30
  184.7 16.5 %collective-permute-done.13 = bf16[1536,384]{1,0:T(8,128)(2,1)S(1)} collective-permute-done((bf16[1536,384]{1,0:T(8,128)(2,1)S(1)}, bf16[1536,384]{1,0:T(8,128)(2,1)S(1)}, u32[]{:S(2)}, u32[]{:S(2)}) %collective-permute-start.13) | collective-permute-done | bytes 1179680 | tf_op jit(solution)/shard_map/ppermute | solution.py:144
  201.2 0.9 fusion.20
  202.1 0.9 fusion.26
  202.9 4.3 %collective-permute-done.11 = bf16[1536,384]{1,0:T(8,128)(2,1)S(1)} collective-permute-done((bf16[1536,384]{1,0:T(8,128)(2,1)S(1)}, bf16[1536,384]{1,0:T(8,128)(2,1)S(1)}, u32[]{:S(2)}, u32[]{:S(2)}) %collective-permute-start.11) | collective-permute-done | bytes 1179680 | tf_op jit(solution)/shard_map/ppermute | solution.py:144
  207.2 0.9 convolution_add_fusion.1
  208.2 0.9 convolution_add_fusion.3
  209.1 21.5 %collective-permute-done.12 = bf16[1536,384]{1,0:T(8,128)(2,1)S(1)} collective-permute-done((bf16[1536,384]{1,0:T(8,128)(2,1)S(1)}, bf16[1536,384]{1,0:T(8,128)(2,1)S(1)}, u32[]{:S(2)}, u32[]{:S(2)}) %collective-permute-start.12) | collective-permute-done | bytes 1179680 | tf_op jit(solution)/shard_map/ppermute | solution.py:144
  230.5 0.9 fusion
  231.4 1.4 fusion.5
  232.8 0.9 convolution_convert_fusion
  233.7 1.9 collective-permute-start.16
  235.7 0.9 convolution_convert_fusion.1
  236.5 4.3 %collective-permute-start.15 = (bf16[1536,384]{1,0:T(8,128)(2,1)S(1)}, bf16[1536,384]{1,0:T(8,128)(2,1)S(1)}, u32[]{:S(2)}, u32[]{:S(2)}) collective-permute-start(bf16[1536,384]{1,0:T(8,128)(2,1)S(1)} %convolution_convert_fusion.1), channel_id=1, source_target_pairs={{0,2},{1,3},{2,0},{3,1},{4,6},{5,7},{6,4},{7,5},{8,10},{9,11},{10,... | collective-permute-start | bytes 3538952 | tf_op jit(solution)/shard_map/ppermute | solution.py:165
  240.9 0.9 convolution_convert_fusion.2
  241.7 2.8 collective-permute-start.14
  244.5 13.3 %collective-permute-done.16 = bf16[1536,384]{1,0:T(8,128)(2,1)S(1)} collective-permute-done((bf16[1536,384]{1,0:T(8,128)(2,1)S(1)}, bf16[1536,384]{1,0:T(8,128)(2,1)S(1)}, u32[]{:S(2)}, u32[]{:S(2)}) %collective-permute-start.16) | collective-permute-done | bytes 1179680 | tf_op jit(solution)/shard_map/ppermute | solution.py:165
  257.8 5.7 %collective-permute-done.15 = bf16[1536,384]{1,0:T(8,128)(2,1)S(1)} collective-permute-done((bf16[1536,384]{1,0:T(8,128)(2,1)S(1)}, bf16[1536,384]{1,0:T(8,128)(2,1)S(1)}, u32[]{:S(2)}, u32[]{:S(2)}) %collective-permute-start.15) | collective-permute-done | bytes 1179680 | tf_op jit(solution)/shard_map/ppermute | solution.py:165
  263.6 29.5 %collective-permute-done.14 = bf16[1536,384]{1,0:T(8,128)(2,1)S(1)} collective-permute-done((bf16[1536,384]{1,0:T(8,128)(2,1)S(1)}, bf16[1536,384]{1,0:T(8,128)(2,1)S(1)}, u32[]{:S(2)}, u32[]{:S(2)}) %collective-permute-start.14) | collective-permute-done | bytes 1179680 | tf_op jit(solution)/shard_map/ppermute | solution.py:165
  293.1 1.3 add_convert_fusion
  294.4 1.3 reshape.215
  295.7 12.9 %all-to-all-start.1 = ((bf16[128,12,384]{2,1,0:T(8,128)(2,1)}), bf16[128,12,384]{2,1,0:T(8,128)(2,1)}, u32[]{:S(2)}, u32[]{:S(2)}) async-start(bf16[128,12,384]{2,1,0:T(8,128)(2,1)} %reshape.215), calls=%async_computation.1 | async-start | bytes 3145728 | tf_op jit(solution)/shard_map/all_to_all | solution.py:171
  308.6 0.5 slice_bitcast_fusion.3
  309.1 40.3 %all-to-all-done.1 = bf16[128,12,384]{2,1,0:T(8,128)(2,1)} async-done(((bf16[128,12,384]{2,1,0:T(8,128)(2,1)}), bf16[128,12,384]{2,1,0:T(8,128)(2,1)}, u32[]{:S(2)}, u32[]{:S(2)}) %all-to-all-start.1) | async-done | bytes 1179680 | tf_op jit(solution)/shard_map/all_to_all | solution.py:171
  349.4 2.3 reshape.216
  351.7 1.9 gather_fusion
  353.7 0.6 fusion.71
  354.5 0.8 fusion.46
  (62 shorter events, 4.1 us)
Async XLA Ops:
  0.0 232.8 %copy-start = (bf16[1,384,1536]{2,1,0:T(8,128)(2,1)S(1)}, bf16[1,384,1536]{2,1,0:T(8,128)(2,1)}, u32[]{:S(2)}) copy-start(bf16[1,384,1536]{2,1,0:T(8,128)(2,1)} %param.17) | copy-start | bytes 3538948
  0.0 9.7 %collective-permute-start.1 = (bf16[12,512]{1,0:T(8,128)(2,1)}, bf16[12,512]{1,0:T(8,128)(2,1)S(1)}, u32[]{:S(2)}, u32[]{:S(2)}) collective-permute-start(bf16[12,512]{1,0:T(8,128)(2,1)} %bitcast.140), channel_id=1, source_target_pairs={{0,256},{4,260},{8,264},{12,268},{16,272},{20,276},{24,280},{28,28... | collective-permute-start | bytes 36872 | tf_op jit(solution)/shard_map/ppermute | solution.py:30
  10.5 12.0 %collective-permute-start.2 = (bf16[2,12,512]{2,1,0:T(8,128)(2,1)S(1)}, bf16[2,12,512]{2,1,0:T(8,128)(2,1)S(1)}, u32[]{:S(2)}, u32[]{:S(2)}) collective-permute-start(bf16[2,12,512]{2,1,0:T(8,128)(2,1)S(1)} %pad_maximum_fusion.7), channel_id=1, source_target_pairs={{0,32},{4,36},{8,40},{12,44},{16,48},{20,52},{24,56},{28,60},{32,0... | collective-permute-start | bytes 73736 | tf_op jit(solution)/shard_map/ppermute | solution.py:30
  22.5 11.2 %collective-permute-start.3 = (bf16[2,2,12,512]{3,2,1,0:T(8,128)(2,1)S(1)}, bf16[2,2,12,512]{3,2,1,0:T(8,128)(2,1)S(1)}, u32[]{:S(2)}, u32[]{:S(2)}) collective-permute-start(bf16[2,2,12,512]{3,2,1,0:T(8,128)(2,1)S(1)} %pad_maximum_fusion.5), channel_id=1, source_target_pairs={{0,128},{4,132},{8,136},{12,140},{16,144},{20,148},{24,152},{28,15... | collective-permute-start | bytes 147464 | tf_op jit(solution)/shard_map/ppermute | solution.py:30
  27.5 29.1 %collective-permute-start = (bf16[128,1,128]{0,2,1:T(8,128)(2,1)S(1)}, bf16[128,1,128]{0,2,1:T(8,128)(2,1)S(1)}, u32[]{:S(2)}, u32[]{:S(2)}) collective-permute-start(bf16[128,1,128]{0,2,1:T(8,128)(2,1)S(1)} %copy.53), channel_id=1, source_target_pairs={{0,4},{4,8},{8,12},{12,16},{16,20},{20,24},{24,28},{28,32},{32,36}... | collective-permute-start | bytes 98312 | tf_op jit(solution)/shard_map/ppermute | solution.py:12
  33.8 10.7 %collective-permute-start.4 = (bf16[2,2,2,12,512]{4,3,2,1,0:T(8,128)(2,1)S(1)}, bf16[2,2,2,12,512]{4,3,2,1,0:T(8,128)(2,1)S(1)}, u32[]{:S(2)}, u32[]{:S(2)}) collective-permute-start(bf16[2,2,2,12,512]{4,3,2,1,0:T(8,128)(2,1)S(1)} %pad_maximum_fusion.4), channel_id=1, source_target_pairs={{0,16},{4,20},{8,24},{12,28},{16,0},{20,4},{24,8},{28,12},{32,48},... | collective-permute-start | bytes 294920 | tf_op jit(solution)/shard_map/ppermute | solution.py:30
  44.6 11.6 %copy-start.4 = (s32[128,4]{0,1:T(4,128)S(1)}, s32[128,4]{0,1:T(4,128)}, u32[]{:S(2)}) copy-start(s32[128,4]{0,1:T(4,128)} %param.18) | copy-start | bytes 6148
  44.6 9.0 %collective-permute-start.5 = (bf16[2,2,2,2,12,512]{5,4,3,2,1,0:T(8,128)(2,1)S(1)}, bf16[2,2,2,2,12,512]{5,4,3,2,1,0:T(8,128)(2,1)S(1)}, u32[]{:S(2)}, u32[]{:S(2)}) collective-permute-start(bf16[2,2,2,2,12,512]{5,4,3,2,1,0:T(8,128)(2,1)S(1)} %pad_maximum_fusion.3), channel_id=1, source_target_pairs={{0,64},{4,68},{8,72},{12,76},{16,80},{20,84},{24,88},{28,92},{32,9... | collective-permute-start | bytes 589832 | tf_op jit(solution)/shard_map/ppermute | solution.py:30
  47.0 9.5 %copy-start.3 = (bf16[128,512]{1,0:T(8,128)(2,1)S(1)}, bf16[128,512]{1,0:T(8,128)(2,1)}, u32[]{:S(2)}) copy-start(bf16[128,512]{1,0:T(8,128)(2,1)} %param.11) | copy-start | bytes 393220
  53.7 13.7 %collective-permute-start.6 = (bf16[2,2,2,2,2,12,512]{6,5,4,3,2,1,0:T(8,128)(2,1)S(1)}, bf16[2,2,2,2,2,12,512]{6,5,4,3,2,1,0:T(8,128)(2,1)S(1)}, u32[]{:S(2)}, u32[]{:S(2)}) collective-permute-start(bf16[2,2,2,2,2,12,512]{6,5,4,3,2,1,0:T(8,128)(2,1)S(1)} %pad_maximum_fusion.1), channel_id=1, source_target_pairs={{0,8},{4,12},{8,0},{12,4},{16,24},{20,28},{24,16},{28,20},{32,40},... | collective-permute-start | bytes 1179656 | tf_op jit(solution)/shard_map/ppermute | solution.py:30
  67.6 5.3 %copy-start.8 = (f32[8]{0:T(128)S(1)}, f32[8]{0:T(128)}, u32[]{:S(2)}) copy-start(f32[8]{0:T(128)} %param.13) | copy-start | bytes 100
  68.5 6.3 %collective-permute-start.7 = (bf16[2,2,2,2,2,2,12,512]{7,5,6,4,3,2,1,0:T(2,128)(2,1)S(1)}, bf16[2,2,2,2,2,2,12,512]{7,5,6,4,3,2,1,0:T(2,128)(2,1)S(1)}, u32[]{:S(2)}, u32[]{:S(2)}) collective-permute-start(bf16[2,2,2,2,2,2,12,512]{7,5,6,4,3,2,1,0:T(2,128)(2,1)S(1)} %copy.57), channel_id=1, source_target_pairs={{0,4},{4,0},{8,12},{12,8},{16,20},{20,16},{24,28},{28,24},{32,36},... | collective-permute-start | bytes 2359304 | tf_op jit(solution)/shard_map/ppermute | solution.py:30
  76.9 2.1 copy-start.1
  79.1 25.2 %collective-permute-start.10 = (bf16[128,1920]{1,0:T(8,128)(2,1)S(1)}, bf16[128,1920]{1,0:T(8,128)(2,1)S(1)}, u32[]{:S(2)}, u32[]{:S(2)}) collective-permute-start(bf16[128,1920]{1,0:T(8,128)(2,1)S(1)} %pad_maximum_fusion.2), channel_id=1, source_target_pairs={{0,3},{1,0},{2,1},{3,2},{4,7},{5,4},{6,5},{7,6},{8,11},{9,8},{10,9... | collective-permute-start | bytes 1474568 | tf_op jit(solution)/shard_map/ppermute | solution.py:108
  83.7 20.6 %collective-permute-start.9 = (bf16[128,1920]{1,0:T(8,128)(2,1)S(1)}, bf16[128,1920]{1,0:T(8,128)(2,1)S(1)}, u32[]{:S(2)}, u32[]{:S(2)}) collective-permute-start(bf16[128,1920]{1,0:T(8,128)(2,1)S(1)} %pad_maximum_fusion.2), channel_id=1, source_target_pairs={{0,2},{1,3},{2,0},{3,1},{4,6},{5,7},{6,4},{7,5},{8,10},{9,11},{10,... | collective-permute-start | bytes 1474568 | tf_op jit(solution)/shard_map/ppermute | solution.py:108
  86.1 24.7 %collective-permute-start.8 = (bf16[128,1920]{1,0:T(8,128)(2,1)S(1)}, bf16[128,1920]{1,0:T(8,128)(2,1)}, u32[]{:S(2)}, u32[]{:S(2)}) collective-permute-start(bf16[128,1920]{1,0:T(8,128)(2,1)S(1)} %pad_maximum_fusion.2), channel_id=1, source_target_pairs={{0,1},{1,2},{2,3},{3,0},{4,5},{5,6},{6,7},{7,4},{8,9},{9,10},{10,1... | collective-permute-start | bytes 1474568 | tf_op jit(solution)/shard_map/ppermute | solution.py:108
  112.0 1.1 copy-start.6
  117.6 53.3 %all-to-all-start = ((bf16[128,12,384]{2,1,0:T(8,128)(2,1)}), bf16[128,12,384]{2,1,0:T(8,128)(2,1)}, u32[]{:S(2)}, u32[]{:S(2)}) async-start(bf16[128,12,384]{2,1,0:T(8,128)(2,1)} %reshape.213), calls=%async_computation | async-start | bytes 3145728 | tf_op jit(solution)/shard_map/all_to_all | solution.py:139
  173.1 28.1 %collective-permute-start.13 = (bf16[1536,384]{1,0:T(8,128)(2,1)S(1)}, bf16[1536,384]{1,0:T(8,128)(2,1)S(1)}, u32[]{:S(2)}, u32[]{:S(2)}) collective-permute-start(bf16[1536,384]{1,0:T(8,128)(2,1)S(1)} %reshape.214), channel_id=1, source_target_pairs={{0,3},{1,0},{2,1},{3,2},{4,7},{5,4},{6,5},{7,6},{8,11},{9,8},{10,9... | collective-permute-start | bytes 3538952 | tf_op jit(solution)/shard_map/ppermute | solution.py:144
  177.2 30.0 %collective-permute-start.11 = (bf16[1536,384]{1,0:T(8,128)(2,1)S(1)}, bf16[1536,384]{1,0:T(8,128)(2,1)S(1)}, u32[]{:S(2)}, u32[]{:S(2)}) collective-permute-start(bf16[1536,384]{1,0:T(8,128)(2,1)S(1)} %reshape.214), channel_id=1, source_target_pairs={{0,1},{1,2},{2,3},{3,0},{4,5},{5,6},{6,7},{7,4},{8,9},{9,10},{10,1... | collective-permute-start | bytes 3538952 | tf_op jit(solution)/shard_map/ppermute | solution.py:144
  180.3 50.2 %collective-permute-start.12 = (bf16[1536,384]{1,0:T(8,128)(2,1)S(1)}, bf16[1536,384]{1,0:T(8,128)(2,1)S(1)}, u32[]{:S(2)}, u32[]{:S(2)}) collective-permute-start(bf16[1536,384]{1,0:T(8,128)(2,1)S(1)} %reshape.214), channel_id=1, source_target_pairs={{0,2},{1,3},{2,0},{3,1},{4,6},{5,7},{6,4},{7,5},{8,10},{9,11},{10,... | collective-permute-start | bytes 3538952 | tf_op jit(solution)/shard_map/ppermute | solution.py:144
  233.7 24.1 %collective-permute-start.16 = (bf16[1536,384]{1,0:T(8,128)(2,1)S(1)}, bf16[1536,384]{1,0:T(8,128)(2,1)S(1)}, u32[]{:S(2)}, u32[]{:S(2)}) collective-permute-start(bf16[1536,384]{1,0:T(8,128)(2,1)S(1)} %convolution_convert_fusion), channel_id=1, source_target_pairs={{0,3},{1,0},{2,1},{3,2},{4,7},{5,4},{6,5},{7,6},{8,11},{9,8},{10,9... | collective-permute-start | bytes 3538952 | tf_op jit(solution)/shard_map/ppermute | solution.py:165
  236.5 27.0 %collective-permute-start.15 = (bf16[1536,384]{1,0:T(8,128)(2,1)S(1)}, bf16[1536,384]{1,0:T(8,128)(2,1)S(1)}, u32[]{:S(2)}, u32[]{:S(2)}) collective-permute-start(bf16[1536,384]{1,0:T(8,128)(2,1)S(1)} %convolution_convert_fusion.1), channel_id=1, source_target_pairs={{0,2},{1,3},{2,0},{3,1},{4,6},{5,7},{6,4},{7,5},{8,10},{9,11},{10,... | collective-permute-start | bytes 3538952 | tf_op jit(solution)/shard_map/ppermute | solution.py:165
  241.7 51.4 %collective-permute-start.14 = (bf16[1536,384]{1,0:T(8,128)(2,1)S(1)}, bf16[1536,384]{1,0:T(8,128)(2,1)S(1)}, u32[]{:S(2)}, u32[]{:S(2)}) collective-permute-start(bf16[1536,384]{1,0:T(8,128)(2,1)S(1)} %convolution_convert_fusion.2), channel_id=1, source_target_pairs={{0,1},{1,2},{2,3},{3,0},{4,5},{5,6},{6,7},{7,4},{8,9},{9,10},{10,1... | collective-permute-start | bytes 3538952 | tf_op jit(solution)/shard_map/ppermute | solution.py:165
  295.7 12.9 %copy-start.5 = (f32[128,4]{0,1:T(4,128)S(1)}, f32[128,4]{0,1:T(4,128)}, u32[]{:S(2)}) copy-start(f32[128,4]{0,1:T(4,128)} %param.19) | copy-start | bytes 6148
  295.7 53.7 %all-to-all-start.1 = ((bf16[128,12,384]{2,1,0:T(8,128)(2,1)}), bf16[128,12,384]{2,1,0:T(8,128)(2,1)}, u32[]{:S(2)}, u32[]{:S(2)}) async-start(bf16[128,12,384]{2,1,0:T(8,128)(2,1)} %reshape.215), calls=%async_computation.1 | async-start | bytes 3145728 | tf_op jit(solution)/shard_map/all_to_all | solution.py:171
  353.6 0.9 copy-start.2
  353.6 0.9 copy-start.7

commit v4 on v3

--- a/solution.py
+++ b/solution.py
@@ -139,10 +139,21 @@
     arrived = lax.all_to_all(
         outbox.reshape(ctx_count, capacity, quarter_w), "ctx", 0, 0, tiled=True
     ).reshape(-1, quarter_w)
-    pieces = [(arrived, tp_index)]
-    for step in range(1, tp_count):
-        got = lax.ppermute(arrived, "tp", [(i, (i + step) % tp_count) for i in range(tp_count)])
-        pieces.append((got, (tp_index - step) % tp_count))
+    assert tp_count == 4
+    ahead = [(i, (i + 1) % tp_count) for i in range(tp_count)]
+    behind = [(i, (i - 1) % tp_count) for i in range(tp_count)]
+    half_rows = arrived.shape[0] // 2
+    from_behind = lax.ppermute(arrived, "tp", ahead)
+    from_ahead = lax.ppermute(arrived, "tp", behind)
+    first_half = lax.ppermute(from_behind[:half_rows], "tp", ahead)
+    second_half = lax.ppermute(from_ahead[half_rows:], "tp", behind)
+    opposite = jnp.concatenate([first_half, second_half], 0)
+    pieces = [
+        (arrived, tp_index),
+        (from_behind, (tp_index - 1) % tp_count),
+        (from_ahead, (tp_index + 1) % tp_count),
+        (opposite, (tp_index + 2) % tp_count),
+    ]
     gate_vals = None
     up_vals = None
     for piece, quarter_id in pieces:
@@ -158,15 +169,24 @@
         cols = lax.dynamic_slice_in_dim(expert_out[0], quarter_id * quarter_w, quarter_w, 1)
         return jnp.dot(activated, cols, preferred_element_type=jnp.float32).astype(jnp.bfloat16)
 
-    arriving = []
-    for step in range(1, tp_count):
-        piece = partial_for((tp_index + step) % tp_count)
-        arriving.append(
-            lax.ppermute(piece, "tp", [(i, (i + step) % tp_count) for i in range(tp_count)])
-        )
-    summed = partial_for(tp_index).astype(jnp.float32)
-    for got in arriving:
-        summed = summed + got.astype(jnp.float32)
+    across = partial_for((tp_index + 2) % tp_count)
+    via_ahead = lax.ppermute(across[:half_rows], "tp", ahead)
+    via_behind = lax.ppermute(across[half_rows:], "tp", behind)
+    for_ahead = partial_for((tp_index + 1) % tp_count).astype(jnp.float32)
+    for_ahead = jnp.concatenate(
+        [for_ahead[:half_rows] + via_ahead.astype(jnp.float32), for_ahead[half_rows:]], 0
+    ).astype(jnp.bfloat16)
+    for_behind = partial_for((tp_index - 1) % tp_count).astype(jnp.float32)
+    for_behind = jnp.concatenate(
+        [for_behind[:half_rows], for_behind[half_rows:] + via_behind.astype(jnp.float32)], 0
+    ).astype(jnp.bfloat16)
+    got_behind = lax.ppermute(for_ahead, "tp", ahead)
+    got_ahead = lax.ppermute(for_behind, "tp", behind)
+    summed = (
+        partial_for(tp_index).astype(jnp.float32)
+        + got_behind.astype(jnp.float32)
+        + got_ahead.astype(jnp.float32)
+    )
     result = summed.astype(jnp.bfloat16).reshape(ctx_count, capacity, quarter_w)
     returned = lax.all_to_all(result, "ctx", 0, 0, tiled=True).reshape(-1, quarter_w)
     expert_result = returned[flat_index].reshape(tok_rows, top_count, quarter_w)

time: 357 us -> 337 us (0.944)
  waiting for transfers between devices: 221 us -> 181 us
  starting transfers between devices: 93.8 us -> 112 us
    ppermute x6 -> x8, waiting for transfers between devices: 90.9 us -> 53.7 us  [the longest x1 18.9 us: body(): from_behind = lax.ppermute(arrived, 'tp', ahead)]
    ppermute x6 -> x8, starting transfers between devices: 16.9 us -> 27.1 us  [the longest x1 5.32 us: body(): via_behind = lax.ppermute(across[half_rows:], 'tp', behind)]
    all_to_all x1, starting transfers between devices: 12.9 us -> 18 us  [body(): lax.all_to_all(result, 'ctx', 0, 0, tiled=True).reshape(-1, quarter_w)]
  transfers between devices with their start and end apart: 19 -> 21, of which waited for: 16 -> 16; matrix products, arithmetic and copies ran while one was open for 4% -> 4% of each run, Pallas kernels for 0% -> 0%
where the time goes in v4:
time: 337 us; the launch traced here: 335 us
  waiting for transfers between devices  181 us (54%)
  starting transfers between devices  112 us (33%)
  local copies, waits for them, and re-layouts  19.4 us (6%)
  matrix products  14 us (4%)
  other arithmetic  7.07 us (2%)
    all_to_all x1, waiting for transfers between devices, body(): lax.all_to_all(outbox.reshape(ctx_count, capacity, quarter_w), 'ctx', 0,...  40.8 us
    all_to_all x1, waiting for transfers between devices, body(): lax.all_to_all(result, 'ctx', 0, 0, tiled=True).reshape(-1, quarter_w)  40.3 us
    ppermute x7, starting transfers between devices, gathered_columns(): lax.ppermute(held, 'ctx', [(i, i ^ 1 << bit) for i in range(count)])  36 us
    ppermute x7, waiting for transfers between devices, gathered_columns(): lax.ppermute(held, 'ctx', [(i, i ^ 1 << bit) for i in range(count)])  27.9 us
    ppermute x1, waiting for transfers between devices, body(): from_behind = lax.ppermute(arrived, 'tp', ahead)  18.9 us
    ppermute x3, waiting for transfers between devices, body(): lax.ppermute(sent, 'tp', [(i, (i + step) % tp_count) for i in range(tp_co...  18.8 us
    ppermute x1, waiting for transfers between devices, body(): got_behind = lax.ppermute(for_ahead, 'tp', ahead)  18.8 us
    all_to_all x1, starting transfers between devices, body(): lax.all_to_all(result, 'ctx', 0, 0, tiled=True).reshape(-1, quarter_w)  18 us
  transfers between devices with their start and end apart: 21, of which 16 were waited for; matrix products, arithmetic and copies ran while one was open for 4% of the time, Pallas kernels for 0%

profile of v4, /device:TPU:1, one launch (start us, length us, event | category | flops | bytes accessed | tf_op | source)
XLA Modules:
  0.0 334.6 jit_solution(2023560368439126704)
XLA Ops:
  0.0 8.4 %collective-permute-start.1 = (bf16[12,512]{1,0:T(8,128)(2,1)}, bf16[12,512]{1,0:T(8,128)(2,1)S(1)}, u32[]{:S(2)}, u32[]{:S(2)}) collective-permute-start(bf16[12,512]{1,0:T(8,128)(2,1)} %bitcast.138), channel_id=1, source_target_pairs={{0,256},{4,260},{8,264},{12,268},{16,272},{20,276},{24,280},{28,28... | collective-permute-start | bytes 36872 | tf_op jit(solution)/shard_map/ppermute | solution.py:30
  8.4 1.3 collective-permute-done.1
  9.7 0.7 select_bitcast_fusion.11
  10.5 10.6 %collective-permute-start.2 = (bf16[2,12,512]{2,1,0:T(8,128)(2,1)S(1)}, bf16[2,12,512]{2,1,0:T(8,128)(2,1)S(1)}, u32[]{:S(2)}, u32[]{:S(2)}) collective-permute-start(bf16[2,12,512]{2,1,0:T(8,128)(2,1)S(1)} %pad_maximum_fusion.9), channel_id=1, source_target_pairs={{0,32},{4,36},{8,40},{12,44},{16,48},{20,52},{24,56},{28,60},{32,0... | collective-permute-start | bytes 73736 | tf_op jit(solution)/shard_map/ppermute | solution.py:30
  21.1 1.3 collective-permute-done.2
  22.5 4.2 %collective-permute-start.3 = (bf16[2,2,12,512]{3,2,1,0:T(8,128)(2,1)S(1)}, bf16[2,2,12,512]{3,2,1,0:T(8,128)(2,1)S(1)}, u32[]{:S(2)}, u32[]{:S(2)}) collective-permute-start(bf16[2,2,12,512]{3,2,1,0:T(8,128)(2,1)S(1)} %pad_maximum_fusion.7), channel_id=1, source_target_pairs={{0,128},{4,132},{8,136},{12,140},{16,144},{20,148},{24,152},{28,15... | collective-permute-start | bytes 147464 | tf_op jit(solution)/shard_map/ppermute | solution.py:30
  26.6 0.9 copy.53
  27.5 6.2 %collective-permute-start = (bf16[128,1,128]{0,2,1:T(8,128)(2,1)S(1)}, bf16[128,1,128]{0,2,1:T(8,128)(2,1)S(1)}, u32[]{:S(2)}, u32[]{:S(2)}) collective-permute-start(bf16[128,1,128]{0,2,1:T(8,128)(2,1)S(1)} %copy.53), channel_id=1, source_target_pairs={{0,4},{4,8},{8,12},{12,16},{16,20},{20,24},{24,28},{28,32},{32,36}... | collective-permute-start | bytes 98312 | tf_op jit(solution)/shard_map/ppermute | solution.py:12
  33.8 3.6 %collective-permute-start.4 = (bf16[2,2,2,12,512]{4,3,2,1,0:T(8,128)(2,1)S(1)}, bf16[2,2,2,12,512]{4,3,2,1,0:T(8,128)(2,1)S(1)}, u32[]{:S(2)}, u32[]{:S(2)}) collective-permute-start(bf16[2,2,2,12,512]{4,3,2,1,0:T(8,128)(2,1)S(1)} %pad_maximum_fusion.6), channel_id=1, source_target_pairs={{0,16},{4,20},{8,24},{12,28},{16,0},{20,4},{24,8},{28,12},{32,48},... | collective-permute-start | bytes 294920 | tf_op jit(solution)/shard_map/ppermute | solution.py:30
  37.4 7.1 %collective-permute-done.4 = bf16[2,2,2,12,512]{4,3,2,1,0:T(8,128)(2,1)S(1)} collective-permute-done((bf16[2,2,2,12,512]{4,3,2,1,0:T(8,128)(2,1)S(1)}, bf16[2,2,2,12,512]{4,3,2,1,0:T(8,128)(2,1)S(1)}, u32[]{:S(2)}, u32[]{:S(2)}) %collective-permute-start.4) | collective-permute-done | bytes 98336 | tf_op jit(solution)/shard_map/ppermute | solution.py:30
  44.6 2.5 collective-permute-start.5
  47.1 6.6 %collective-permute-done.5 = bf16[2,2,2,2,12,512]{5,4,3,2,1,0:T(8,128)(2,1)S(1)} collective-permute-done((bf16[2,2,2,2,12,512]{5,4,3,2,1,0:T(8,128)(2,1)S(1)}, bf16[2,2,2,2,12,512]{5,4,3,2,1,0:T(8,128)(2,1)S(1)}, u32[]{:S(2)}, u32[]{:S(2)}) %collective-permute-start.5) | collective-permute-done | bytes 196640 | tf_op jit(solution)/shard_map/ppermute | solution.py:30
  53.8 2.3 collective-permute-start.6
  57.1 10.4 %collective-permute-done.6 = bf16[2,2,2,2,2,12,512]{6,5,4,3,2,1,0:T(8,128)(2,1)S(1)} collective-permute-done((bf16[2,2,2,2,2,12,512]{6,5,4,3,2,1,0:T(8,128)(2,1)S(1)}, bf16[2,2,2,2,2,12,512]{6,5,4,3,2,1,0:T(8,128)(2,1)S(1)}, u32[]{:S(2)}, u32[]{:S(2)}) %collective-permute-start.6) | collective-permute-done | bytes 393248 | tf_op jit(solution)/shard_map/ppermute | solution.py:30
  67.8 0.8 copy.57
  68.6 4.4 %collective-permute-start.7 = (bf16[2,2,2,2,2,2,12,512]{7,5,6,4,3,2,1,0:T(2,128)(2,1)S(1)}, bf16[2,2,2,2,2,2,12,512]{7,5,6,4,3,2,1,0:T(2,128)(2,1)S(1)}, u32[]{:S(2)}, u32[]{:S(2)}) collective-permute-start(bf16[2,2,2,2,2,2,12,512]{7,5,6,4,3,2,1,0:T(2,128)(2,1)S(1)} %copy.57), channel_id=1, source_target_pairs={{0,4},{4,0},{8,12},{12,8},{16,20},{20,16},{24,28},{28,24},{32,36},... | collective-permute-start | bytes 2359304 | tf_op jit(solution)/shard_map/ppermute | solution.py:30
  73.8 1.2 collective-permute-done.7
  75.7 1.4 reshape.210
  77.1 2.1 convolution_convert_fusion.4
  79.2 4.6 %collective-permute-start.10 = (bf16[128,1920]{1,0:T(8,128)(2,1)S(1)}, bf16[128,1920]{1,0:T(8,128)(2,1)S(1)}, u32[]{:S(2)}, u32[]{:S(2)}) collective-permute-start(bf16[128,1920]{1,0:T(8,128)(2,1)S(1)} %pad_maximum_fusion.4), channel_id=1, source_target_pairs={{0,3},{1,0},{2,1},{3,2},{4,7},{5,4},{6,5},{7,6},{8,11},{9,8},{10,9... | collective-permute-start | bytes 1474568 | tf_op jit(solution)/shard_map/ppermute | solution.py:108
  83.8 1.9 collective-permute-start.8
  85.8 3.6 %collective-permute-start.9 = (bf16[128,1920]{1,0:T(8,128)(2,1)S(1)}, bf16[128,1920]{1,0:T(8,128)(2,1)}, u32[]{:S(2)}, u32[]{:S(2)}) collective-permute-start(bf16[128,1920]{1,0:T(8,128)(2,1)S(1)} %pad_maximum_fusion.4), channel_id=1, source_target_pairs={{0,2},{1,3},{2,0},{3,1},{4,6},{5,7},{6,4},{7,5},{8,10},{9,11},{10,... | collective-permute-start | bytes 1474568 | tf_op jit(solution)/shard_map/ppermute | solution.py:108
  90.0 14.4 %collective-permute-done.10 = bf16[128,1920]{1,0:T(8,128)(2,1)S(1)} collective-permute-done((bf16[128,1920]{1,0:T(8,128)(2,1)S(1)}, bf16[128,1920]{1,0:T(8,128)(2,1)S(1)}, u32[]{:S(2)}, u32[]{:S(2)}) %collective-permute-start.10) | collective-permute-done | bytes 491552 | tf_op jit(solution)/shard_map/ppermute | solution.py:108
  104.4 4.4 %collective-permute-done.9 = bf16[128,1920]{1,0:T(8,128)(2,1)} collective-permute-done((bf16[128,1920]{1,0:T(8,128)(2,1)S(1)}, bf16[128,1920]{1,0:T(8,128)(2,1)}, u32[]{:S(2)}, u32[]{:S(2)}) %collective-permute-start.9) | collective-permute-done | bytes 491552 | tf_op jit(solution)/shard_map/ppermute | solution.py:108
  108.8 1.2 convert_add_fusion
  110.0 1.1 multiply_reduce_fusion.2
  111.5 2.8 scatter_custom_fusion
  114.2 1.3 reshape.213
  115.5 14.2 %all-to-all-start = ((bf16[128,12,384]{2,1,0:T(8,128)(2,1)}), bf16[128,12,384]{2,1,0:T(8,128)(2,1)}, u32[]{:S(2)}, u32[]{:S(2)}) async-start(bf16[128,12,384]{2,1,0:T(8,128)(2,1)} %reshape.213), calls=%async_computation | async-start | bytes 3145728 | tf_op jit(solution)/shard_map/all_to_all | solution.py:139
  129.8 40.8 %all-to-all-done = bf16[128,12,384]{2,1,0:T(8,128)(2,1)} async-done(((bf16[128,12,384]{2,1,0:T(8,128)(2,1)}), bf16[128,12,384]{2,1,0:T(8,128)(2,1)}, u32[]{:S(2)}, u32[]{:S(2)}) %all-to-all-start) | async-done | bytes 1179680 | tf_op jit(solution)/shard_map/all_to_all | solution.py:139
  170.6 2.3 reshape.214
  172.9 1.9 collective-permute-start.11
  174.8 4.8 %collective-permute-start.12 = (bf16[1536,384]{1,0:T(8,128)(2,1)S(1)}, bf16[1536,384]{1,0:T(8,128)(2,1)S(1)}, u32[]{:S(2)}, u32[]{:S(2)}) collective-permute-start(bf16[1536,384]{1,0:T(8,128)(2,1)S(1)} %reshape.214), channel_id=1, source_target_pairs={{0,3},{1,0},{2,1},{3,2},{4,7},{5,4},{6,5},{7,6},{8,11},{9,8},{10,9... | collective-permute-start | bytes 3538952 | tf_op jit(solution)/shard_map/ppermute | solution.py:147
  179.6 1.9 fusion.68
  181.4 0.9 fusion.28
  182.3 0.9 fusion.22
  183.2 18.9 %collective-permute-done.11 = bf16[1536,384]{1,0:T(8,128)(2,1)S(1)} collective-permute-done((bf16[1536,384]{1,0:T(8,128)(2,1)S(1)}, bf16[1536,384]{1,0:T(8,128)(2,1)S(1)}, u32[]{:S(2)}, u32[]{:S(2)}) %collective-permute-start.11) | collective-permute-done | bytes 1179680 | tf_op jit(solution)/shard_map/ppermute | solution.py:146
  202.2 1.9 collective-permute-start.13
  204.2 4.6 %collective-permute-start.14 = (bf16[768,384]{1,0:T(8,128)(2,1)S(1)}, bf16[768,384]{1,0:T(8,128)(2,1)S(1)}, u32[]{:S(2)}, u32[]{:S(2)}) collective-permute-start(bf16[768,384]{1,0:T(8,128)(2,1)S(1)} %slice.131), channel_id=1, source_target_pairs={{0,3},{1,0},{2,1},{3,2},{4,7},{5,4},{6,5},{7,6},{8,11},{9,8},{10,9... | collective-permute-start | bytes 1769480 | tf_op jit(solution)/shard_map/ppermute | solution.py:149
  208.8 0.9 convolution_add_fusion.3
  209.7 0.9 convolution_add_fusion.1
  210.6 7.3 %collective-permute-done.13 = bf16[768,384]{1,0:T(8,128)(2,1)S(1)} collective-permute-done((bf16[768,384]{1,0:T(8,128)(2,1)S(1)}, bf16[768,384]{1,0:T(8,128)(2,1)S(1)}, u32[]{:S(2)}, u32[]{:S(2)}) %collective-permute-start.13) | collective-permute-done | bytes 589856 | tf_op jit(solution)/shard_map/ppermute | solution.py:148
  218.0 0.9 collective-permute-done.14
  219.1 0.9 fusion.18
  219.9 0.9 fusion.24
  220.8 1.0 fusion
  221.8 1.4 fusion.5
  223.2 0.9 convolution_convert_fusion.1
  224.2 1.9 collective-permute-start.15
  226.2 5.3 %collective-permute-start.17 = (bf16[768,384]{1,0:T(8,128)(2,1)S(1)}, bf16[768,384]{1,0:T(8,128)(2,1)S(1)}, u32[]{:S(2)}, u32[]{:S(2)}) collective-permute-start(bf16[768,384]{1,0:T(8,128)(2,1)S(1)} %get-tuple-element.14), channel_id=1, source_target_pairs={{0,3},{1,0},{2,1},{3,2},{4,7},{5,4},{6,5},{7,6},{8,11},{9,8},{10,9... | collective-permute-start | bytes 1769480 | tf_op jit(solution)/shard_map/ppermute | solution.py:174
  231.5 0.9 convolution_convert_fusion.2
  232.4 0.9 convolution_convert_fusion
  233.4 6.5 %collective-permute-done.15 = bf16[768,384]{1,0:T(8,128)(2,1)S(1)} collective-permute-done((bf16[768,384]{1,0:T(8,128)(2,1)S(1)}, bf16[768,384]{1,0:T(8,128)(2,1)S(1)}, u32[]{:S(2)}, u32[]{:S(2)}) %collective-permute-start.15) | collective-permute-done | bytes 589856 | tf_op jit(solution)/shard_map/ppermute | solution.py:173
  240.2 1.9 collective-permute-start.16
  242.4 4.8 %collective-permute-start.18 = (bf16[1536,384]{1,0:T(8,128)(2,1)S(1)}, bf16[1536,384]{1,0:T(8,128)(2,1)S(1)}, u32[]{:S(2)}, u32[]{:S(2)}) collective-permute-start(bf16[1536,384]{1,0:T(8,128)(2,1)S(1)} %pad_maximum_fusion.1), channel_id=1, source_target_pairs={{0,3},{1,0},{2,1},{3,2},{4,7},{5,4},{6,5},{7,6},{8,11},{9,8},{10,9... | collective-permute-start | bytes 3538952 | tf_op jit(solution)/shard_map/ppermute | solution.py:184
  247.2 0.9 fusion.6
  248.1 18.8 %collective-permute-done.16 = bf16[1536,384]{1,0:T(8,128)(2,1)S(1)} collective-permute-done((bf16[1536,384]{1,0:T(8,128)(2,1)S(1)}, bf16[1536,384]{1,0:T(8,128)(2,1)S(1)}, u32[]{:S(2)}, u32[]{:S(2)}) %collective-permute-start.16) | collective-permute-done | bytes 1179680 | tf_op jit(solution)/shard_map/ppermute | solution.py:183
  266.9 1.2 collective-permute-done.18
  268.5 1.3 reshape.215
  269.8 18.0 %all-to-all-start.1 = ((bf16[128,12,384]{2,1,0:T(8,128)(2,1)}), bf16[128,12,384]{2,1,0:T(8,128)(2,1)}, u32[]{:S(2)}, u32[]{:S(2)}) async-start(bf16[128,12,384]{2,1,0:T(8,128)(2,1)} %reshape.215), calls=%async_computation.1 | async-start | bytes 3145728 | tf_op jit(solution)/shard_map/all_to_all | solution.py:191
  288.4 40.3 %all-to-all-done.1 = bf16[128,12,384]{2,1,0:T(8,128)(2,1)} async-done(((bf16[128,12,384]{2,1,0:T(8,128)(2,1)}), bf16[128,12,384]{2,1,0:T(8,128)(2,1)}, u32[]{:S(2)}, u32[]{:S(2)}) %all-to-all-start.1) | async-done | bytes 1179680 | tf_op jit(solution)/shard_map/all_to_all | solution.py:191
  328.7 2.3 reshape.216
  330.9 1.9 gather_fusion
  333.8 0.8 fusion.44
  (78 shorter events, 6.6 us)
Async XLA Ops:
  0.0 223.2 %copy-start = (bf16[1,384,1536]{2,1,0:T(8,128)(2,1)S(1)}, bf16[1,384,1536]{2,1,0:T(8,128)(2,1)}, u32[]{:S(2)}) copy-start(bf16[1,384,1536]{2,1,0:T(8,128)(2,1)} %param.17) | copy-start | bytes 3538948
  0.0 9.7 %collective-permute-start.1 = (bf16[12,512]{1,0:T(8,128)(2,1)}, bf16[12,512]{1,0:T(8,128)(2,1)S(1)}, u32[]{:S(2)}, u32[]{:S(2)}) collective-permute-start(bf16[12,512]{1,0:T(8,128)(2,1)} %bitcast.138), channel_id=1, source_target_pairs={{0,256},{4,260},{8,264},{12,268},{16,272},{20,276},{24,280},{28,28... | collective-permute-start | bytes 36872 | tf_op jit(solution)/shard_map/ppermute | solution.py:30
  10.5 12.0 %collective-permute-start.2 = (bf16[2,12,512]{2,1,0:T(8,128)(2,1)S(1)}, bf16[2,12,512]{2,1,0:T(8,128)(2,1)S(1)}, u32[]{:S(2)}, u32[]{:S(2)}) collective-permute-start(bf16[2,12,512]{2,1,0:T(8,128)(2,1)S(1)} %pad_maximum_fusion.9), channel_id=1, source_target_pairs={{0,32},{4,36},{8,40},{12,44},{16,48},{20,52},{24,56},{28,60},{32,0... | collective-permute-start | bytes 73736 | tf_op jit(solution)/shard_map/ppermute | solution.py:30
  22.5 11.2 %collective-permute-start.3 = (bf16[2,2,12,512]{3,2,1,0:T(8,128)(2,1)S(1)}, bf16[2,2,12,512]{3,2,1,0:T(8,128)(2,1)S(1)}, u32[]{:S(2)}, u32[]{:S(2)}) collective-permute-start(bf16[2,2,12,512]{3,2,1,0:T(8,128)(2,1)S(1)} %pad_maximum_fusion.7), channel_id=1, source_target_pairs={{0,128},{4,132},{8,136},{12,140},{16,144},{20,148},{24,152},{28,15... | collective-permute-start | bytes 147464 | tf_op jit(solution)/shard_map/ppermute | solution.py:30
  27.5 29.3 %collective-permute-start = (bf16[128,1,128]{0,2,1:T(8,128)(2,1)S(1)}, bf16[128,1,128]{0,2,1:T(8,128)(2,1)S(1)}, u32[]{:S(2)}, u32[]{:S(2)}) collective-permute-start(bf16[128,1,128]{0,2,1:T(8,128)(2,1)S(1)} %copy.53), channel_id=1, source_target_pairs={{0,4},{4,8},{8,12},{12,16},{16,20},{20,24},{24,28},{28,32},{32,36}... | collective-permute-start | bytes 98312 | tf_op jit(solution)/shard_map/ppermute | solution.py:12
  33.8 10.7 %collective-permute-start.4 = (bf16[2,2,2,12,512]{4,3,2,1,0:T(8,128)(2,1)S(1)}, bf16[2,2,2,12,512]{4,3,2,1,0:T(8,128)(2,1)S(1)}, u32[]{:S(2)}, u32[]{:S(2)}) collective-permute-start(bf16[2,2,2,12,512]{4,3,2,1,0:T(8,128)(2,1)S(1)} %pad_maximum_fusion.6), channel_id=1, source_target_pairs={{0,16},{4,20},{8,24},{12,28},{16,0},{20,4},{24,8},{28,12},{32,48},... | collective-permute-start | bytes 294920 | tf_op jit(solution)/shard_map/ppermute | solution.py:30
  44.6 11.7 %copy-start.4 = (s32[128,4]{0,1:T(4,128)S(1)}, s32[128,4]{0,1:T(4,128)}, u32[]{:S(2)}) copy-start(s32[128,4]{0,1:T(4,128)} %param.18) | copy-start | bytes 6148
  44.6 11.9 %copy-start.3 = (bf16[128,512]{1,0:T(8,128)(2,1)S(1)}, bf16[128,512]{1,0:T(8,128)(2,1)}, u32[]{:S(2)}) copy-start(bf16[128,512]{1,0:T(8,128)(2,1)} %param.11) | copy-start | bytes 393220
  44.6 9.1 %collective-permute-start.5 = (bf16[2,2,2,2,12,512]{5,4,3,2,1,0:T(8,128)(2,1)S(1)}, bf16[2,2,2,2,12,512]{5,4,3,2,1,0:T(8,128)(2,1)S(1)}, u32[]{:S(2)}, u32[]{:S(2)}) collective-permute-start(bf16[2,2,2,2,12,512]{5,4,3,2,1,0:T(8,128)(2,1)S(1)} %pad_maximum_fusion.5), channel_id=1, source_target_pairs={{0,64},{4,68},{8,72},{12,76},{16,80},{20,84},{24,88},{28,92},{32,9... | collective-permute-start | bytes 589832 | tf_op jit(solution)/shard_map/ppermute | solution.py:30
  53.8 13.7 %collective-permute-start.6 = (bf16[2,2,2,2,2,12,512]{6,5,4,3,2,1,0:T(8,128)(2,1)S(1)}, bf16[2,2,2,2,2,12,512]{6,5,4,3,2,1,0:T(8,128)(2,1)S(1)}, u32[]{:S(2)}, u32[]{:S(2)}) collective-permute-start(bf16[2,2,2,2,2,12,512]{6,5,4,3,2,1,0:T(8,128)(2,1)S(1)} %pad_maximum_fusion.3), channel_id=1, source_target_pairs={{0,8},{4,12},{8,0},{12,4},{16,24},{20,28},{24,16},{28,20},{32,40},... | collective-permute-start | bytes 1179656 | tf_op jit(solution)/shard_map/ppermute | solution.py:30
  67.8 5.3 %copy-start.8 = (f32[8]{0:T(128)S(1)}, f32[8]{0:T(128)}, u32[]{:S(2)}) copy-start(f32[8]{0:T(128)} %param.13) | copy-start | bytes 100
  68.6 6.3 %collective-permute-start.7 = (bf16[2,2,2,2,2,2,12,512]{7,5,6,4,3,2,1,0:T(2,128)(2,1)S(1)}, bf16[2,2,2,2,2,2,12,512]{7,5,6,4,3,2,1,0:T(2,128)(2,1)S(1)}, u32[]{:S(2)}, u32[]{:S(2)}) collective-permute-start(bf16[2,2,2,2,2,2,12,512]{7,5,6,4,3,2,1,0:T(2,128)(2,1)S(1)} %copy.57), channel_id=1, source_target_pairs={{0,4},{4,0},{8,12},{12,8},{16,20},{20,16},{24,28},{28,24},{32,36},... | collective-permute-start | bytes 2359304 | tf_op jit(solution)/shard_map/ppermute | solution.py:30
  77.1 2.1 copy-start.1
  79.2 25.2 %collective-permute-start.10 = (bf16[128,1920]{1,0:T(8,128)(2,1)S(1)}, bf16[128,1920]{1,0:T(8,128)(2,1)S(1)}, u32[]{:S(2)}, u32[]{:S(2)}) collective-permute-start(bf16[128,1920]{1,0:T(8,128)(2,1)S(1)} %pad_maximum_fusion.4), channel_id=1, source_target_pairs={{0,3},{1,0},{2,1},{3,2},{4,7},{5,4},{6,5},{7,6},{8,11},{9,8},{10,9... | collective-permute-start | bytes 1474568 | tf_op jit(solution)/shard_map/ppermute | solution.py:108
  83.8 20.6 %collective-permute-start.8 = (bf16[128,1920]{1,0:T(8,128)(2,1)S(1)}, bf16[128,1920]{1,0:T(8,128)(2,1)S(1)}, u32[]{:S(2)}, u32[]{:S(2)}) collective-permute-start(bf16[128,1920]{1,0:T(8,128)(2,1)S(1)} %pad_maximum_fusion.4), channel_id=1, source_target_pairs={{0,1},{1,2},{2,3},{3,0},{4,5},{5,6},{6,7},{7,4},{8,9},{9,10},{10,1... | collective-permute-start | bytes 1474568 | tf_op jit(solution)/shard_map/ppermute | solution.py:108
  85.8 23.1 %collective-permute-start.9 = (bf16[128,1920]{1,0:T(8,128)(2,1)S(1)}, bf16[128,1920]{1,0:T(8,128)(2,1)}, u32[]{:S(2)}, u32[]{:S(2)}) collective-permute-start(bf16[128,1920]{1,0:T(8,128)(2,1)S(1)} %pad_maximum_fusion.4), channel_id=1, source_target_pairs={{0,2},{1,3},{2,0},{3,1},{4,6},{5,7},{6,4},{7,5},{8,10},{9,11},{10,... | collective-permute-start | bytes 1474568 | tf_op jit(solution)/shard_map/ppermute | solution.py:108
  110.0 1.1 copy-start.6
  115.5 55.1 %all-to-all-start = ((bf16[128,12,384]{2,1,0:T(8,128)(2,1)}), bf16[128,12,384]{2,1,0:T(8,128)(2,1)}, u32[]{:S(2)}, u32[]{:S(2)}) async-start(bf16[128,12,384]{2,1,0:T(8,128)(2,1)} %reshape.213), calls=%async_computation | async-start | bytes 3145728 | tf_op jit(solution)/shard_map/all_to_all | solution.py:139
  172.9 29.3 %collective-permute-start.11 = (bf16[1536,384]{1,0:T(8,128)(2,1)S(1)}, bf16[1536,384]{1,0:T(8,128)(2,1)S(1)}, u32[]{:S(2)}, u32[]{:S(2)}) collective-permute-start(bf16[1536,384]{1,0:T(8,128)(2,1)S(1)} %reshape.214), channel_id=1, source_target_pairs={{0,1},{1,2},{2,3},{3,0},{4,5},{5,6},{6,7},{7,4},{8,9},{9,10},{10,1... | collective-permute-start | bytes 3538952 | tf_op jit(solution)/shard_map/ppermute | solution.py:146
  174.8 29.3 %collective-permute-start.12 = (bf16[1536,384]{1,0:T(8,128)(2,1)S(1)}, bf16[1536,384]{1,0:T(8,128)(2,1)S(1)}, u32[]{:S(2)}, u32[]{:S(2)}) collective-permute-start(bf16[1536,384]{1,0:T(8,128)(2,1)S(1)} %reshape.214), channel_id=1, source_target_pairs={{0,3},{1,0},{2,1},{3,2},{4,7},{5,4},{6,5},{7,6},{8,11},{9,8},{10,9... | collective-permute-start | bytes 3538952 | tf_op jit(solution)/shard_map/ppermute | solution.py:147
  202.2 15.8 %collective-permute-start.13 = (bf16[768,384]{1,0:T(8,128)(2,1)S(1)}, bf16[768,384]{1,0:T(8,128)(2,1)S(1)}, u32[]{:S(2)}, u32[]{:S(2)}) collective-permute-start(bf16[768,384]{1,0:T(8,128)(2,1)S(1)} %slice.130), channel_id=1, source_target_pairs={{0,1},{1,2},{2,3},{3,0},{4,5},{5,6},{6,7},{7,4},{8,9},{9,10},{10,1... | collective-permute-start | bytes 1769480 | tf_op jit(solution)/shard_map/ppermute | solution.py:148
  204.2 14.7 %collective-permute-start.14 = (bf16[768,384]{1,0:T(8,128)(2,1)S(1)}, bf16[768,384]{1,0:T(8,128)(2,1)S(1)}, u32[]{:S(2)}, u32[]{:S(2)}) collective-permute-start(bf16[768,384]{1,0:T(8,128)(2,1)S(1)} %slice.131), channel_id=1, source_target_pairs={{0,3},{1,0},{2,1},{3,2},{4,7},{5,4},{6,5},{7,6},{8,11},{9,8},{10,9... | collective-permute-start | bytes 1769480 | tf_op jit(solution)/shard_map/ppermute | solution.py:149
  224.2 15.7 %collective-permute-start.15 = (bf16[768,384]{1,0:T(8,128)(2,1)S(1)}, bf16[768,384]{1,0:T(8,128)(2,1)S(1)}, u32[]{:S(2)}, u32[]{:S(2)}) collective-permute-start(bf16[768,384]{1,0:T(8,128)(2,1)S(1)} %get-tuple-element.13), channel_id=1, source_target_pairs={{0,1},{1,2},{2,3},{3,0},{4,5},{5,6},{6,7},{7,4},{8,9},{9,10},{10,1... | collective-permute-start | bytes 1769480 | tf_op jit(solution)/shard_map/ppermute | solution.py:173
  226.2 16.0 %collective-permute-start.17 = (bf16[768,384]{1,0:T(8,128)(2,1)S(1)}, bf16[768,384]{1,0:T(8,128)(2,1)S(1)}, u32[]{:S(2)}, u32[]{:S(2)}) collective-permute-start(bf16[768,384]{1,0:T(8,128)(2,1)S(1)} %get-tuple-element.14), channel_id=1, source_target_pairs={{0,3},{1,0},{2,1},{3,2},{4,7},{5,4},{6,5},{7,6},{8,11},{9,8},{10,9... | collective-permute-start | bytes 1769480 | tf_op jit(solution)/shard_map/ppermute | solution.py:174
  240.2 26.7 %collective-permute-start.16 = (bf16[1536,384]{1,0:T(8,128)(2,1)S(1)}, bf16[1536,384]{1,0:T(8,128)(2,1)S(1)}, u32[]{:S(2)}, u32[]{:S(2)}) collective-permute-start(bf16[1536,384]{1,0:T(8,128)(2,1)S(1)} %pad_maximum_fusion), channel_id=1, source_target_pairs={{0,1},{1,2},{2,3},{3,0},{4,5},{5,6},{6,7},{7,4},{8,9},{9,10},{10,1... | collective-permute-start | bytes 3538952 | tf_op jit(solution)/shard_map/ppermute | solution.py:183
  242.4 25.7 %collective-permute-start.18 = (bf16[1536,384]{1,0:T(8,128)(2,1)S(1)}, bf16[1536,384]{1,0:T(8,128)(2,1)S(1)}, u32[]{:S(2)}, u32[]{:S(2)}) collective-permute-start(bf16[1536,384]{1,0:T(8,128)(2,1)S(1)} %pad_maximum_fusion.1), channel_id=1, source_target_pairs={{0,3},{1,0},{2,1},{3,2},{4,7},{5,4},{6,5},{7,6},{8,11},{9,8},{10,9... | collective-permute-start | bytes 3538952 | tf_op jit(solution)/shard_map/ppermute | solution.py:184
  269.8 18.1 %copy-start.5 = (f32[128,4]{0,1:T(4,128)S(1)}, f32[128,4]{0,1:T(4,128)}, u32[]{:S(2)}) copy-start(f32[128,4]{0,1:T(4,128)} %param.19) | copy-start | bytes 6148
  269.8 58.9 %all-to-all-start.1 = ((bf16[128,12,384]{2,1,0:T(8,128)(2,1)}), bf16[128,12,384]{2,1,0:T(8,128)(2,1)}, u32[]{:S(2)}, u32[]{:S(2)}) async-start(bf16[128,12,384]{2,1,0:T(8,128)(2,1)} %reshape.215), calls=%async_computation.1 | async-start | bytes 3145728 | tf_op jit(solution)/shard_map/all_to_all | solution.py:191
  332.9 0.9 copy-start.2
  332.9 0.9 copy-start.7

commit v5 on v4

--- a/solution.py
+++ b/solution.py
@@ -1,40 +1,56 @@
 import jax
 import jax.numpy as jnp
 from jax import lax
-from jax.sharding import PartitionSpec as P
+from jax.sharding import Mesh, PartitionSpec as P
 
 WINDOW_KEYS = 128
 
 
-def shifted(value, axis, steps):
-    count = lax.axis_size(axis)
+CTX = ("yz", "core")
+
+
+def ctx_size():
+    return lax.axis_size("yz") * lax.axis_size("core")
+
+
+def shifted(value, steps):
+    count = ctx_size()
     first, last = (max(0, -steps), min(count, count - steps))
-    return lax.ppermute(value, axis, [(source, source + steps) for source in range(first, last)])
+    return lax.ppermute(value, CTX, [(source, source + steps) for source in range(first, last)])
+
+
+def by_core(mine, theirs):
+    first = lax.axis_index("core") == 0
+    return jnp.stack([jnp.where(first, mine, theirs), jnp.where(first, theirs, mine)], 1)
+
+
+def other_core(value):
+    return lax.ppermute(value, "core", [(0, 1), (1, 0)])
 
 
 def gathered_columns(block):
-    count = lax.axis_size("ctx")
-    bits = count.bit_length() - 1
-    me = lax.axis_index("ctx")
-    order = []
-    half = (bits - 1) // 2
-    y_bits, z_bits = list(range(bits - 1, half, -1)), list(range(half, 0, -1))
-    for pair in range(max(len(y_bits), len(z_bits))):
-        if pair < len(y_bits):
-            order.append(y_bits[pair])
-        if pair < len(z_bits):
-            order.append(z_bits[pair])
-    order.append(0)
-    held = block.T
-    for bit in order:
-        theirs = lax.ppermute(held, "ctx", [(i, i ^ (1 << bit)) for i in range(count)])
-        upper = ((me >> bit) & 1) == 1
-        lo = jnp.where(upper, theirs, held)
-        hi = jnp.where(upper, held, theirs)
-        held = jnp.stack([lo, hi], 0)
-    axis_of = {bit: place for place, bit in enumerate(reversed(order))}
-    perm = [axis_of[bit] for bit in range(bits - 1, -1, -1)] + [bits, bits + 1]
-    return held.transpose(perm).reshape(count * block.shape[1], block.shape[0])
+    rows = block.T
+    spread = jnp.broadcast_to(rows[None], (lax.axis_size("yz"),) + rows.shape)
+    mine = lax.all_to_all(spread, "yz", 0, 0, tiled=True)
+    return by_core(mine, other_core(mine)).reshape(-1, rows.shape[1])
+
+
+def to_experts(outbox):
+    parts = outbox.reshape((lax.axis_size("yz"), 2) + outbox.shape[1:])
+    first = lax.axis_index("core") == 0
+    mine = jnp.where(first, parts[:, 0], parts[:, 1])
+    theirs = jnp.where(first, parts[:, 1], parts[:, 0])
+    staged = by_core(mine, other_core(theirs))
+    return lax.all_to_all(staged, "yz", 0, 0, tiled=True).reshape(outbox.shape)
+
+
+def from_experts(result):
+    parts = result.reshape((lax.axis_size("yz"), 2) + result.shape[1:])
+    staged = lax.all_to_all(parts, "yz", 0, 0, tiled=True)
+    first = lax.axis_index("core") == 0
+    mine = jnp.where(first, staged[:, 0], staged[:, 1])
+    theirs = jnp.where(first, staged[:, 1], staged[:, 0])
+    return by_core(mine, other_core(theirs)).reshape(result.shape)
 
 
 def attend(query_block, key_blk, value_blk, inside, sink_row_block, factor):
@@ -70,9 +86,9 @@
     queries_per_group = q_heads // kv_heads
     factor = head_dim ** (-0.5)
     sink_row_block = sink_logit_table.reshape(kv_heads, queries_per_group)
-    earlier = shifted(rotated_key_value, "ctx", 1)
+    earlier = shifted(rotated_key_value, 1)
     keys_all = jnp.concatenate([earlier, rotated_key_value], 0)
-    first_pos = lax.axis_index("ctx") * tok_rows
+    first_pos = lax.axis_index(CTX) * tok_rows
     block_row_count = min(512, tok_rows)
     query_block = queries.reshape(block_row_count, kv_heads, queries_per_group, head_dim)
     query_pos = first_pos + 0 + jnp.arange(block_row_count, dtype=jnp.int32)[:, None]
@@ -103,10 +119,25 @@
     tp_index = lax.axis_index("tp")
     quarter_w = d_model // tp_count
     sent = jnp.concatenate([head_partial.astype(jnp.bfloat16), hidden_in], 1)
-    held = [(sent, tp_index)]
-    for step in range(1, tp_count):
-        got = lax.ppermute(sent, "tp", [(i, (i + step) % tp_count) for i in range(tp_count)])
-        held.append((got, (tp_index - step) % tp_count))
+    assert tp_count == 4
+    ahead = [(i, (i + 1) % tp_count) for i in range(tp_count)]
+    behind = [(i, (i - 1) % tp_count) for i in range(tp_count)]
+    from_behind = lax.ppermute(sent, "tp", ahead)
+    from_ahead = lax.ppermute(sent, "tp", behind)
+    half_tok = tok_rows // 2
+    opposite = jnp.concatenate(
+        [
+            lax.ppermute(from_behind[:half_tok], "tp", ahead),
+            lax.ppermute(from_ahead[half_tok:], "tp", behind),
+        ],
+        0,
+    )
+    held = [
+        (sent, tp_index),
+        (from_behind, (tp_index - 1) % tp_count),
+        (from_ahead, (tp_index + 1) % tp_count),
+        (opposite, (tp_index + 2) % tp_count),
+    ]
     head_sum = held[0][0][:, :d_model].astype(jnp.float32)
     for got, _ in held[1:]:
         head_sum = head_sum + got[:, :d_model].astype(jnp.float32)
@@ -122,7 +153,7 @@
     normed = (residual * lax.rsqrt(square_total[:, None] / d_model + 1e-05) * norm_gain).astype(
         jnp.bfloat16
     )
-    ctx_count = lax.axis_size("ctx")
+    ctx_count = ctx_size()
     top_count = routes.shape[1]
     experts = ctx_count * expert_in.shape[0]
     capacity = max(2, min(tok_rows, 3 * top_count * tok_rows // experts))
@@ -136,12 +167,7 @@
         -1, quarter_w
     )
     outbox = jnp.zeros((experts * capacity, quarter_w), jnp.bfloat16).at[flat_index].set(spread)
-    arrived = lax.all_to_all(
-        outbox.reshape(ctx_count, capacity, quarter_w), "ctx", 0, 0, tiled=True
-    ).reshape(-1, quarter_w)
-    assert tp_count == 4
-    ahead = [(i, (i + 1) % tp_count) for i in range(tp_count)]
-    behind = [(i, (i - 1) % tp_count) for i in range(tp_count)]
+    arrived = lax.all_to_all(outbox.reshape(ctx_count, capacity, quarter_w), CTX, 0, 0, tiled=True).reshape(-1, quarter_w)
     half_rows = arrived.shape[0] // 2
     from_behind = lax.ppermute(arrived, "tp", ahead)
     from_ahead = lax.ppermute(arrived, "tp", behind)
@@ -188,7 +214,7 @@
         + got_ahead.astype(jnp.float32)
     )
     result = summed.astype(jnp.bfloat16).reshape(ctx_count, capacity, quarter_w)
-    returned = lax.all_to_all(result, "ctx", 0, 0, tiled=True).reshape(-1, quarter_w)
+    returned = lax.all_to_all(result, CTX, 0, 0, tiled=True).reshape(-1, quarter_w)
     expert_result = returned[flat_index].reshape(tok_rows, top_count, quarter_w)
     moe_sum = jnp.zeros((tok_rows, quarter_w), jnp.float32)
     for member in range(top_count):
@@ -199,17 +225,19 @@
 
 
 def solution(mesh):
+    chips = mesh.devices.reshape(mesh.shape["ctx"] // 2, 2, mesh.shape["tp"])
+    split = Mesh(chips, ("yz", "core", "tp"))
     in_specs = (
-        P("ctx", "tp"),
-        P("ctx", "tp"),
-        P("ctx", "tp", None),
+        P(CTX, "tp"),
+        P(CTX, "tp"),
+        P(CTX, "tp", None),
         P("tp"),
-        P("tp", "ctx"),
+        P("tp", CTX),
         P("tp"),
-        P("ctx", None, None, "tp"),
-        P("ctx", "tp", None),
-        P("ctx", None),
-        P("ctx", None),
-    )
-    out_specs = P("ctx", "tp")
-    return jax.shard_map(body, mesh=mesh, in_specs=in_specs, out_specs=out_specs, check_vma=False)
+        P(CTX, None, None, "tp"),
+        P(CTX, "tp", None),
+        P(CTX, None),
+        P(CTX, None),
+    )
+    out_specs = P(CTX, "tp")
+    return jax.shard_map(body, mesh=split, in_specs=in_specs, out_specs=out_specs, check_vma=False)

time: 337 us -> 310 us (0.920)
  waiting for transfers between devices: 181 us -> 130 us
  blocking collectives: 0 us -> 50.5 us
  starting transfers between devices: 112 us -> 85.1 us
  local copies, waits for them, and re-layouts: 19.4 us -> 24 us
    all_to_all x0 -> x1, blocking collectives: none -> 50.5 us  [body(): lax.all_to_all(outbox.reshape(ctx_count, capacity, quarter_w), CTX, 0, 0,...]
    ppermute x11 -> x6, starting transfers between devices: 52.4 us -> 22.5 us  [the longest x1 5.52 us: other_core(): return lax.ppermute(value, 'core', [(0, 1), (1, 0)])]
    ppermute x11 -> x6, waiting for transfers between devices: 46.7 us -> 17.3 us  [the longest x1 8.43 us: body(): from_behind = lax.ppermute(sent, 'tp', ahead)]
    all_to_all x2, waiting for transfers between devices: 81.1 us -> 57.4 us  [the longest x1 40.3 us: body(): lax.all_to_all(result, CTX, 0, 0, tiled=True).reshape(-1, quarter_w)]
  transfers between devices with their start and end apart: 21 -> 16, of which waited for: 16 -> 12; matrix products, arithmetic and copies ran while one was open for 4% -> 4% of each run, Pallas kernels for 0% -> 0%
where the time goes in v5:
time: 310 us; the launch traced here: 308 us
  waiting for transfers between devices  130 us (42%)
  starting transfers between devices  85.1 us (27%)
  blocking collectives  50.5 us (16%)
  local copies, waits for them, and re-layouts  24 us (8%)
  matrix products  14 us (5%)
  other arithmetic  4.21 us (1%)
    all_to_all x1, blocking collectives, body(): lax.all_to_all(outbox.reshape(ctx_count, capacity, quarter_w), CTX, 0, 0,...  50.5 us
    all_to_all x1, waiting for transfers between devices, body(): lax.all_to_all(result, CTX, 0, 0, tiled=True).reshape(-1, quarter_w)  40.3 us
    ppermute x1, waiting for transfers between devices, body(): from_behind = lax.ppermute(arrived, 'tp', ahead)  19.2 us
    ppermute x1, waiting for transfers between devices, body(): got_behind = lax.ppermute(for_ahead, 'tp', ahead)  19.1 us
    all_to_all x1, starting transfers between devices, body(): lax.all_to_all(result, CTX, 0, 0, tiled=True).reshape(-1, quarter_w)  17.4 us
    all_to_all x1, starting transfers between devices, gathered_columns(): mine = lax.all_to_all(spread, 'yz', 0, 0, tiled=True)  17.3 us
    all_to_all x1, waiting for transfers between devices, gathered_columns(): mine = lax.all_to_all(spread, 'yz', 0, 0, tiled=True)  17.2 us
    ppermute x1, waiting for transfers between devices, body(): from_behind = lax.ppermute(sent, 'tp', ahead)  8.43 us
  transfers between devices with their start and end apart: 16, of which 12 were waited for; matrix products, arithmetic and copies ran while one was open for 4% of the time, Pallas kernels for 0%

profile of v5, /device:TPU:1, one launch (start us, length us, event | category | flops | bytes accessed | tf_op | source)
XLA Modules:
  0.0 308.0 jit_solution(9870556929960752131)
XLA Ops:
  0.0 1.9 broadcast_in_dim.21
  1.9 17.3 %all-to-all-start = ((bf16[64,12,512]{2,1,0:T(8,128)(2,1)}), bf16[64,12,512]{2,1,0:T(8,128)(2,1)S(1)}, u32[]{:S(2)}, u32[]{:S(2)}) async-start(bf16[64,12,512]{2,1,0:T(8,128)(2,1)} %broadcast_in_dim.21), calls=%async_computation | async-start | bytes 2097152 | tf_op jit(solution)/shard_map/all_to_all | solution.py:34
  19.3 4.0 %collective-permute-start = (bf16[128,1,128]{0,2,1:T(8,128)(2,1)S(1)}, bf16[128,1,128]{0,2,1:T(8,128)(2,1)S(1)}, u32[]{:S(2)}, u32[]{:S(2)}) collective-permute-start(bf16[128,1,128]{0,2,1:T(8,128)(2,1)S(1)} %copy.52), channel_id=1, source_target_pairs={{0,4},{4,8},{8,12},{12,16},{16,20},{20,24},{24,28},{28,32},{32,36}... | collective-permute-start | bytes 98312 | tf_op jit(solution)/shard_map/ppermute | solution.py:19
  23.7 4.8 %collective-permute-done = bf16[128,1,128]{0,2,1:T(8,128)(2,1)S(1)} collective-permute-done((bf16[128,1,128]{0,2,1:T(8,128)(2,1)S(1)}, bf16[128,1,128]{0,2,1:T(8,128)(2,1)S(1)}, u32[]{:S(2)}, u32[]{:S(2)}) %collective-permute-start) | collective-permute-done | bytes 32800 | tf_op jit(solution)/shard_map/ppermute | solution.py:19
  28.5 0.3 select_reduce_fusion
  28.9 17.2 %all-to-all-done = bf16[64,12,512]{2,1,0:T(8,128)(2,1)S(1)} async-done(((bf16[64,12,512]{2,1,0:T(8,128)(2,1)}), bf16[64,12,512]{2,1,0:T(8,128)(2,1)S(1)}, u32[]{:S(2)}, u32[]{:S(2)}) %all-to-all-start) | async-done | bytes 786464 | tf_op jit(solution)/shard_map/all_to_all | solution.py:34
  46.0 0.4 copy.56
  46.4 5.5 %collective-permute-start.1 = (bf16[64,12,512]{2,0,1:T(8,128)(2,1)S(1)}, bf16[64,12,512]{2,0,1:T(8,128)(2,1)S(1)}, u32[]{:S(2)}, u32[]{:S(2)}) collective-permute-start(bf16[64,12,512]{2,0,1:T(8,128)(2,1)S(1)} %copy.56), channel_id=1, source_target_pairs={{0,4},{4,0},{1,5},{5,1},{2,6},{6,2},{3,7},{7,3},{8,12},{12,8},{9,1... | collective-permute-start | bytes 2359304 | tf_op jit(solution)/shard_map/ppermute | solution.py:28
  52.3 0.4 convolution_convert_fusion.5
  52.7 1.2 collective-permute-done.1
  53.9 0.5 fusion.8
  54.4 0.3 pad_maximum_fusion
  54.9 1.4 reshape.211
  56.2 2.1 convolution_convert_fusion.4
  58.4 3.1 %collective-permute-start.2 = (bf16[128,1920]{1,0:T(8,128)(2,1)S(1)}, bf16[128,1920]{1,0:T(8,128)(2,1)S(1)}, u32[]{:S(2)}, u32[]{:S(2)}) collective-permute-start(bf16[128,1920]{1,0:T(8,128)(2,1)S(1)} %pad_maximum_fusion.3), channel_id=1, source_target_pairs={{0,1},{1,2},{2,3},{3,0},{4,5},{5,6},{6,7},{7,4},{8,9},{9,10},{10,1... | collective-permute-start | bytes 1474568 | tf_op jit(solution)/shard_map/ppermute | solution.py:125
  61.5 3.4 %collective-permute-start.3 = (bf16[128,1920]{1,0:T(8,128)(2,1)S(1)}, bf16[128,1920]{1,0:T(8,128)(2,1)S(1)}, u32[]{:S(2)}, u32[]{:S(2)}) collective-permute-start(bf16[128,1920]{1,0:T(8,128)(2,1)S(1)} %pad_maximum_fusion.3), channel_id=1, source_target_pairs={{0,3},{1,0},{2,1},{3,2},{4,7},{5,4},{6,5},{7,6},{8,11},{9,8},{10,9... | collective-permute-start | bytes 1474568 | tf_op jit(solution)/shard_map/ppermute | solution.py:126
  65.2 0.2 select_reduce_fusion.1
  65.5 8.4 %collective-permute-done.2 = bf16[128,1920]{1,0:T(8,128)(2,1)S(1)} collective-permute-done((bf16[128,1920]{1,0:T(8,128)(2,1)S(1)}, bf16[128,1920]{1,0:T(8,128)(2,1)S(1)}, u32[]{:S(2)}, u32[]{:S(2)}) %collective-permute-start.2) | collective-permute-done | bytes 491552 | tf_op jit(solution)/shard_map/ppermute | solution.py:125
  73.9 0.7 slice.134
  74.6 1.9 collective-permute-start.4
  76.8 4.6 %collective-permute-start.5 = (bf16[64,1920]{1,0:T(8,128)(2,1)S(1)}, bf16[64,1920]{1,0:T(8,128)(2,1)S(1)}, u32[]{:S(2)}, u32[]{:S(2)}) collective-permute-start(bf16[64,1920]{1,0:T(8,128)(2,1)S(1)} %slice.135), channel_id=1, source_target_pairs={{0,3},{1,0},{2,1},{3,2},{4,7},{5,4},{6,5},{7,6},{8,11},{9,8},{10,9... | collective-permute-start | bytes 737288 | tf_op jit(solution)/shard_map/ppermute | solution.py:131
  81.5 2.9 collective-permute-done.4
  84.3 1.0 constant_dynamic-update-slice_fusion.1
  85.7 0.5 copy-done.7
  86.5 3.5 %scatter_custom_fusion = bf16[1536,384]{1,0:T(8,128)(2,1)} fusion(s32[512]{0:T(512)S(1)} %bitcast.111, bf16[512,384]{1,0:T(8,128)(2,1)S(1)} %reshape.235, bf16[]{:T(256)} %constant.94.clone.1), kind=kCustom, calls=%fused_computation.36 | custom fusion | bytes 1179650 | tf_op jit(solution)/shard_map/scatter | solution.py:169
  90.0 2.2 reshape.214
  92.2 50.5 %all_to_all.15 = bf16[128,12,384]{2,1,0:T(8,128)(2,1)} all-to-all(bf16[128,12,384]{2,1,0:T(8,128)(2,1)S(1)} %reshape.214), channel_id=1, replica_groups=mesh['yz'=64,'core'=2,'tp'=4] {'yz','core'}, dimensions={0} | all-to-all | bytes 2359296 | tf_op jit(solution)/shard_map/all_to_all | solution.py:170
  142.8 2.3 reshape.215
  145.0 2.6 collective-permute-start.6
  147.7 4.8 %collective-permute-start.7 = (bf16[1536,384]{1,0:T(8,128)(2,1)S(1)}, bf16[1536,384]{1,0:T(8,128)(2,1)S(1)}, u32[]{:S(2)}, u32[]{:S(2)}) collective-permute-start(bf16[1536,384]{1,0:T(8,128)(2,1)S(1)} %reshape.215), channel_id=1, source_target_pairs={{0,3},{1,0},{2,1},{3,2},{4,7},{5,4},{6,5},{7,6},{8,11},{9,8},{10,9... | collective-permute-start | bytes 3538952 | tf_op jit(solution)/shard_map/ppermute | solution.py:173
  152.5 1.9 fusion.68
  154.3 0.9 fusion.28
  155.2 0.9 fusion.22
  156.1 19.2 %collective-permute-done.6 = bf16[1536,384]{1,0:T(8,128)(2,1)S(1)} collective-permute-done((bf16[1536,384]{1,0:T(8,128)(2,1)S(1)}, bf16[1536,384]{1,0:T(8,128)(2,1)S(1)}, u32[]{:S(2)}, u32[]{:S(2)}) %collective-permute-start.6) | collective-permute-done | bytes 1179680 | tf_op jit(solution)/shard_map/ppermute | solution.py:172
  175.4 1.9 collective-permute-start.8
  177.4 4.6 %collective-permute-start.9 = (bf16[768,384]{1,0:T(8,128)(2,1)S(1)}, bf16[768,384]{1,0:T(8,128)(2,1)S(1)}, u32[]{:S(2)}, u32[]{:S(2)}) collective-permute-start(bf16[768,384]{1,0:T(8,128)(2,1)S(1)} %slice.141), channel_id=1, source_target_pairs={{0,3},{1,0},{2,1},{3,2},{4,7},{5,4},{6,5},{7,6},{8,11},{9,8},{10,9... | collective-permute-start | bytes 1769480 | tf_op jit(solution)/shard_map/ppermute | solution.py:175
  182.0 0.9 convolution_add_fusion.3
  182.9 0.9 convolution_add_fusion.1
  183.8 7.6 %collective-permute-done.8 = bf16[768,384]{1,0:T(8,128)(2,1)S(1)} collective-permute-done((bf16[768,384]{1,0:T(8,128)(2,1)S(1)}, bf16[768,384]{1,0:T(8,128)(2,1)S(1)}, u32[]{:S(2)}, u32[]{:S(2)}) %collective-permute-start.8) | collective-permute-done | bytes 589856 | tf_op jit(solution)/shard_map/ppermute | solution.py:174
  191.5 0.9 collective-permute-done.9
  192.5 0.9 fusion.18
  193.4 0.9 fusion.24
  194.3 1.0 fusion
  195.3 1.4 fusion.5
  196.7 0.9 convolution_convert_fusion.1
  197.7 2.0 collective-permute-start.10
  199.7 5.2 %collective-permute-start.12 = (bf16[768,384]{1,0:T(8,128)(2,1)S(1)}, bf16[768,384]{1,0:T(8,128)(2,1)S(1)}, u32[]{:S(2)}, u32[]{:S(2)}) collective-permute-start(bf16[768,384]{1,0:T(8,128)(2,1)S(1)} %get-tuple-element.14), channel_id=1, source_target_pairs={{0,3},{1,0},{2,1},{3,2},{4,7},{5,4},{6,5},{7,6},{8,11},{9,8},{10,9... | collective-permute-start | bytes 1769480 | tf_op jit(solution)/shard_map/ppermute | solution.py:200
  204.9 0.9 convolution_convert_fusion.2
  205.8 0.9 convolution_convert_fusion
  206.8 6.8 %collective-permute-done.10 = bf16[768,384]{1,0:T(8,128)(2,1)S(1)} collective-permute-done((bf16[768,384]{1,0:T(8,128)(2,1)S(1)}, bf16[768,384]{1,0:T(8,128)(2,1)S(1)}, u32[]{:S(2)}, u32[]{:S(2)}) %collective-permute-start.10) | collective-permute-done | bytes 589856 | tf_op jit(solution)/shard_map/ppermute | solution.py:199
  213.9 1.9 collective-permute-start.11
  216.2 4.8 %collective-permute-start.13 = (bf16[1536,384]{1,0:T(8,128)(2,1)S(1)}, bf16[1536,384]{1,0:T(8,128)(2,1)S(1)}, u32[]{:S(2)}, u32[]{:S(2)}) collective-permute-start(bf16[1536,384]{1,0:T(8,128)(2,1)S(1)} %pad_maximum_fusion.2), channel_id=1, source_target_pairs={{0,3},{1,0},{2,1},{3,2},{4,7},{5,4},{6,5},{7,6},{8,11},{9,8},{10,9... | collective-permute-start | bytes 3538952 | tf_op jit(solution)/shard_map/ppermute | solution.py:210
  221.0 0.9 fusion.6
  221.8 19.1 %collective-permute-done.11 = bf16[1536,384]{1,0:T(8,128)(2,1)S(1)} collective-permute-done((bf16[1536,384]{1,0:T(8,128)(2,1)S(1)}, bf16[1536,384]{1,0:T(8,128)(2,1)S(1)}, u32[]{:S(2)}, u32[]{:S(2)}) %collective-permute-start.11) | collective-permute-done | bytes 1179680 | tf_op jit(solution)/shard_map/ppermute | solution.py:209
  240.9 1.2 collective-permute-done.13
  242.1 0.4 add_convert_fusion
  242.5 1.3 reshape.216
  243.8 17.4 %all-to-all-start.2 = ((bf16[128,12,384]{2,1,0:T(8,128)(2,1)}), bf16[128,12,384]{2,1,0:T(8,128)(2,1)}, u32[]{:S(2)}, u32[]{:S(2)}) async-start(bf16[128,12,384]{2,1,0:T(8,128)(2,1)} %reshape.216), calls=%async_computation.2 | async-start | bytes 3145728 | tf_op jit(solution)/shard_map/all_to_all | solution.py:217
  261.3 0.5 slice_bitcast_fusion.3
  261.8 40.3 %all-to-all-done.2 = bf16[128,12,384]{2,1,0:T(8,128)(2,1)} async-done(((bf16[128,12,384]{2,1,0:T(8,128)(2,1)}), bf16[128,12,384]{2,1,0:T(8,128)(2,1)}, u32[]{:S(2)}, u32[]{:S(2)}) %all-to-all-start.2) | async-done | bytes 1179680 | tf_op jit(solution)/shard_map/all_to_all | solution.py:217
  302.1 2.3 reshape.217
  304.4 1.9 gather_fusion
  306.4 0.6 fusion.70
  307.2 0.8 fusion.44
  (64 shorter events, 3.7 us)
Async XLA Ops:
  0.0 196.7 %copy-start = (bf16[1,384,1536]{2,1,0:T(8,128)(2,1)S(1)}, bf16[1,384,1536]{2,1,0:T(8,128)(2,1)}, u32[]{:S(2)}) copy-start(bf16[1,384,1536]{2,1,0:T(8,128)(2,1)} %param.17) | copy-start | bytes 3538948
  1.9 17.3 %copy-start.4 = (bf16[128,1,128]{2,0,1:T(8,128)(2,1)S(1)}, bf16[128,1,128]{2,0,1:T(8,128)(2,1)}, u32[]{:S(2)}) copy-start(bf16[128,1,128]{2,0,1:T(8,128)(2,1)} %param.12) | copy-start | bytes 98308
  1.9 21.6 %copy-start.3 = (bf16[128,512]{1,0:T(8,128)(2,1)S(1)}, bf16[128,512]{1,0:T(8,128)(2,1)}, u32[]{:S(2)}) copy-start(bf16[128,512]{1,0:T(8,128)(2,1)} %param.11) | copy-start | bytes 393220
  1.9 44.1 %all-to-all-start = ((bf16[64,12,512]{2,1,0:T(8,128)(2,1)}), bf16[64,12,512]{2,1,0:T(8,128)(2,1)S(1)}, u32[]{:S(2)}, u32[]{:S(2)}) async-start(bf16[64,12,512]{2,1,0:T(8,128)(2,1)} %broadcast_in_dim.21), calls=%async_computation | async-start | bytes 2097152 | tf_op jit(solution)/shard_map/all_to_all | solution.py:34
  19.3 9.2 %collective-permute-start = (bf16[128,1,128]{0,2,1:T(8,128)(2,1)S(1)}, bf16[128,1,128]{0,2,1:T(8,128)(2,1)S(1)}, u32[]{:S(2)}, u32[]{:S(2)}) collective-permute-start(bf16[128,1,128]{0,2,1:T(8,128)(2,1)S(1)} %copy.52), channel_id=1, source_target_pairs={{0,4},{4,8},{8,12},{12,16},{16,20},{20,24},{24,28},{28,32},{32,36}... | collective-permute-start | bytes 98312 | tf_op jit(solution)/shard_map/ppermute | solution.py:19
  28.8 23.1 %copy-start.9 = (f32[8]{0:T(128)S(1)}, f32[8]{0:T(128)}, u32[]{:S(2)}) copy-start(f32[8]{0:T(128)} %param.13) | copy-start | bytes 100
  46.4 7.4 %collective-permute-start.1 = (bf16[64,12,512]{2,0,1:T(8,128)(2,1)S(1)}, bf16[64,12,512]{2,0,1:T(8,128)(2,1)S(1)}, u32[]{:S(2)}, u32[]{:S(2)}) collective-permute-start(bf16[64,12,512]{2,0,1:T(8,128)(2,1)S(1)} %copy.56), channel_id=1, source_target_pairs={{0,4},{4,0},{1,5},{5,1},{2,6},{6,2},{3,7},{7,3},{8,12},{12,8},{9,1... | collective-permute-start | bytes 2359304 | tf_op jit(solution)/shard_map/ppermute | solution.py:28
  56.2 2.1 copy-start.1
  56.2 8.7 %copy-start.5 = (s32[128,4]{0,1:T(4,128)S(1)}, s32[128,4]{0,1:T(4,128)}, u32[]{:S(2)}) copy-start(s32[128,4]{0,1:T(4,128)} %param.18) | copy-start | bytes 6148
  58.4 15.5 %collective-permute-start.2 = (bf16[128,1920]{1,0:T(8,128)(2,1)S(1)}, bf16[128,1920]{1,0:T(8,128)(2,1)S(1)}, u32[]{:S(2)}, u32[]{:S(2)}) collective-permute-start(bf16[128,1920]{1,0:T(8,128)(2,1)S(1)} %pad_maximum_fusion.3), channel_id=1, source_target_pairs={{0,1},{1,2},{2,3},{3,0},{4,5},{5,6},{6,7},{7,4},{8,9},{9,10},{10,1... | collective-permute-start | bytes 1474568 | tf_op jit(solution)/shard_map/ppermute | solution.py:125
  61.5 15.3 %collective-permute-start.3 = (bf16[128,1920]{1,0:T(8,128)(2,1)S(1)}, bf16[128,1920]{1,0:T(8,128)(2,1)S(1)}, u32[]{:S(2)}, u32[]{:S(2)}) collective-permute-start(bf16[128,1920]{1,0:T(8,128)(2,1)S(1)} %pad_maximum_fusion.3), channel_id=1, source_target_pairs={{0,3},{1,0},{2,1},{3,2},{4,7},{5,4},{6,5},{7,6},{8,11},{9,8},{10,9... | collective-permute-start | bytes 1474568 | tf_op jit(solution)/shard_map/ppermute | solution.py:126
  74.6 9.7 %collective-permute-start.4 = (bf16[64,1920]{1,0:T(8,128)(2,1)}, bf16[64,1920]{1,0:T(8,128)(2,1)}, u32[]{:S(2)}, u32[]{:S(2)}) collective-permute-start(bf16[64,1920]{1,0:T(8,128)(2,1)} %slice.134), channel_id=1, source_target_pairs={{0,1},{1,2},{2,3},{3,0},{4,5},{5,6},{6,7},{7,4},{8,9},{9,10},{10,1... | collective-permute-start | bytes 737288 | tf_op jit(solution)/shard_map/ppermute | solution.py:130
  76.8 8.5 %collective-permute-start.5 = (bf16[64,1920]{1,0:T(8,128)(2,1)S(1)}, bf16[64,1920]{1,0:T(8,128)(2,1)S(1)}, u32[]{:S(2)}, u32[]{:S(2)}) collective-permute-start(bf16[64,1920]{1,0:T(8,128)(2,1)S(1)} %slice.135), channel_id=1, source_target_pairs={{0,3},{1,0},{2,1},{3,2},{4,7},{5,4},{6,5},{7,6},{8,11},{9,8},{10,9... | collective-permute-start | bytes 737288 | tf_op jit(solution)/shard_map/ppermute | solution.py:131
  85.5 0.7 copy-start.7
  145.0 30.3 %collective-permute-start.6 = (bf16[1536,384]{1,0:T(8,128)(2,1)S(1)}, bf16[1536,384]{1,0:T(8,128)(2,1)S(1)}, u32[]{:S(2)}, u32[]{:S(2)}) collective-permute-start(bf16[1536,384]{1,0:T(8,128)(2,1)S(1)} %reshape.215), channel_id=1, source_target_pairs={{0,1},{1,2},{2,3},{3,0},{4,5},{5,6},{6,7},{7,4},{8,9},{9,10},{10,1... | collective-permute-start | bytes 3538952 | tf_op jit(solution)/shard_map/ppermute | solution.py:172
  147.7 29.7 %collective-permute-start.7 = (bf16[1536,384]{1,0:T(8,128)(2,1)S(1)}, bf16[1536,384]{1,0:T(8,128)(2,1)S(1)}, u32[]{:S(2)}, u32[]{:S(2)}) collective-permute-start(bf16[1536,384]{1,0:T(8,128)(2,1)S(1)} %reshape.215), channel_id=1, source_target_pairs={{0,3},{1,0},{2,1},{3,2},{4,7},{5,4},{6,5},{7,6},{8,11},{9,8},{10,9... | collective-permute-start | bytes 3538952 | tf_op jit(solution)/shard_map/ppermute | solution.py:173
  175.4 16.1 %collective-permute-start.8 = (bf16[768,384]{1,0:T(8,128)(2,1)S(1)}, bf16[768,384]{1,0:T(8,128)(2,1)S(1)}, u32[]{:S(2)}, u32[]{:S(2)}) collective-permute-start(bf16[768,384]{1,0:T(8,128)(2,1)S(1)} %slice.140), channel_id=1, source_target_pairs={{0,1},{1,2},{2,3},{3,0},{4,5},{5,6},{6,7},{7,4},{8,9},{9,10},{10,1... | collective-permute-start | bytes 1769480 | tf_op jit(solution)/shard_map/ppermute | solution.py:174
  177.4 15.0 %collective-permute-start.9 = (bf16[768,384]{1,0:T(8,128)(2,1)S(1)}, bf16[768,384]{1,0:T(8,128)(2,1)S(1)}, u32[]{:S(2)}, u32[]{:S(2)}) collective-permute-start(bf16[768,384]{1,0:T(8,128)(2,1)S(1)} %slice.141), channel_id=1, source_target_pairs={{0,3},{1,0},{2,1},{3,2},{4,7},{5,4},{6,5},{7,6},{8,11},{9,8},{10,9... | collective-permute-start | bytes 1769480 | tf_op jit(solution)/shard_map/ppermute | solution.py:175
  197.7 15.9 %collective-permute-start.10 = (bf16[768,384]{1,0:T(8,128)(2,1)S(1)}, bf16[768,384]{1,0:T(8,128)(2,1)S(1)}, u32[]{:S(2)}, u32[]{:S(2)}) collective-permute-start(bf16[768,384]{1,0:T(8,128)(2,1)S(1)} %get-tuple-element.13), channel_id=1, source_target_pairs={{0,1},{1,2},{2,3},{3,0},{4,5},{5,6},{6,7},{7,4},{8,9},{9,10},{10,1... | collective-permute-start | bytes 1769480 | tf_op jit(solution)/shard_map/ppermute | solution.py:199
  199.7 16.1 %collective-permute-start.12 = (bf16[768,384]{1,0:T(8,128)(2,1)S(1)}, bf16[768,384]{1,0:T(8,128)(2,1)S(1)}, u32[]{:S(2)}, u32[]{:S(2)}) collective-permute-start(bf16[768,384]{1,0:T(8,128)(2,1)S(1)} %get-tuple-element.14), channel_id=1, source_target_pairs={{0,3},{1,0},{2,1},{3,2},{4,7},{5,4},{6,5},{7,6},{8,11},{9,8},{10,9... | collective-permute-start | bytes 1769480 | tf_op jit(solution)/shard_map/ppermute | solution.py:200
  213.9 27.0 %collective-permute-start.11 = (bf16[1536,384]{1,0:T(8,128)(2,1)S(1)}, bf16[1536,384]{1,0:T(8,128)(2,1)S(1)}, u32[]{:S(2)}, u32[]{:S(2)}) collective-permute-start(bf16[1536,384]{1,0:T(8,128)(2,1)S(1)} %pad_maximum_fusion.1), channel_id=1, source_target_pairs={{0,1},{1,2},{2,3},{3,0},{4,5},{5,6},{6,7},{7,4},{8,9},{9,10},{10,1... | collective-permute-start | bytes 3538952 | tf_op jit(solution)/shard_map/ppermute | solution.py:209
  216.2 26.0 %collective-permute-start.13 = (bf16[1536,384]{1,0:T(8,128)(2,1)S(1)}, bf16[1536,384]{1,0:T(8,128)(2,1)S(1)}, u32[]{:S(2)}, u32[]{:S(2)}) collective-permute-start(bf16[1536,384]{1,0:T(8,128)(2,1)S(1)} %pad_maximum_fusion.2), channel_id=1, source_target_pairs={{0,3},{1,0},{2,1},{3,2},{4,7},{5,4},{6,5},{7,6},{8,11},{9,8},{10,9... | collective-permute-start | bytes 3538952 | tf_op jit(solution)/shard_map/ppermute | solution.py:210
  243.8 17.4 %copy-start.6 = (f32[128,4]{0,1:T(4,128)S(1)}, f32[128,4]{0,1:T(4,128)}, u32[]{:S(2)}) copy-start(f32[128,4]{0,1:T(4,128)} %param.19) | copy-start | bytes 6148
  243.8 58.3 %all-to-all-start.2 = ((bf16[128,12,384]{2,1,0:T(8,128)(2,1)}), bf16[128,12,384]{2,1,0:T(8,128)(2,1)}, u32[]{:S(2)}, u32[]{:S(2)}) async-start(bf16[128,12,384]{2,1,0:T(8,128)(2,1)} %reshape.216), calls=%async_computation.2 | async-start | bytes 3145728 | tf_op jit(solution)/shard_map/all_to_all | solution.py:217
  306.3 0.9 copy-start.2
  306.3 0.9 copy-start.8

commit v6 on v5

--- a/solution.py
+++ b/solution.py
@@ -167,7 +167,7 @@
         -1, quarter_w
     )
     outbox = jnp.zeros((experts * capacity, quarter_w), jnp.bfloat16).at[flat_index].set(spread)
-    arrived = lax.all_to_all(outbox.reshape(ctx_count, capacity, quarter_w), CTX, 0, 0, tiled=True).reshape(-1, quarter_w)
+    arrived = to_experts(outbox.reshape(ctx_count, capacity, quarter_w)).reshape(-1, quarter_w)
     half_rows = arrived.shape[0] // 2
     from_behind = lax.ppermute(arrived, "tp", ahead)
     from_ahead = lax.ppermute(arrived, "tp", behind)

time: 310 us -> 305 us (0.984)
  blocking collectives: 50.5 us -> 36.1 us
  starting transfers between devices: 85.1 us -> 96.6 us
  waiting for transfers between devices: 130 us -> 124 us
    all_to_all x1, blocking collectives: 50.5 us -> 36.1 us  [to_experts(): return lax.all_to_all(staged, 'yz', 0, 0, tiled=True).reshape(outbox.shape)]
    all_to_all x1, starting transfers between devices: 17.4 us -> 24.9 us  [body(): lax.all_to_all(result, CTX, 0, 0, tiled=True).reshape(-1, quarter_w)]
    reshape x2 -> x0, local copies, waits for them, and re-layouts: 4.42 us -> none  [the longest x1 2.26 us: body(): lax.all_to_all(outbox.reshape(ctx_count, capacity, quarter_w), CTX, 0, 0,...]
    another operation x0 -> x2, local copies, waits for them, and re-layouts: none -> 4.42 us  [the longest x1 2.26 us: body(): to_experts(outbox.reshape(ctx_count, capacity, quarter_w))]
    ppermute x1 -> x2, starting transfers between devices: 5.52 us -> 9.67 us  [other_core(): return lax.ppermute(value, 'core', [(0, 1), (1, 0)])]
  transfers between devices with their start and end apart: 16 -> 17, of which waited for: 12 -> 13; matrix products, arithmetic and copies ran while one was open for 4% -> 4% of each run, Pallas kernels for 0% -> 0%
where the time goes in v6:
time: 305 us; the launch traced here: 303 us
  waiting for transfers between devices  124 us (41%)
  starting transfers between devices  96.6 us (32%)
  blocking collectives  36.1 us (12%)
  local copies, waits for them, and re-layouts  26.8 us (9%)
  matrix products  14 us (5%)
  other arithmetic  5.12 us (2%)
    all_to_all x1, waiting for transfers between devices, body(): lax.all_to_all(result, CTX, 0, 0, tiled=True).reshape(-1, quarter_w)  40.3 us
    all_to_all x1, blocking collectives, to_experts(): return lax.all_to_all(staged, 'yz', 0, 0, tiled=True).reshape(outbox.shape)  36.1 us
    all_to_all x1, starting transfers between devices, body(): lax.all_to_all(result, CTX, 0, 0, tiled=True).reshape(-1, quarter_w)  24.9 us
    ppermute x1, waiting for transfers between devices, body(): from_behind = lax.ppermute(arrived, 'tp', ahead)  17.6 us
    ppermute x1, waiting for transfers between devices, body(): got_behind = lax.ppermute(for_ahead, 'tp', ahead)  17.4 us
    all_to_all x1, starting transfers between devices, gathered_columns(): mine = lax.all_to_all(spread, 'yz', 0, 0, tiled=True)  17.3 us
    all_to_all x1, waiting for transfers between devices, gathered_columns(): mine = lax.all_to_all(spread, 'yz', 0, 0, tiled=True)  17.2 us
    ppermute x2, starting transfers between devices, other_core(): return lax.ppermute(value, 'core', [(0, 1), (1, 0)])  9.67 us
  transfers between devices with their start and end apart: 17, of which 13 were waited for; matrix products, arithmetic and copies ran while one was open for 4% of the time, Pallas kernels for 0%

profile of v6, /device:TPU:1, one launch (start us, length us, event | category | flops | bytes accessed | tf_op | source)
XLA Modules:
  0.0 303.2 jit_solution(13981626767558248242)
XLA Ops:
  0.0 1.9 broadcast_in_dim.21
  1.9 17.3 %all-to-all-start = ((bf16[64,12,512]{2,1,0:T(8,128)(2,1)}), bf16[64,12,512]{2,1,0:T(8,128)(2,1)S(1)}, u32[]{:S(2)}, u32[]{:S(2)}) async-start(bf16[64,12,512]{2,1,0:T(8,128)(2,1)} %broadcast_in_dim.21), calls=%async_computation | async-start | bytes 2097152 | tf_op jit(solution)/shard_map/all_to_all | solution.py:34
  19.3 4.0 %collective-permute-start = (bf16[128,1,128]{0,2,1:T(8,128)(2,1)S(1)}, bf16[128,1,128]{0,2,1:T(8,128)(2,1)S(1)}, u32[]{:S(2)}, u32[]{:S(2)}) collective-permute-start(bf16[128,1,128]{0,2,1:T(8,128)(2,1)S(1)} %copy.67), channel_id=1, source_target_pairs={{0,4},{4,8},{8,12},{12,16},{16,20},{20,24},{24,28},{28,32},{32,36}... | collective-permute-start | bytes 98312 | tf_op jit(solution)/shard_map/ppermute | solution.py:19
  23.7 4.8 %collective-permute-done = bf16[128,1,128]{0,2,1:T(8,128)(2,1)S(1)} collective-permute-done((bf16[128,1,128]{0,2,1:T(8,128)(2,1)S(1)}, bf16[128,1,128]{0,2,1:T(8,128)(2,1)S(1)}, u32[]{:S(2)}, u32[]{:S(2)}) %collective-permute-start) | collective-permute-done | bytes 32800 | tf_op jit(solution)/shard_map/ppermute | solution.py:19
  28.9 17.2 %all-to-all-done = bf16[64,12,512]{2,1,0:T(8,128)(2,1)S(1)} async-done(((bf16[64,12,512]{2,1,0:T(8,128)(2,1)}), bf16[64,12,512]{2,1,0:T(8,128)(2,1)S(1)}, u32[]{:S(2)}, u32[]{:S(2)}) %all-to-all-start) | async-done | bytes 786464 | tf_op jit(solution)/shard_map/all_to_all | solution.py:34
  46.0 0.4 copy.71
  46.5 5.5 %collective-permute-start.1 = (bf16[64,12,512]{2,0,1:T(8,128)(2,1)S(1)}, bf16[64,12,512]{2,0,1:T(8,128)(2,1)S(1)}, u32[]{:S(2)}, u32[]{:S(2)}) collective-permute-start(bf16[64,12,512]{2,0,1:T(8,128)(2,1)S(1)} %copy.71), channel_id=1, source_target_pairs={{0,4},{4,0},{1,5},{5,1},{2,6},{6,2},{3,7},{7,3},{8,12},{12,8},{9,1... | collective-permute-start | bytes 2359304 | tf_op jit(solution)/shard_map/ppermute | solution.py:28
  52.7 1.2 collective-permute-done.1
  53.9 0.5 fusion.8
  54.9 1.3 reshape.209
  56.2 2.1 convolution_convert_fusion.4
  58.4 3.1 %collective-permute-start.2 = (bf16[128,1920]{1,0:T(8,128)(2,1)S(1)}, bf16[128,1920]{1,0:T(8,128)(2,1)S(1)}, u32[]{:S(2)}, u32[]{:S(2)}) collective-permute-start(bf16[128,1920]{1,0:T(8,128)(2,1)S(1)} %pad_maximum_fusion.4), channel_id=1, source_target_pairs={{0,1},{1,2},{2,3},{3,0},{4,5},{5,6},{6,7},{7,4},{8,9},{9,10},{10,1... | collective-permute-start | bytes 1474568 | tf_op jit(solution)/shard_map/ppermute | solution.py:125
  61.5 3.4 %collective-permute-start.3 = (bf16[128,1920]{1,0:T(8,128)(2,1)S(1)}, bf16[128,1920]{1,0:T(8,128)(2,1)S(1)}, u32[]{:S(2)}, u32[]{:S(2)}) collective-permute-start(bf16[128,1920]{1,0:T(8,128)(2,1)S(1)} %pad_maximum_fusion.4), channel_id=1, source_target_pairs={{0,3},{1,0},{2,1},{3,2},{4,7},{5,4},{6,5},{7,6},{8,11},{9,8},{10,9... | collective-permute-start | bytes 1474568 | tf_op jit(solution)/shard_map/ppermute | solution.py:126
  65.5 8.4 %collective-permute-done.2 = bf16[128,1920]{1,0:T(8,128)(2,1)S(1)} collective-permute-done((bf16[128,1920]{1,0:T(8,128)(2,1)S(1)}, bf16[128,1920]{1,0:T(8,128)(2,1)S(1)}, u32[]{:S(2)}, u32[]{:S(2)}) %collective-permute-start.2) | collective-permute-done | bytes 491552 | tf_op jit(solution)/shard_map/ppermute | solution.py:125
  73.9 0.7 slice.144
  74.6 1.9 collective-permute-start.4
  76.8 4.6 %collective-permute-start.5 = (bf16[64,1920]{1,0:T(8,128)(2,1)S(1)}, bf16[64,1920]{1,0:T(8,128)(2,1)S(1)}, u32[]{:S(2)}, u32[]{:S(2)}) collective-permute-start(bf16[64,1920]{1,0:T(8,128)(2,1)S(1)} %slice.145), channel_id=1, source_target_pairs={{0,3},{1,0},{2,1},{3,2},{4,7},{5,4},{6,5},{7,6},{8,11},{9,8},{10,9... | collective-permute-start | bytes 737288 | tf_op jit(solution)/shard_map/ppermute | solution.py:131
  81.4 2.9 collective-permute-done.4
  84.3 1.0 constant_dynamic-update-slice_fusion.1
  85.7 0.5 copy-done.7
  86.5 3.5 %scatter_custom_fusion = bf16[1536,384]{1,0:T(8,128)(2,1)} fusion(s32[512]{0:T(512)S(1)} %bitcast.120, bf16[512,384]{1,0:T(8,128)(2,1)S(1)} %reshape.231, bf16[]{:T(256)} %constant.94.clone.1), kind=kCustom, calls=%fused_computation.43 | custom fusion | bytes 1179650 | tf_op jit(solution)/shard_map/scatter | solution.py:169
  90.0 2.2 reshape_reshape.6
  92.4 4.2 %collective-permute-start.6 = (bf16[64,12,384]{2,0,1:T(8,128)(2,1)S(1)}, bf16[64,12,384]{2,0,1:T(8,128)(2,1)S(1)}, u32[]{:S(2)}, u32[]{:S(2)}) collective-permute-start(bf16[64,12,384]{2,0,1:T(8,128)(2,1)S(1)} %copy.76), channel_id=1, source_target_pairs={{0,4},{4,0},{1,5},{5,1},{2,6},{6,2},{3,7},{7,3},{8,12},{12,8},{9,1... | collective-permute-start | bytes 1769480 | tf_op jit(solution)/shard_map/ppermute | solution.py:28
  96.6 1.6 collective-permute-done.6
  98.2 0.5 fusion.11
  99.0 1.2 copy.79
  100.2 36.1 %all_to_all.15 = bf16[64,2,12,384]{3,1,2,0:T(2,128)(2,1)S(1)} all-to-all(bf16[64,2,12,384]{3,1,2,0:T(2,128)(2,1)S(1)} %copy.79), channel_id=1, replica_groups=mesh['yz'=64,'core'=2,'tp'=4] {'yz'}, dimensions={0} | all-to-all | bytes 2359296 | tf_op jit(solution)/shard_map/all_to_all | solution.py:44
  136.3 1.4 copy.80
  137.8 2.3 reshape_reshape.7
  140.1 2.6 collective-permute-start.7
  142.7 4.6 %collective-permute-start.8 = (bf16[1536,384]{1,0:T(8,128)(2,1)S(1)}, bf16[1536,384]{1,0:T(8,128)(2,1)S(1)}, u32[]{:S(2)}, u32[]{:S(2)}) collective-permute-start(bf16[1536,384]{1,0:T(8,128)(2,1)S(1)} %reshape_reshape.7), channel_id=1, source_target_pairs={{0,3},{1,0},{2,1},{3,2},{4,7},{5,4},{6,5},{7,6},{8,11},{9,8},{10,9... | collective-permute-start | bytes 3538952 | tf_op jit(solution)/shard_map/ppermute | solution.py:173
  147.3 1.9 fusion.70
  149.2 0.9 fusion.30
  150.1 0.9 fusion.24
  150.9 17.6 %collective-permute-done.7 = bf16[1536,384]{1,0:T(8,128)(2,1)S(1)} collective-permute-done((bf16[1536,384]{1,0:T(8,128)(2,1)S(1)}, bf16[1536,384]{1,0:T(8,128)(2,1)S(1)}, u32[]{:S(2)}, u32[]{:S(2)}) %collective-permute-start.7) | collective-permute-done | bytes 1179680 | tf_op jit(solution)/shard_map/ppermute | solution.py:172
  168.6 1.9 collective-permute-start.9
  170.6 4.6 %collective-permute-start.10 = (bf16[768,384]{1,0:T(8,128)(2,1)S(1)}, bf16[768,384]{1,0:T(8,128)(2,1)S(1)}, u32[]{:S(2)}, u32[]{:S(2)}) collective-permute-start(bf16[768,384]{1,0:T(8,128)(2,1)S(1)} %slice.153), channel_id=1, source_target_pairs={{0,3},{1,0},{2,1},{3,2},{4,7},{5,4},{6,5},{7,6},{8,11},{9,8},{10,9... | collective-permute-start | bytes 1769480 | tf_op jit(solution)/shard_map/ppermute | solution.py:175
  175.2 0.9 convolution_add_fusion.3
  176.1 0.9 convolution_add_fusion.1
  177.0 5.8 %collective-permute-done.9 = bf16[768,384]{1,0:T(8,128)(2,1)S(1)} collective-permute-done((bf16[768,384]{1,0:T(8,128)(2,1)S(1)}, bf16[768,384]{1,0:T(8,128)(2,1)S(1)}, u32[]{:S(2)}, u32[]{:S(2)}) %collective-permute-start.9) | collective-permute-done | bytes 589856 | tf_op jit(solution)/shard_map/ppermute | solution.py:174
  182.8 0.9 collective-permute-done.10
  183.9 0.9 fusion.20
  184.7 0.9 fusion.26
  185.6 1.0 fusion
  186.6 1.4 fusion.5
  188.0 0.9 convolution_convert_fusion.1
  189.0 2.0 collective-permute-start.11
  191.0 5.4 %collective-permute-start.13 = (bf16[768,384]{1,0:T(8,128)(2,1)S(1)}, bf16[768,384]{1,0:T(8,128)(2,1)S(1)}, u32[]{:S(2)}, u32[]{:S(2)}) collective-permute-start(bf16[768,384]{1,0:T(8,128)(2,1)S(1)} %get-tuple-element.16), channel_id=1, source_target_pairs={{0,3},{1,0},{2,1},{3,2},{4,7},{5,4},{6,5},{7,6},{8,11},{9,8},{10,9... | collective-permute-start | bytes 1769480 | tf_op jit(solution)/shard_map/ppermute | solution.py:200
  196.5 0.9 convolution_convert_fusion.2
  197.4 0.9 convolution_convert_fusion
  198.4 4.7 %collective-permute-done.11 = bf16[768,384]{1,0:T(8,128)(2,1)S(1)} collective-permute-done((bf16[768,384]{1,0:T(8,128)(2,1)S(1)}, bf16[768,384]{1,0:T(8,128)(2,1)S(1)}, u32[]{:S(2)}, u32[]{:S(2)}) %collective-permute-start.11) | collective-permute-done | bytes 589856 | tf_op jit(solution)/shard_map/ppermute | solution.py:199
  203.4 1.9 collective-permute-start.12
  205.7 4.6 %collective-permute-start.14 = (bf16[1536,384]{1,0:T(8,128)(2,1)S(1)}, bf16[1536,384]{1,0:T(8,128)(2,1)S(1)}, u32[]{:S(2)}, u32[]{:S(2)}) collective-permute-start(bf16[1536,384]{1,0:T(8,128)(2,1)S(1)} %pad_maximum_fusion.3), channel_id=1, source_target_pairs={{0,3},{1,0},{2,1},{3,2},{4,7},{5,4},{6,5},{7,6},{8,11},{9,8},{10,9... | collective-permute-start | bytes 3538952 | tf_op jit(solution)/shard_map/ppermute | solution.py:210
  210.2 0.9 fusion.6
  211.1 17.4 %collective-permute-done.12 = bf16[1536,384]{1,0:T(8,128)(2,1)S(1)} collective-permute-done((bf16[1536,384]{1,0:T(8,128)(2,1)S(1)}, bf16[1536,384]{1,0:T(8,128)(2,1)S(1)}, u32[]{:S(2)}, u32[]{:S(2)}) %collective-permute-start.12) | collective-permute-done | bytes 1179680 | tf_op jit(solution)/shard_map/ppermute | solution.py:209
  228.6 1.2 collective-permute-done.14
  230.2 1.3 reshape.212
  231.5 24.9 %all-to-all-start.2 = ((bf16[128,12,384]{2,1,0:T(8,128)(2,1)}), bf16[128,12,384]{2,1,0:T(8,128)(2,1)}, u32[]{:S(2)}, u32[]{:S(2)}) async-start(bf16[128,12,384]{2,1,0:T(8,128)(2,1)} %reshape.212), calls=%async_computation.2 | async-start | bytes 3145728 | tf_op jit(solution)/shard_map/all_to_all | solution.py:217
  256.5 0.5 slice_bitcast_fusion.3
  257.0 40.3 %all-to-all-done.2 = bf16[128,12,384]{2,1,0:T(8,128)(2,1)} async-done(((bf16[128,12,384]{2,1,0:T(8,128)(2,1)}), bf16[128,12,384]{2,1,0:T(8,128)(2,1)}, u32[]{:S(2)}, u32[]{:S(2)}) %all-to-all-start.2) | async-done | bytes 1179680 | tf_op jit(solution)/shard_map/all_to_all | solution.py:217
  297.3 2.3 reshape.213
  299.5 1.9 gather_fusion
  301.6 0.6 fusion.72
  302.4 0.8 fusion.46
  (72 shorter events, 5.8 us)
Async XLA Ops:
  0.0 188.0 %copy-start = (bf16[1,384,1536]{2,1,0:T(8,128)(2,1)S(1)}, bf16[1,384,1536]{2,1,0:T(8,128)(2,1)}, u32[]{:S(2)}) copy-start(bf16[1,384,1536]{2,1,0:T(8,128)(2,1)} %param.17) | copy-start | bytes 3538948
  1.9 17.3 %copy-start.4 = (bf16[128,1,128]{2,0,1:T(8,128)(2,1)S(1)}, bf16[128,1,128]{2,0,1:T(8,128)(2,1)}, u32[]{:S(2)}) copy-start(bf16[128,1,128]{2,0,1:T(8,128)(2,1)} %param.12) | copy-start | bytes 98308
  1.9 21.6 %copy-start.3 = (bf16[128,512]{1,0:T(8,128)(2,1)S(1)}, bf16[128,512]{1,0:T(8,128)(2,1)}, u32[]{:S(2)}) copy-start(bf16[128,512]{1,0:T(8,128)(2,1)} %param.11) | copy-start | bytes 393220
  1.9 44.1 %all-to-all-start = ((bf16[64,12,512]{2,1,0:T(8,128)(2,1)}), bf16[64,12,512]{2,1,0:T(8,128)(2,1)S(1)}, u32[]{:S(2)}, u32[]{:S(2)}) async-start(bf16[64,12,512]{2,1,0:T(8,128)(2,1)} %broadcast_in_dim.21), calls=%async_computation | async-start | bytes 2097152 | tf_op jit(solution)/shard_map/all_to_all | solution.py:34
  19.3 9.2 %collective-permute-start = (bf16[128,1,128]{0,2,1:T(8,128)(2,1)S(1)}, bf16[128,1,128]{0,2,1:T(8,128)(2,1)S(1)}, u32[]{:S(2)}, u32[]{:S(2)}) collective-permute-start(bf16[128,1,128]{0,2,1:T(8,128)(2,1)S(1)} %copy.67), channel_id=1, source_target_pairs={{0,4},{4,8},{8,12},{12,16},{16,20},{20,24},{24,28},{28,32},{32,36}... | collective-permute-start | bytes 98312 | tf_op jit(solution)/shard_map/ppermute | solution.py:19
  28.9 23.1 %copy-start.9 = (f32[8]{0:T(128)S(1)}, f32[8]{0:T(128)}, u32[]{:S(2)}) copy-start(f32[8]{0:T(128)} %param.13) | copy-start | bytes 100
  46.5 7.4 %collective-permute-start.1 = (bf16[64,12,512]{2,0,1:T(8,128)(2,1)S(1)}, bf16[64,12,512]{2,0,1:T(8,128)(2,1)S(1)}, u32[]{:S(2)}, u32[]{:S(2)}) collective-permute-start(bf16[64,12,512]{2,0,1:T(8,128)(2,1)S(1)} %copy.71), channel_id=1, source_target_pairs={{0,4},{4,0},{1,5},{5,1},{2,6},{6,2},{3,7},{7,3},{8,12},{12,8},{9,1... | collective-permute-start | bytes 2359304 | tf_op jit(solution)/shard_map/ppermute | solution.py:28
  56.2 2.1 copy-start.1
  56.2 8.7 %copy-start.5 = (s32[128,4]{0,1:T(4,128)S(1)}, s32[128,4]{0,1:T(4,128)}, u32[]{:S(2)}) copy-start(s32[128,4]{0,1:T(4,128)} %param.18) | copy-start | bytes 6148
  58.4 15.5 %collective-permute-start.2 = (bf16[128,1920]{1,0:T(8,128)(2,1)S(1)}, bf16[128,1920]{1,0:T(8,128)(2,1)S(1)}, u32[]{:S(2)}, u32[]{:S(2)}) collective-permute-start(bf16[128,1920]{1,0:T(8,128)(2,1)S(1)} %pad_maximum_fusion.4), channel_id=1, source_target_pairs={{0,1},{1,2},{2,3},{3,0},{4,5},{5,6},{6,7},{7,4},{8,9},{9,10},{10,1... | collective-permute-start | bytes 1474568 | tf_op jit(solution)/shard_map/ppermute | solution.py:125
  61.5 15.2 %collective-permute-start.3 = (bf16[128,1920]{1,0:T(8,128)(2,1)S(1)}, bf16[128,1920]{1,0:T(8,128)(2,1)S(1)}, u32[]{:S(2)}, u32[]{:S(2)}) collective-permute-start(bf16[128,1920]{1,0:T(8,128)(2,1)S(1)} %pad_maximum_fusion.4), channel_id=1, source_target_pairs={{0,3},{1,0},{2,1},{3,2},{4,7},{5,4},{6,5},{7,6},{8,11},{9,8},{10,9... | collective-permute-start | bytes 1474568 | tf_op jit(solution)/shard_map/ppermute | solution.py:126
  74.6 9.7 %collective-permute-start.4 = (bf16[64,1920]{1,0:T(8,128)(2,1)}, bf16[64,1920]{1,0:T(8,128)(2,1)}, u32[]{:S(2)}, u32[]{:S(2)}) collective-permute-start(bf16[64,1920]{1,0:T(8,128)(2,1)} %slice.144), channel_id=1, source_target_pairs={{0,1},{1,2},{2,3},{3,0},{4,5},{5,6},{6,7},{7,4},{8,9},{9,10},{10,1... | collective-permute-start | bytes 737288 | tf_op jit(solution)/shard_map/ppermute | solution.py:130
  76.8 8.5 %collective-permute-start.5 = (bf16[64,1920]{1,0:T(8,128)(2,1)S(1)}, bf16[64,1920]{1,0:T(8,128)(2,1)S(1)}, u32[]{:S(2)}, u32[]{:S(2)}) collective-permute-start(bf16[64,1920]{1,0:T(8,128)(2,1)S(1)} %slice.145), channel_id=1, source_target_pairs={{0,3},{1,0},{2,1},{3,2},{4,7},{5,4},{6,5},{7,6},{8,11},{9,8},{10,9... | collective-permute-start | bytes 737288 | tf_op jit(solution)/shard_map/ppermute | solution.py:131
  85.5 0.7 copy-start.7
  92.4 5.8 %collective-permute-start.6 = (bf16[64,12,384]{2,0,1:T(8,128)(2,1)S(1)}, bf16[64,12,384]{2,0,1:T(8,128)(2,1)S(1)}, u32[]{:S(2)}, u32[]{:S(2)}) collective-permute-start(bf16[64,12,384]{2,0,1:T(8,128)(2,1)S(1)} %copy.76), channel_id=1, source_target_pairs={{0,4},{4,0},{1,5},{5,1},{2,6},{6,2},{3,7},{7,3},{8,12},{12,8},{9,1... | collective-permute-start | bytes 1769480 | tf_op jit(solution)/shard_map/ppermute | solution.py:28
  140.1 28.5 %collective-permute-start.7 = (bf16[1536,384]{1,0:T(8,128)(2,1)S(1)}, bf16[1536,384]{1,0:T(8,128)(2,1)S(1)}, u32[]{:S(2)}, u32[]{:S(2)}) collective-permute-start(bf16[1536,384]{1,0:T(8,128)(2,1)S(1)} %reshape_reshape.7), channel_id=1, source_target_pairs={{0,1},{1,2},{2,3},{3,0},{4,5},{5,6},{6,7},{7,4},{8,9},{9,10},{10,1... | collective-permute-start | bytes 3538952 | tf_op jit(solution)/shard_map/ppermute | solution.py:172
  142.7 27.8 %collective-permute-start.8 = (bf16[1536,384]{1,0:T(8,128)(2,1)S(1)}, bf16[1536,384]{1,0:T(8,128)(2,1)S(1)}, u32[]{:S(2)}, u32[]{:S(2)}) collective-permute-start(bf16[1536,384]{1,0:T(8,128)(2,1)S(1)} %reshape_reshape.7), channel_id=1, source_target_pairs={{0,3},{1,0},{2,1},{3,2},{4,7},{5,4},{6,5},{7,6},{8,11},{9,8},{10,9... | collective-permute-start | bytes 3538952 | tf_op jit(solution)/shard_map/ppermute | solution.py:173
  168.6 14.2 %collective-permute-start.9 = (bf16[768,384]{1,0:T(8,128)(2,1)S(1)}, bf16[768,384]{1,0:T(8,128)(2,1)S(1)}, u32[]{:S(2)}, u32[]{:S(2)}) collective-permute-start(bf16[768,384]{1,0:T(8,128)(2,1)S(1)} %slice.152), channel_id=1, source_target_pairs={{0,1},{1,2},{2,3},{3,0},{4,5},{5,6},{6,7},{7,4},{8,9},{9,10},{10,1... | collective-permute-start | bytes 1769480 | tf_op jit(solution)/shard_map/ppermute | solution.py:174
  170.6 13.2 %collective-permute-start.10 = (bf16[768,384]{1,0:T(8,128)(2,1)S(1)}, bf16[768,384]{1,0:T(8,128)(2,1)S(1)}, u32[]{:S(2)}, u32[]{:S(2)}) collective-permute-start(bf16[768,384]{1,0:T(8,128)(2,1)S(1)} %slice.153), channel_id=1, source_target_pairs={{0,3},{1,0},{2,1},{3,2},{4,7},{5,4},{6,5},{7,6},{8,11},{9,8},{10,9... | collective-permute-start | bytes 1769480 | tf_op jit(solution)/shard_map/ppermute | solution.py:175
  189.0 14.1 %collective-permute-start.11 = (bf16[768,384]{1,0:T(8,128)(2,1)S(1)}, bf16[768,384]{1,0:T(8,128)(2,1)S(1)}, u32[]{:S(2)}, u32[]{:S(2)}) collective-permute-start(bf16[768,384]{1,0:T(8,128)(2,1)S(1)} %get-tuple-element.15), channel_id=1, source_target_pairs={{0,1},{1,2},{2,3},{3,0},{4,5},{5,6},{6,7},{7,4},{8,9},{9,10},{10,1... | collective-permute-start | bytes 1769480 | tf_op jit(solution)/shard_map/ppermute | solution.py:199
  191.0 14.3 %collective-permute-start.13 = (bf16[768,384]{1,0:T(8,128)(2,1)S(1)}, bf16[768,384]{1,0:T(8,128)(2,1)S(1)}, u32[]{:S(2)}, u32[]{:S(2)}) collective-permute-start(bf16[768,384]{1,0:T(8,128)(2,1)S(1)} %get-tuple-element.16), channel_id=1, source_target_pairs={{0,3},{1,0},{2,1},{3,2},{4,7},{5,4},{6,5},{7,6},{8,11},{9,8},{10,9... | collective-permute-start | bytes 1769480 | tf_op jit(solution)/shard_map/ppermute | solution.py:200
  203.4 25.1 %collective-permute-start.12 = (bf16[1536,384]{1,0:T(8,128)(2,1)S(1)}, bf16[1536,384]{1,0:T(8,128)(2,1)S(1)}, u32[]{:S(2)}, u32[]{:S(2)}) collective-permute-start(bf16[1536,384]{1,0:T(8,128)(2,1)S(1)} %pad_maximum_fusion.2), channel_id=1, source_target_pairs={{0,1},{1,2},{2,3},{3,0},{4,5},{5,6},{6,7},{7,4},{8,9},{9,10},{10,1... | collective-permute-start | bytes 3538952 | tf_op jit(solution)/shard_map/ppermute | solution.py:209
  205.7 24.1 %collective-permute-start.14 = (bf16[1536,384]{1,0:T(8,128)(2,1)S(1)}, bf16[1536,384]{1,0:T(8,128)(2,1)S(1)}, u32[]{:S(2)}, u32[]{:S(2)}) collective-permute-start(bf16[1536,384]{1,0:T(8,128)(2,1)S(1)} %pad_maximum_fusion.3), channel_id=1, source_target_pairs={{0,3},{1,0},{2,1},{3,2},{4,7},{5,4},{6,5},{7,6},{8,11},{9,8},{10,9... | collective-permute-start | bytes 3538952 | tf_op jit(solution)/shard_map/ppermute | solution.py:210
  231.5 24.9 %copy-start.6 = (f32[128,4]{0,1:T(4,128)S(1)}, f32[128,4]{0,1:T(4,128)}, u32[]{:S(2)}) copy-start(f32[128,4]{0,1:T(4,128)} %param.19) | copy-start | bytes 6148
  231.5 65.8 %all-to-all-start.2 = ((bf16[128,12,384]{2,1,0:T(8,128)(2,1)}), bf16[128,12,384]{2,1,0:T(8,128)(2,1)}, u32[]{:S(2)}, u32[]{:S(2)}) async-start(bf16[128,12,384]{2,1,0:T(8,128)(2,1)} %reshape.212), calls=%async_computation.2 | async-start | bytes 3145728 | tf_op jit(solution)/shard_map/all_to_all | solution.py:217
  301.5 0.9 copy-start.2
  301.5 0.9 copy-start.8

commit v7 on v6

--- a/solution.py
+++ b/solution.py
@@ -180,14 +180,12 @@
         (from_ahead, (tp_index + 1) % tp_count),
         (opposite, (tp_index + 2) % tp_count),
     ]
-    gate_vals = None
-    up_vals = None
+    both_vals = None
     for piece, quarter_id in pieces:
-        rows_of = lambda w: lax.dynamic_slice_in_dim(w, quarter_id * quarter_w, quarter_w, 0)
-        gate_part = jnp.dot(piece, rows_of(expert_in[0, 0]), preferred_element_type=jnp.float32)
-        up_part = jnp.dot(piece, rows_of(expert_in[0, 1]), preferred_element_type=jnp.float32)
-        gate_vals = gate_part if gate_vals is None else gate_vals + gate_part
-        up_vals = up_part if up_vals is None else up_vals + up_part
+        rows = lax.dynamic_slice_in_dim(expert_in[0], quarter_id * quarter_w, quarter_w, 1)
+        both_part = jnp.einsum("rk,jkh->jrh", piece, rows, preferred_element_type=jnp.float32)
+        both_vals = both_part if both_vals is None else both_vals + both_part
+    gate_vals, up_vals = both_vals[0], both_vals[1]
     activated = ((up_vals + 1.0) * gate_vals * jax.nn.sigmoid(1.702 * gate_vals)).astype(
         jnp.bfloat16
     )
@@ -214,7 +212,7 @@
         + got_ahead.astype(jnp.float32)
     )
     result = summed.astype(jnp.bfloat16).reshape(ctx_count, capacity, quarter_w)
-    returned = lax.all_to_all(result, CTX, 0, 0, tiled=True).reshape(-1, quarter_w)
+    returned = from_experts(result).reshape(-1, quarter_w)
     expert_result = returned[flat_index].reshape(tok_rows, top_count, quarter_w)
     moe_sum = jnp.zeros((tok_rows, quarter_w), jnp.float32)
     for member in range(top_count):

time: 305 us -> 326 us (1.069)
  blocking collectives: 36.1 us -> 84.3 us
  waiting for transfers between devices: 124 us -> 77.8 us
  local copies, waits for them, and re-layouts: 26.8 us -> 47.4 us
  starting transfers between devices: 96.6 us -> 80.6 us
  other arithmetic: 5.12 us -> 14 us
  matrix products: 14 us -> 19.4 us
    all_to_all x0 -> x1, blocking collectives: none -> 46.3 us  [from_experts(): staged = lax.all_to_all(parts, 'yz', 0, 0, tiled=True)]
    all_to_all x1 -> x0, waiting for transfers between devices: 40.3 us -> none  [body(): lax.all_to_all(result, CTX, 0, 0, tiled=True).reshape(-1, quarter_w)]
    all_to_all x1 -> x0, starting transfers between devices: 24.9 us -> none  [body(): lax.all_to_all(result, CTX, 0, 0, tiled=True).reshape(-1, quarter_w)]
    ppermute x1, waiting for transfers between devices: 1.21 us -> 16.1 us  [body(): got_ahead = lax.ppermute(for_behind, 'tp', behind)]
    ppermute x1, waiting for transfers between devices: 17.4 us -> 5.35 us  [body(): got_behind = lax.ppermute(for_ahead, 'tp', ahead)]
    ppermute x2 -> x3, starting transfers between devices: 9.67 us -> 18.1 us  [other_core(): return lax.ppermute(value, 'core', [(0, 1), (1, 0)])]
    another operation x0 -> x3, local copies, waits for them, and re-layouts: none -> 5.35 us  [the longest x2 3.09 us: from_experts(): parts = result.reshape((lax.axis_size('yz'), 2) + result.shape[1:])]
    ppermute x1, waiting for transfers between devices: 4.72 us -> 0.01 us  [body(): via_ahead = lax.ppermute(across[:half_rows], 'tp', ahead)]
  transfers between devices with their start and end apart: 17 -> 17, of which waited for: 13 -> 13; matrix products, arithmetic and copies ran while one was open for 4% -> 9% of each run, Pallas kernels for 0% -> 0%
where the time goes in v7:
time: 326 us; the launch traced here: 324 us
  blocking collectives  84.3 us (26%)
  starting transfers between devices  80.6 us (25%)
  waiting for transfers between devices  77.8 us (24%)
  local copies, waits for them, and re-layouts  47.4 us (15%)
  matrix products  19.4 us (6%)
  other arithmetic  14 us (4%)
    all_to_all x1, blocking collectives, from_experts(): staged = lax.all_to_all(parts, 'yz', 0, 0, tiled=True)  46.3 us
    all_to_all x1, blocking collectives, to_experts(): return lax.all_to_all(staged, 'yz', 0, 0, tiled=True).reshape(outbox.shape)  38 us
    ppermute x3, starting transfers between devices, other_core(): return lax.ppermute(value, 'core', [(0, 1), (1, 0)])  18.1 us
    all_to_all x1, starting transfers between devices, gathered_columns(): mine = lax.all_to_all(spread, 'yz', 0, 0, tiled=True)  17.3 us
    ppermute x1, waiting for transfers between devices, body(): got_ahead = lax.ppermute(for_behind, 'tp', behind)  16.1 us
    ppermute x1, waiting for transfers between devices, body(): from_behind = lax.ppermute(arrived, 'tp', ahead)  15.6 us
    all_to_all x1, waiting for transfers between devices, gathered_columns(): mine = lax.all_to_all(spread, 'yz', 0, 0, tiled=True)  15.2 us
    dot_general x4, matrix products, body(): jnp.einsum('rk,jkh->jrh', piece, rows, preferred_element_type=jnp.float32)  9.68 us
  transfers between devices with their start and end apart: 17, of which 13 were waited for; matrix products, arithmetic and copies ran while one was open for 9% of the time, Pallas kernels for 0%

profile of v7, /device:TPU:1, one launch (start us, length us, event | category | flops | bytes accessed | tf_op | source)
XLA Modules:
  0.0 324.2 jit_solution(17309769069299345660)
XLA Ops:
  0.0 2.0 broadcast_in_dim.21
  2.0 17.3 %all-to-all-start = ((bf16[64,12,512]{2,1,0:T(8,128)(2,1)}), bf16[64,12,512]{2,1,0:T(8,128)(2,1)S(1)}, u32[]{:S(2)}, u32[]{:S(2)}) async-start(bf16[64,12,512]{2,1,0:T(8,128)(2,1)} %broadcast_in_dim.21), calls=%async_computation | async-start | bytes 2097152 | tf_op jit(solution)/shard_map/all_to_all | solution.py:34
  20.0 4.0 %collective-permute-start = (bf16[128,1,128]{0,2,1:T(8,128)(2,1)}, bf16[128,1,128]{0,2,1:T(8,128)(2,1)}, u32[]{:S(2)}, u32[]{:S(2)}) collective-permute-start(bf16[128,1,128]{0,2,1:T(8,128)(2,1)} %copy.106), channel_id=1, source_target_pairs={{0,4},{4,8},{8,12},{12,16},{16,20},{20,24},{24,28},{28,32},{32,36}... | collective-permute-start | bytes 98312 | tf_op jit(solution)/shard_map/ppermute | solution.py:19
  24.8 1.0 copy.108
  25.8 2.9 collective-permute-done
  28.8 2.1 select_reduce_fusion
  30.9 15.2 %all-to-all-done = bf16[64,12,512]{2,1,0:T(8,128)(2,1)S(1)} async-done(((bf16[64,12,512]{2,1,0:T(8,128)(2,1)}), bf16[64,12,512]{2,1,0:T(8,128)(2,1)S(1)}, u32[]{:S(2)}, u32[]{:S(2)}) %all-to-all-start) | async-done | bytes 786464 | tf_op jit(solution)/shard_map/all_to_all | solution.py:34
  46.5 5.5 %collective-permute-start.1 = (bf16[64,12,512]{2,0,1:T(8,128)(2,1)S(1)}, bf16[64,12,512]{2,0,1:T(8,128)(2,1)S(1)}, u32[]{:S(2)}, u32[]{:S(2)}) collective-permute-start(bf16[64,12,512]{2,0,1:T(8,128)(2,1)S(1)} %copy.110), channel_id=1, source_target_pairs={{0,4},{4,0},{1,5},{5,1},{2,6},{6,2},{3,7},{7,3},{8,12},{12,8},{9,1... | collective-permute-start | bytes 2359304 | tf_op jit(solution)/shard_map/ppermute | solution.py:28
  52.4 1.7 convolution_convert_fusion.5
  55.0 1.5 copy.113
  56.5 3.7 %reshape.207 = bf16[1536,512]{1,0:T(8,128)(2,1)} reshape(bf16[64,2,12,512]{3,2,1,0:T(8,128)(2,1)} %copy.113) | data formatting | bytes 3145728 | tf_op jit(solution)/shard_map/reshape | solution.py:35
  60.2 2.1 convolution_convert_fusion.4
  63.1 3.1 collective-permute-start.2
  66.2 3.4 %collective-permute-start.3 = (bf16[128,1920]{1,0:T(8,128)(2,1)}, bf16[128,1920]{1,0:T(8,128)(2,1)}, u32[]{:S(2)}, u32[]{:S(2)}) collective-permute-start(bf16[128,1920]{1,0:T(8,128)(2,1)} %pad_maximum_fusion.5), channel_id=1, source_target_pairs={{0,3},{1,0},{2,1},{3,2},{4,7},{5,4},{6,5},{7,6},{8,11},{9,8},{10,9... | collective-permute-start | bytes 1474568 | tf_op jit(solution)/shard_map/ppermute | solution.py:126
  70.2 8.9 %collective-permute-done.2 = bf16[128,1920]{1,0:T(8,128)(2,1)S(1)} collective-permute-done((bf16[128,1920]{1,0:T(8,128)(2,1)}, bf16[128,1920]{1,0:T(8,128)(2,1)S(1)}, u32[]{:S(2)}, u32[]{:S(2)}) %collective-permute-start.2) | collective-permute-done | bytes 491552 | tf_op jit(solution)/shard_map/ppermute | solution.py:125
  79.8 2.0 collective-permute-start.4
  82.1 1.7 slice.149
  83.7 4.5 %collective-permute-start.5 = (bf16[64,1920]{1,0:T(8,128)(2,1)}, bf16[64,1920]{1,0:T(8,128)(2,1)S(1)}, u32[]{:S(2)}, u32[]{:S(2)}) collective-permute-start(bf16[64,1920]{1,0:T(8,128)(2,1)} %slice.149), channel_id=1, source_target_pairs={{0,3},{1,0},{2,1},{3,2},{4,7},{5,4},{6,5},{7,6},{8,11},{9,8},{10,9... | collective-permute-start | bytes 737288 | tf_op jit(solution)/shard_map/ppermute | solution.py:131
  88.3 1.5 collective-permute-done.4
  89.7 1.0 constant_dynamic-update-slice_fusion.1
  90.7 1.8 collective-permute-done.5
  92.6 1.3 convert_add_fusion
  93.9 1.1 multiply_reduce_fusion.2
  96.1 4.0 %scatter_custom_fusion = bf16[1536,384]{1,0:T(8,128)(2,1)} fusion(s32[512]{0:T(512)S(1)} %bitcast.148, bf16[512,384]{1,0:T(8,128)(2,1)} %reshape.227, bf16[]{:T(256)} %constant.90.clone.1), kind=kCustom, calls=%fused_computation.67 | custom fusion | bytes 1180160 | tf_op jit(solution)/shard_map/scatter | solution.py:169
  100.1 3.2 reshape_reshape.12
  103.3 1.6 fusion.24
  105.0 4.0 %collective-permute-start.6 = (bf16[64,12,384]{2,0,1:T(8,128)(2,1)S(1)}, bf16[64,12,384]{2,0,1:T(8,128)(2,1)S(1)}, u32[]{:S(2)}, u32[]{:S(2)}) collective-permute-start(bf16[64,12,384]{2,0,1:T(8,128)(2,1)S(1)} %copy.118), channel_id=1, source_target_pairs={{0,4},{4,0},{1,5},{5,1},{2,6},{6,2},{3,7},{7,3},{8,12},{12,8},{9,1... | collective-permute-start | bytes 1769480 | tf_op jit(solution)/shard_map/ppermute | solution.py:28
  109.1 1.6 collective-permute-done.6
  111.5 1.2 copy.121
  112.7 38.0 %all_to_all.15 = bf16[64,2,12,384]{3,1,2,0:T(2,128)(2,1)S(1)} all-to-all(bf16[64,2,12,384]{3,1,2,0:T(2,128)(2,1)S(1)} %copy.121), channel_id=1, replica_groups=mesh['yz'=64,'core'=2,'tp'=4] {'yz'}, dimensions={0} | all-to-all | bytes 2359296 | tf_op jit(solution)/shard_map/all_to_all | solution.py:44
  150.7 1.4 copy.122
  152.1 3.2 reshape_reshape.13
  155.4 2.6 collective-permute-start.7
  158.0 4.5 %collective-permute-start.8 = (bf16[1536,384]{1,0:T(8,128)(2,1)}, bf16[1536,384]{1,0:T(8,128)(2,1)}, u32[]{:S(2)}, u32[]{:S(2)}) collective-permute-start(bf16[1536,384]{1,0:T(8,128)(2,1)} %reshape_reshape.13), channel_id=1, source_target_pairs={{0,3},{1,0},{2,1},{3,2},{4,7},{5,4},{6,5},{7,6},{8,11},{9,8},{10,9... | collective-permute-start | bytes 3538952 | tf_op jit(solution)/shard_map/ppermute | solution.py:173
  162.5 3.2 reshape.233
  165.7 2.7 fusion.28
  168.4 15.6 %collective-permute-done.7 = bf16[1536,384]{1,0:T(8,128)(2,1)} collective-permute-done((bf16[1536,384]{1,0:T(8,128)(2,1)}, bf16[1536,384]{1,0:T(8,128)(2,1)}, u32[]{:S(2)}, u32[]{:S(2)}) %collective-permute-start.7) | collective-permute-done | bytes 1179680 | tf_op jit(solution)/shard_map/ppermute | solution.py:172
  184.0 1.1 slice.156
  185.1 1.9 collective-permute-start.9
  187.1 1.1 slice.157
  188.2 4.6 %collective-permute-start.10 = (bf16[768,384]{1,0:T(8,128)(2,1)S(1)}, bf16[768,384]{1,0:T(8,128)(2,1)S(1)}, u32[]{:S(2)}, u32[]{:S(2)}) collective-permute-start(bf16[768,384]{1,0:T(8,128)(2,1)S(1)} %slice.157), channel_id=1, source_target_pairs={{0,3},{1,0},{2,1},{3,2},{4,7},{5,4},{6,5},{7,6},{8,11},{9,8},{10,9... | collective-permute-start | bytes 1769480 | tf_op jit(solution)/shard_map/ppermute | solution.py:175
  192.8 2.7 fusion.12
  195.5 2.7 fusion.14
  198.2 1.1 collective-permute-done.9
  199.3 2.0 collective-permute-done.10
  201.4 1.6 add_bitcast_fusion
  205.3 5.3 %collective-permute-start.13 = (bf16[768,384]{1,0:T(8,128)(2,1)S(1)}, bf16[768,384]{1,0:T(8,128)(2,1)S(1)}, u32[]{:S(2)}, u32[]{:S(2)}) collective-permute-start(bf16[768,384]{1,0:T(8,128)(2,1)S(1)} %get-tuple-element.18), channel_id=1, source_target_pairs={{0,3},{1,0},{2,1},{3,2},{4,7},{5,4},{6,5},{7,6},{8,11},{9,8},{10,9... | collective-permute-start | bytes 1769480 | tf_op jit(solution)/shard_map/ppermute | solution.py:198
  210.6 1.9 collective-permute-start.11
  214.6 3.8 %collective-permute-done.13 = bf16[768,384]{1,0:T(8,128)(2,1)S(1)} collective-permute-done((bf16[768,384]{1,0:T(8,128)(2,1)S(1)}, bf16[768,384]{1,0:T(8,128)(2,1)S(1)}, u32[]{:S(2)}, u32[]{:S(2)}) %collective-permute-start.13) | collective-permute-done | bytes 589856 | tf_op jit(solution)/shard_map/ppermute | solution.py:198
  218.6 5.3 %collective-permute-start.14 = (bf16[1536,384]{1,0:T(8,128)(2,1)S(1)}, bf16[1536,384]{1,0:T(8,128)(2,1)S(1)}, u32[]{:S(2)}, u32[]{:S(2)}) collective-permute-start(bf16[1536,384]{1,0:T(8,128)(2,1)S(1)} %pad_maximum_fusion.4), channel_id=1, source_target_pairs={{0,3},{1,0},{2,1},{3,2},{4,7},{5,4},{6,5},{7,6},{8,11},{9,8},{10,9... | collective-permute-start | bytes 3538952 | tf_op jit(solution)/shard_map/ppermute | solution.py:208
  224.3 2.1 collective-permute-start.12
  227.4 16.1 %collective-permute-done.14 = bf16[1536,384]{1,0:T(8,128)(2,1)S(1)} collective-permute-done((bf16[1536,384]{1,0:T(8,128)(2,1)S(1)}, bf16[1536,384]{1,0:T(8,128)(2,1)S(1)}, u32[]{:S(2)}, u32[]{:S(2)}) %collective-permute-start.14) | collective-permute-done | bytes 1179680 | tf_op jit(solution)/shard_map/ppermute | solution.py:208
  243.5 5.3 %collective-permute-done.12 = bf16[1536,384]{1,0:T(8,128)(2,1)S(1)} collective-permute-done((bf16[1536,384]{1,0:T(8,128)(2,1)S(1)}, bf16[1536,384]{1,0:T(8,128)(2,1)S(1)}, u32[]{:S(2)}, u32[]{:S(2)}) %collective-permute-start.12) | collective-permute-done | bytes 1179680 | tf_op jit(solution)/shard_map/ppermute | solution.py:207
  248.8 1.5 add_convert_fusion
  250.3 2.2 reshape_reshape.14
  253.4 46.3 %all_to_all.16 = bf16[64,2,12,384]{3,1,2,0:T(2,128)(2,1)S(1)} all-to-all(bf16[64,2,12,384]{3,1,2,0:T(2,128)(2,1)S(1)} %copy.126), channel_id=1, replica_groups=mesh['yz'=64,'core'=2,'tp'=4] {'yz'}, dimensions={0} | all-to-all | bytes 2359296 | tf_op jit(solution)/shard_map/all_to_all | solution.py:49
  299.8 1.6 fusion.68
  302.6 8.5 %collective-permute-start.15 = (bf16[64,12,384]{2,0,1:T(8,128)(2,1)}, bf16[64,12,384]{2,0,1:T(8,128)(2,1)}, u32[]{:S(2)}, u32[]{:S(2)}) collective-permute-start(bf16[64,12,384]{2,0,1:T(8,128)(2,1)} %copy.129), channel_id=1, source_target_pairs={{0,4},{4,0},{1,5},{5,1},{2,6},{6,2},{3,7},{7,3},{8,12},{12,8},{9,1... | collective-permute-start | bytes 1769480 | tf_op jit(solution)/shard_map/ppermute | solution.py:28
  311.2 1.9 collective-permute-done.15
  313.1 1.6 fusion.21
  315.0 1.3 copy.132
  316.4 2.3 reshape_reshape.15
  318.6 2.6 gather_fusion
  321.2 1.2 reshape.210
  (87 shorter events, 17.4 us)
Async XLA Ops:
  0.0 165.7 %copy-start = (bf16[1,2,1536,384]{3,2,1,0:T(8,128)(2,1)S(1)}, bf16[1,2,1536,384]{3,2,1,0:T(8,128)(2,1)}, u32[]{:S(2)}) copy-start(bf16[1,2,1536,384]{3,2,1,0:T(8,128)(2,1)} %param.16) | copy-start | bytes 7077892
  2.0 17.3 %copy-start.11 = (bf16[128,1,128]{2,0,1:T(8,128)(2,1)S(1)}, bf16[128,1,128]{2,0,1:T(8,128)(2,1)}, u32[]{:S(2)}) copy-start(bf16[128,1,128]{2,0,1:T(8,128)(2,1)} %param.12) | copy-start | bytes 98308
  2.0 44.1 %all-to-all-start = ((bf16[64,12,512]{2,1,0:T(8,128)(2,1)}), bf16[64,12,512]{2,1,0:T(8,128)(2,1)S(1)}, u32[]{:S(2)}, u32[]{:S(2)}) async-start(bf16[64,12,512]{2,1,0:T(8,128)(2,1)} %broadcast_in_dim.21), calls=%async_computation | async-start | bytes 2097152 | tf_op jit(solution)/shard_map/all_to_all | solution.py:34
  20.0 8.8 %collective-permute-start = (bf16[128,1,128]{0,2,1:T(8,128)(2,1)}, bf16[128,1,128]{0,2,1:T(8,128)(2,1)}, u32[]{:S(2)}, u32[]{:S(2)}) collective-permute-start(bf16[128,1,128]{0,2,1:T(8,128)(2,1)} %copy.106), channel_id=1, source_target_pairs={{0,4},{4,8},{8,12},{12,16},{16,20},{20,24},{24,28},{28,32},{32,36}... | collective-permute-start | bytes 98312 | tf_op jit(solution)/shard_map/ppermute | solution.py:19
  30.9 21.1 %copy-start.15 = (f32[8]{0:T(128)S(1)}, f32[8]{0:T(128)}, u32[]{:S(2)}) copy-start(f32[8]{0:T(128)} %param.13) | copy-start | bytes 100
  30.9 21.2 %copy-start.8 = (pred[128,256]{0,1:T(8,128)(4,1)S(1)}, pred[128,256]{0,1:T(8,128)(4,1)}, u32[]{:S(2)}) copy-start(pred[128,256]{0,1:T(8,128)(4,1)} %and_and_fusion) | copy-start | bytes 98308
  46.1 6.1 %copy-start.3 = (f32[1,8,128,256]{2,3,1,0:T(8,128)S(1)}, f32[1,8,128,256]{2,3,1,0:T(8,128)}, u32[]{:S(2)}) copy-start(f32[1,8,128,256]{2,3,1,0:T(8,128)} %get-tuple-element.28) | copy-start | bytes 3145732
  46.5 7.6 %collective-permute-start.1 = (bf16[64,12,512]{2,0,1:T(8,128)(2,1)S(1)}, bf16[64,12,512]{2,0,1:T(8,128)(2,1)S(1)}, u32[]{:S(2)}, u32[]{:S(2)}) collective-permute-start(bf16[64,12,512]{2,0,1:T(8,128)(2,1)S(1)} %copy.110), channel_id=1, source_target_pairs={{0,4},{4,0},{1,5},{5,1},{2,6},{6,2},{3,7},{7,3},{8,12},{12,8},{9,1... | collective-permute-start | bytes 2359304 | tf_op jit(solution)/shard_map/ppermute | solution.py:28
  56.5 3.7 %copy-start.9 = (bf16[64,8,128]{2,0,1:T(8,128)(2,1)S(1)}, bf16[64,8,128]{2,0,1:T(8,128)(2,1)}, u32[]{:S(2)}) copy-start(bf16[64,8,128]{2,0,1:T(8,128)(2,1)} %convolution_convert_fusion.5) | copy-start | bytes 393220
  60.2 2.1 copy-start.4
  60.2 9.4 %copy-start.12 = (s32[128,4]{0,1:T(4,128)S(1)}, s32[128,4]{0,1:T(4,128)}, u32[]{:S(2)}) copy-start(s32[128,4]{0,1:T(4,128)} %param.18) | copy-start | bytes 6148
  63.1 15.9 %collective-permute-start.2 = (bf16[128,1920]{1,0:T(8,128)(2,1)}, bf16[128,1920]{1,0:T(8,128)(2,1)S(1)}, u32[]{:S(2)}, u32[]{:S(2)}) collective-permute-start(bf16[128,1920]{1,0:T(8,128)(2,1)} %pad_maximum_fusion.5), channel_id=1, source_target_pairs={{0,1},{1,2},{2,3},{3,0},{4,5},{5,6},{6,7},{7,4},{8,9},{9,10},{10,1... | collective-permute-start | bytes 1474568 | tf_op jit(solution)/shard_map/ppermute | solution.py:125
  66.2 15.8 %collective-permute-start.3 = (bf16[128,1920]{1,0:T(8,128)(2,1)}, bf16[128,1920]{1,0:T(8,128)(2,1)}, u32[]{:S(2)}, u32[]{:S(2)}) collective-permute-start(bf16[128,1920]{1,0:T(8,128)(2,1)} %pad_maximum_fusion.5), channel_id=1, source_target_pairs={{0,3},{1,0},{2,1},{3,2},{4,7},{5,4},{6,5},{7,6},{8,11},{9,8},{10,9... | collective-permute-start | bytes 1474568 | tf_op jit(solution)/shard_map/ppermute | solution.py:126
  79.1 13.5 %copy-start.7 = (bf16[128,1920]{1,0:T(8,128)(2,1)}, bf16[128,1920]{1,0:T(8,128)(2,1)S(1)}, u32[]{:S(2)}) copy-start(bf16[128,1920]{1,0:T(8,128)(2,1)S(1)} %collective-permute-done.2) | copy-start | bytes 1474564
  79.8 9.9 %collective-permute-start.4 = (bf16[64,1920]{1,0:T(8,128)(2,1)}, bf16[64,1920]{1,0:T(8,128)(2,1)}, u32[]{:S(2)}, u32[]{:S(2)}) collective-permute-start(bf16[64,1920]{1,0:T(8,128)(2,1)} %slice.148), channel_id=1, source_target_pairs={{0,1},{1,2},{2,3},{3,0},{4,5},{5,6},{6,7},{7,4},{8,9},{9,10},{10,1... | collective-permute-start | bytes 737288 | tf_op jit(solution)/shard_map/ppermute | solution.py:130
  83.7 8.8 %collective-permute-start.5 = (bf16[64,1920]{1,0:T(8,128)(2,1)}, bf16[64,1920]{1,0:T(8,128)(2,1)S(1)}, u32[]{:S(2)}, u32[]{:S(2)}) collective-permute-start(bf16[64,1920]{1,0:T(8,128)(2,1)} %slice.149), channel_id=1, source_target_pairs={{0,3},{1,0},{2,1},{3,2},{4,7},{5,4},{6,5},{7,6},{8,11},{9,8},{10,9... | collective-permute-start | bytes 737288 | tf_op jit(solution)/shard_map/ppermute | solution.py:131
  92.6 1.3 copy-start.5
  93.9 1.2 copy-start.14
  103.3 7.4 %copy-start.2 = (bf16[64,2,12,384]{3,2,1,0:T(8,128)(2,1)S(1)}, bf16[64,2,12,384]{3,2,1,0:T(8,128)(2,1)}, u32[]{:S(2)}) copy-start(bf16[64,2,12,384]{3,2,1,0:T(8,128)(2,1)} %reshape_reshape.12) | copy-start | bytes 3538948
  105.0 5.7 %collective-permute-start.6 = (bf16[64,12,384]{2,0,1:T(8,128)(2,1)S(1)}, bf16[64,12,384]{2,0,1:T(8,128)(2,1)S(1)}, u32[]{:S(2)}, u32[]{:S(2)}) collective-permute-start(bf16[64,12,384]{2,0,1:T(8,128)(2,1)S(1)} %copy.118), channel_id=1, source_target_pairs={{0,4},{4,0},{1,5},{5,1},{2,6},{6,2},{3,7},{7,3},{8,12},{12,8},{9,1... | collective-permute-start | bytes 1769480 | tf_op jit(solution)/shard_map/ppermute | solution.py:28
  155.4 28.6 %collective-permute-start.7 = (bf16[1536,384]{1,0:T(8,128)(2,1)}, bf16[1536,384]{1,0:T(8,128)(2,1)}, u32[]{:S(2)}, u32[]{:S(2)}) collective-permute-start(bf16[1536,384]{1,0:T(8,128)(2,1)} %reshape_reshape.13), channel_id=1, source_target_pairs={{0,1},{1,2},{2,3},{3,0},{4,5},{5,6},{6,7},{7,4},{8,9},{9,10},{10,1... | collective-permute-start | bytes 3538952 | tf_op jit(solution)/shard_map/ppermute | solution.py:172
  158.0 29.1 %collective-permute-start.8 = (bf16[1536,384]{1,0:T(8,128)(2,1)}, bf16[1536,384]{1,0:T(8,128)(2,1)}, u32[]{:S(2)}, u32[]{:S(2)}) collective-permute-start(bf16[1536,384]{1,0:T(8,128)(2,1)} %reshape_reshape.13), channel_id=1, source_target_pairs={{0,3},{1,0},{2,1},{3,2},{4,7},{5,4},{6,5},{7,6},{8,11},{9,8},{10,9... | collective-permute-start | bytes 3538952 | tf_op jit(solution)/shard_map/ppermute | solution.py:173
  185.1 14.2 %collective-permute-start.9 = (bf16[768,384]{1,0:T(8,128)(2,1)S(1)}, bf16[768,384]{1,0:T(8,128)(2,1)S(1)}, u32[]{:S(2)}, u32[]{:S(2)}) collective-permute-start(bf16[768,384]{1,0:T(8,128)(2,1)S(1)} %slice.156), channel_id=1, source_target_pairs={{0,1},{1,2},{2,3},{3,0},{4,5},{5,6},{6,7},{7,4},{8,9},{9,10},{10,1... | collective-permute-start | bytes 1769480 | tf_op jit(solution)/shard_map/ppermute | solution.py:174
  188.2 13.2 %collective-permute-start.10 = (bf16[768,384]{1,0:T(8,128)(2,1)S(1)}, bf16[768,384]{1,0:T(8,128)(2,1)S(1)}, u32[]{:S(2)}, u32[]{:S(2)}) collective-permute-start(bf16[768,384]{1,0:T(8,128)(2,1)S(1)} %slice.157), channel_id=1, source_target_pairs={{0,3},{1,0},{2,1},{3,2},{4,7},{5,4},{6,5},{7,6},{8,11},{9,8},{10,9... | collective-permute-start | bytes 1769480 | tf_op jit(solution)/shard_map/ppermute | solution.py:175
  202.9 1.3 copy-start.10
  205.3 13.1 %collective-permute-start.13 = (bf16[768,384]{1,0:T(8,128)(2,1)S(1)}, bf16[768,384]{1,0:T(8,128)(2,1)S(1)}, u32[]{:S(2)}, u32[]{:S(2)}) collective-permute-start(bf16[768,384]{1,0:T(8,128)(2,1)S(1)} %get-tuple-element.18), channel_id=1, source_target_pairs={{0,3},{1,0},{2,1},{3,2},{4,7},{5,4},{6,5},{7,6},{8,11},{9,8},{10,9... | collective-permute-start | bytes 1769480 | tf_op jit(solution)/shard_map/ppermute | solution.py:198
  210.6 13.4 %collective-permute-start.11 = (bf16[768,384]{1,0:T(8,128)(2,1)S(1)}, bf16[768,384]{1,0:T(8,128)(2,1)S(1)}, u32[]{:S(2)}, u32[]{:S(2)}) collective-permute-start(bf16[768,384]{1,0:T(8,128)(2,1)S(1)} %get-tuple-element.17), channel_id=1, source_target_pairs={{0,1},{1,2},{2,3},{3,0},{4,5},{5,6},{6,7},{7,4},{8,9},{9,10},{10,1... | collective-permute-start | bytes 1769480 | tf_op jit(solution)/shard_map/ppermute | solution.py:197
  218.6 24.9 %collective-permute-start.14 = (bf16[1536,384]{1,0:T(8,128)(2,1)S(1)}, bf16[1536,384]{1,0:T(8,128)(2,1)S(1)}, u32[]{:S(2)}, u32[]{:S(2)}) collective-permute-start(bf16[1536,384]{1,0:T(8,128)(2,1)S(1)} %pad_maximum_fusion.4), channel_id=1, source_target_pairs={{0,3},{1,0},{2,1},{3,2},{4,7},{5,4},{6,5},{7,6},{8,11},{9,8},{10,9... | collective-permute-start | bytes 3538952 | tf_op jit(solution)/shard_map/ppermute | solution.py:208
  224.3 24.6 %collective-permute-start.12 = (bf16[1536,384]{1,0:T(8,128)(2,1)S(1)}, bf16[1536,384]{1,0:T(8,128)(2,1)S(1)}, u32[]{:S(2)}, u32[]{:S(2)}) collective-permute-start(bf16[1536,384]{1,0:T(8,128)(2,1)S(1)} %pad_maximum_fusion.3), channel_id=1, source_target_pairs={{0,1},{1,2},{2,3},{3,0},{4,5},{5,6},{6,7},{7,4},{8,9},{9,10},{10,1... | collective-permute-start | bytes 3538952 | tf_op jit(solution)/shard_map/ppermute | solution.py:207
  301.6 9.5 %copy-start.13 = (f32[128,4]{0,1:T(4,128)S(1)}, f32[128,4]{0,1:T(4,128)}, u32[]{:S(2)}) copy-start(f32[128,4]{0,1:T(4,128)} %param.19) | copy-start | bytes 6148
  302.6 10.4 %collective-permute-start.15 = (bf16[64,12,384]{2,0,1:T(8,128)(2,1)}, bf16[64,12,384]{2,0,1:T(8,128)(2,1)}, u32[]{:S(2)}, u32[]{:S(2)}) collective-permute-start(bf16[64,12,384]{2,0,1:T(8,128)(2,1)} %copy.129), channel_id=1, source_target_pairs={{0,4},{4,0},{1,5},{5,1},{2,6},{6,2},{3,7},{7,3},{8,12},{12,8},{9,1... | collective-permute-start | bytes 1769480 | tf_op jit(solution)/shard_map/ppermute | solution.py:28
  321.2 3.0 copy-start.1
  322.5 0.9 copy-start.6

commit v8 on v6

--- a/solution.py
+++ b/solution.py
@@ -32,7 +32,7 @@
     rows = block.T
     spread = jnp.broadcast_to(rows[None], (lax.axis_size("yz"),) + rows.shape)
     mine = lax.all_to_all(spread, "yz", 0, 0, tiled=True)
-    return by_core(mine, other_core(mine)).reshape(-1, rows.shape[1])
+    return mine, other_core(mine)
 
 
 def to_experts(outbox):
@@ -108,12 +108,14 @@
         factor,
     )
     outputs = mixed.reshape(block_row_count, q_heads * head_dim)
-    head_partial = lax.dot_general(
-        outputs,
-        gathered_columns(out_proj),
-        (((1,), (1,)), ((), ())),
-        preferred_element_type=jnp.float32,
-    )
+    own_columns, other_columns = gathered_columns(out_proj)
+    contract = (((1,), (2,)), ((), ()))
+    own_part = lax.dot_general(outputs, own_columns, contract, preferred_element_type=jnp.float32)
+    other_part = lax.dot_general(outputs, other_columns, contract, preferred_element_type=jnp.float32)
+    first_core = lax.axis_index("core") == 0
+    head_partial = jnp.stack(
+        [jnp.where(first_core, own_part, other_part), jnp.where(first_core, other_part, own_part)], 2
+    ).reshape(own_part.shape[0], -1)
     d_model = head_partial.shape[1]
     tp_count = lax.axis_size("tp")
     tp_index = lax.axis_index("tp")

time: 305 us -> 313 us (1.026)
  waiting for transfers between devices: 124 us -> 130 us
    ppermute x1, waiting for transfers between devices: 8.42 us -> 0.01 us  [body(): from_behind = lax.ppermute(sent, 'tp', ahead)]
    ppermute x1, waiting for transfers between devices: 0.01 us -> 8 us  [body(): from_ahead = lax.ppermute(sent, 'tp', behind)]
    ppermute x1, waiting for transfers between devices: 0.01 us -> 7.08 us  [body(): lax.ppermute(from_ahead[half_tok:], 'tp', behind)]
  transfers between devices with their start and end apart: 17 -> 17, of which waited for: 13 -> 14; matrix products, arithmetic and copies ran while one was open for 4% -> 4% of each run, Pallas kernels for 0% -> 0%
where the time goes in v8:
time: 313 us; the launch traced here: 311 us
  waiting for transfers between devices  130 us (42%)
  starting transfers between devices  96.7 us (31%)
  blocking collectives  37.5 us (12%)
  local copies, waits for them, and re-layouts  25.8 us (8%)
  matrix products  13.4 us (4%)
  other arithmetic  6.82 us (2%)
    all_to_all x1, waiting for transfers between devices, body(): lax.all_to_all(result, CTX, 0, 0, tiled=True).reshape(-1, quarter_w)  40.2 us
    all_to_all x1, blocking collectives, to_experts(): return lax.all_to_all(staged, 'yz', 0, 0, tiled=True).reshape(outbox.shape)  37.5 us
    all_to_all x1, starting transfers between devices, body(): lax.all_to_all(result, CTX, 0, 0, tiled=True).reshape(-1, quarter_w)  25.2 us
    ppermute x1, waiting for transfers between devices, body(): from_behind = lax.ppermute(arrived, 'tp', ahead)  17.3 us
    all_to_all x1, starting transfers between devices, gathered_columns(): mine = lax.all_to_all(spread, 'yz', 0, 0, tiled=True)  17.3 us
    ppermute x1, waiting for transfers between devices, body(): got_behind = lax.ppermute(for_ahead, 'tp', ahead)  17.2 us
    all_to_all x1, waiting for transfers between devices, gathered_columns(): mine = lax.all_to_all(spread, 'yz', 0, 0, tiled=True)  15.6 us
    ppermute x2, starting transfers between devices, other_core(): return lax.ppermute(value, 'core', [(0, 1), (1, 0)])  9.79 us
  transfers between devices with their start and end apart: 17, of which 14 were waited for; matrix products, arithmetic and copies ran while one was open for 4% of the time, Pallas kernels for 0%

profile of v8, /device:TPU:1, one launch (start us, length us, event | category | flops | bytes accessed | tf_op | source)
XLA Modules:
  0.0 311.0 jit_solution(13212435685409214911)
XLA Ops:
  0.0 1.9 broadcast_in_dim.21
  1.9 17.3 %all-to-all-start = ((bf16[64,12,512]{2,1,0:T(8,128)(2,1)}), bf16[64,12,512]{2,1,0:T(8,128)(2,1)S(1)}, u32[]{:S(2)}, u32[]{:S(2)}) async-start(bf16[64,12,512]{2,1,0:T(8,128)(2,1)} %broadcast_in_dim.21), calls=%async_computation | async-start | bytes 2097152 | tf_op jit(solution)/shard_map/all_to_all | solution.py:34
  19.3 4.0 %collective-permute-start = (bf16[128,1,128]{0,2,1:T(8,128)(2,1)S(1)}, bf16[128,1,128]{0,2,1:T(8,128)(2,1)S(1)}, u32[]{:S(2)}, u32[]{:S(2)}) collective-permute-start(bf16[128,1,128]{0,2,1:T(8,128)(2,1)S(1)} %copy.69), channel_id=1, source_target_pairs={{0,4},{4,8},{8,12},{12,16},{16,20},{20,24},{24,28},{28,32},{32,36}... | collective-permute-start | bytes 98312 | tf_op jit(solution)/shard_map/ppermute | solution.py:19
  23.9 4.8 %collective-permute-done = bf16[128,1,128]{0,2,1:T(8,128)(2,1)S(1)} collective-permute-done((bf16[128,1,128]{0,2,1:T(8,128)(2,1)S(1)}, bf16[128,1,128]{0,2,1:T(8,128)(2,1)S(1)}, u32[]{:S(2)}, u32[]{:S(2)}) %collective-permute-start) | collective-permute-done | bytes 32800 | tf_op jit(solution)/shard_map/ppermute | solution.py:19
  28.6 0.6 copy-done.7
  29.2 1.1 select_reduce_fusion
  30.4 15.6 %all-to-all-done = bf16[64,12,512]{2,1,0:T(8,128)(2,1)S(1)} async-done(((bf16[64,12,512]{2,1,0:T(8,128)(2,1)}), bf16[64,12,512]{2,1,0:T(8,128)(2,1)S(1)}, u32[]{:S(2)}, u32[]{:S(2)}) %all-to-all-start) | async-done | bytes 786464 | tf_op jit(solution)/shard_map/all_to_all | solution.py:34
  46.0 0.4 copy.74
  46.5 5.5 %collective-permute-start.1 = (bf16[64,12,512]{2,0,1:T(8,128)(2,1)S(1)}, bf16[64,12,512]{2,0,1:T(8,128)(2,1)S(1)}, u32[]{:S(2)}, u32[]{:S(2)}) collective-permute-start(bf16[64,12,512]{2,0,1:T(8,128)(2,1)S(1)} %copy.74), channel_id=1, source_target_pairs={{0,4},{4,0},{1,5},{5,1},{2,6},{6,2},{3,7},{7,3},{8,12},{12,8},{9,1... | collective-permute-start | bytes 2359304 | tf_op jit(solution)/shard_map/ppermute | solution.py:28
  53.0 0.9 collective-permute-done.1
  54.7 0.8 pad_maximum_fusion.3
  55.5 4.4 %collective-permute-start.3 = (bf16[128,1920]{0,1:T(8,128)(2,1)}, bf16[128,1920]{0,1:T(8,128)(2,1)S(1)}, u32[]{:S(2)}, u32[]{:S(2)}) collective-permute-start(bf16[128,1920]{0,1:T(8,128)(2,1)} %pad_maximum_fusion.3), channel_id=1, source_target_pairs={{0,3},{1,0},{2,1},{3,2},{4,7},{5,4},{6,5},{7,6},{8,11},{9,8},{10,9... | collective-permute-start | bytes 1474568 | tf_op jit(solution)/shard_map/ppermute | solution.py:128
  59.9 1.9 collective-permute-start.2
  62.4 8.0 %collective-permute-done.3 = bf16[128,1920]{0,1:T(8,128)(2,1)S(1)} collective-permute-done((bf16[128,1920]{0,1:T(8,128)(2,1)}, bf16[128,1920]{0,1:T(8,128)(2,1)S(1)}, u32[]{:S(2)}, u32[]{:S(2)}) %collective-permute-start.3) | collective-permute-done | bytes 491552 | tf_op jit(solution)/shard_map/ppermute | solution.py:128
  70.6 5.2 %collective-permute-start.5 = (bf16[64,1920]{0,1:T(8,128)(2,1)S(1)}, bf16[64,1920]{0,1:T(8,128)(2,1)}, u32[]{:S(2)}, u32[]{:S(2)}) collective-permute-start(bf16[64,1920]{0,1:T(8,128)(2,1)S(1)} %slice.145), channel_id=1, source_target_pairs={{0,3},{1,0},{2,1},{3,2},{4,7},{5,4},{6,5},{7,6},{8,11},{9,8},{10,9... | collective-permute-start | bytes 737288 | tf_op jit(solution)/shard_map/ppermute | solution.py:133
  75.8 1.9 collective-permute-start.4
  78.1 7.1 %collective-permute-done.5 = bf16[64,1920]{0,1:T(8,128)(2,1)} collective-permute-done((bf16[64,1920]{0,1:T(8,128)(2,1)S(1)}, bf16[64,1920]{0,1:T(8,128)(2,1)}, u32[]{:S(2)}, u32[]{:S(2)}) %collective-permute-start.5) | collective-permute-done | bytes 245792 | tf_op jit(solution)/shard_map/ppermute | solution.py:133
  85.2 5.4 %collective-permute-done.4 = bf16[64,1920]{0,1:T(8,128)(2,1)} collective-permute-done((bf16[64,1920]{0,1:T(8,128)(2,1)}, bf16[64,1920]{0,1:T(8,128)(2,1)}, u32[]{:S(2)}, u32[]{:S(2)}) %collective-permute-start.4) | collective-permute-done | bytes 245792 | tf_op jit(solution)/shard_map/ppermute | solution.py:132
  90.5 1.6 convert_add_fusion
  92.1 1.2 multiply_reduce_fusion.2
  93.8 3.5 %scatter_custom_fusion = bf16[1536,384]{1,0:T(8,128)(2,1)} fusion(s32[512]{0:T(512)S(1)} %bitcast.121, bf16[512,384]{1,0:T(8,128)(2,1)S(1)} %reshape.229, bf16[]{:T(256)} %constant.94.clone.1), kind=kCustom, calls=%fused_computation.37 | custom fusion | bytes 1179650 | tf_op jit(solution)/shard_map/scatter | solution.py:171
  97.3 2.2 reshape_reshape.6
  99.7 4.3 %collective-permute-start.6 = (bf16[64,12,384]{2,0,1:T(8,128)(2,1)S(1)}, bf16[64,12,384]{2,0,1:T(8,128)(2,1)S(1)}, u32[]{:S(2)}, u32[]{:S(2)}) collective-permute-start(bf16[64,12,384]{2,0,1:T(8,128)(2,1)S(1)} %copy.81), channel_id=1, source_target_pairs={{0,4},{4,0},{1,5},{5,1},{2,6},{6,2},{3,7},{7,3},{8,12},{12,8},{9,1... | collective-permute-start | bytes 1769480 | tf_op jit(solution)/shard_map/ppermute | solution.py:28
  104.0 1.6 collective-permute-done.6
  105.6 0.5 fusion.9
  106.4 1.2 copy.84
  107.6 37.5 %all_to_all.15 = bf16[64,2,12,384]{3,1,2,0:T(2,128)(2,1)S(1)} all-to-all(bf16[64,2,12,384]{3,1,2,0:T(2,128)(2,1)S(1)} %copy.84), channel_id=1, replica_groups=mesh['yz'=64,'core'=2,'tp'=4] {'yz'}, dimensions={0} | all-to-all | bytes 2359296 | tf_op jit(solution)/shard_map/all_to_all | solution.py:44
  145.1 1.4 copy.85
  146.6 2.3 reshape_reshape.7
  148.9 1.9 collective-permute-start.7
  150.8 4.6 %collective-permute-start.8 = (bf16[1536,384]{1,0:T(8,128)(2,1)S(1)}, bf16[1536,384]{1,0:T(8,128)(2,1)S(1)}, u32[]{:S(2)}, u32[]{:S(2)}) collective-permute-start(bf16[1536,384]{1,0:T(8,128)(2,1)S(1)} %reshape_reshape.7), channel_id=1, source_target_pairs={{0,3},{1,0},{2,1},{3,2},{4,7},{5,4},{6,5},{7,6},{8,11},{9,8},{10,9... | collective-permute-start | bytes 3538952 | tf_op jit(solution)/shard_map/ppermute | solution.py:175
  155.4 1.9 fusion.71
  157.2 0.9 fusion.29
  158.1 0.9 fusion.23
  159.0 17.3 %collective-permute-done.7 = bf16[1536,384]{1,0:T(8,128)(2,1)S(1)} collective-permute-done((bf16[1536,384]{1,0:T(8,128)(2,1)S(1)}, bf16[1536,384]{1,0:T(8,128)(2,1)S(1)}, u32[]{:S(2)}, u32[]{:S(2)}) %collective-permute-start.7) | collective-permute-done | bytes 1179680 | tf_op jit(solution)/shard_map/ppermute | solution.py:174
  176.3 1.9 collective-permute-start.9
  178.3 4.6 %collective-permute-start.10 = (bf16[768,384]{1,0:T(8,128)(2,1)S(1)}, bf16[768,384]{1,0:T(8,128)(2,1)S(1)}, u32[]{:S(2)}, u32[]{:S(2)}) collective-permute-start(bf16[768,384]{1,0:T(8,128)(2,1)S(1)} %slice.153), channel_id=1, source_target_pairs={{0,3},{1,0},{2,1},{3,2},{4,7},{5,4},{6,5},{7,6},{8,11},{9,8},{10,9... | collective-permute-start | bytes 1769480 | tf_op jit(solution)/shard_map/ppermute | solution.py:177
  182.9 0.9 convolution_add_fusion.3
  183.8 0.9 convolution_add_fusion.1
  184.8 5.5 %collective-permute-done.9 = bf16[768,384]{1,0:T(8,128)(2,1)S(1)} collective-permute-done((bf16[768,384]{1,0:T(8,128)(2,1)S(1)}, bf16[768,384]{1,0:T(8,128)(2,1)S(1)}, u32[]{:S(2)}, u32[]{:S(2)}) %collective-permute-start.9) | collective-permute-done | bytes 589856 | tf_op jit(solution)/shard_map/ppermute | solution.py:176
  190.3 0.9 collective-permute-done.10
  191.3 0.9 fusion.19
  192.2 0.9 fusion.25
  193.1 1.0 fusion
  194.1 1.4 fusion.5
  195.5 0.9 convolution_convert_fusion.1
  196.5 1.9 collective-permute-start.11
  198.4 5.5 %collective-permute-start.13 = (bf16[768,384]{1,0:T(8,128)(2,1)S(1)}, bf16[768,384]{1,0:T(8,128)(2,1)S(1)}, u32[]{:S(2)}, u32[]{:S(2)}) collective-permute-start(bf16[768,384]{1,0:T(8,128)(2,1)S(1)} %get-tuple-element.14), channel_id=1, source_target_pairs={{0,3},{1,0},{2,1},{3,2},{4,7},{5,4},{6,5},{7,6},{8,11},{9,8},{10,9... | collective-permute-start | bytes 1769480 | tf_op jit(solution)/shard_map/ppermute | solution.py:202
  204.0 0.9 convolution_convert_fusion.2
  204.9 0.9 convolution_convert_fusion
  205.9 4.4 %collective-permute-done.11 = bf16[768,384]{1,0:T(8,128)(2,1)S(1)} collective-permute-done((bf16[768,384]{1,0:T(8,128)(2,1)S(1)}, bf16[768,384]{1,0:T(8,128)(2,1)S(1)}, u32[]{:S(2)}, u32[]{:S(2)}) %collective-permute-start.11) | collective-permute-done | bytes 589856 | tf_op jit(solution)/shard_map/ppermute | solution.py:201
  210.6 1.9 collective-permute-start.12
  212.9 4.6 %collective-permute-start.14 = (bf16[1536,384]{1,0:T(8,128)(2,1)S(1)}, bf16[1536,384]{1,0:T(8,128)(2,1)S(1)}, u32[]{:S(2)}, u32[]{:S(2)}) collective-permute-start(bf16[1536,384]{1,0:T(8,128)(2,1)S(1)} %pad_maximum_fusion.2), channel_id=1, source_target_pairs={{0,3},{1,0},{2,1},{3,2},{4,7},{5,4},{6,5},{7,6},{8,11},{9,8},{10,9... | collective-permute-start | bytes 3538952 | tf_op jit(solution)/shard_map/ppermute | solution.py:212
  217.4 0.9 fusion.6
  218.3 17.2 %collective-permute-done.12 = bf16[1536,384]{1,0:T(8,128)(2,1)S(1)} collective-permute-done((bf16[1536,384]{1,0:T(8,128)(2,1)S(1)}, bf16[1536,384]{1,0:T(8,128)(2,1)S(1)}, u32[]{:S(2)}, u32[]{:S(2)}) %collective-permute-start.12) | collective-permute-done | bytes 1179680 | tf_op jit(solution)/shard_map/ppermute | solution.py:211
  235.5 1.2 collective-permute-done.14
  237.1 1.3 reshape.210
  238.4 25.2 %all-to-all-start.2 = ((bf16[128,12,384]{2,1,0:T(8,128)(2,1)}), bf16[128,12,384]{2,1,0:T(8,128)(2,1)}, u32[]{:S(2)}, u32[]{:S(2)}) async-start(bf16[128,12,384]{2,1,0:T(8,128)(2,1)} %reshape.210), calls=%async_computation.2 | async-start | bytes 3145728 | tf_op jit(solution)/shard_map/all_to_all | solution.py:219
  263.7 0.6 slice_bitcast_fusion.3
  264.3 40.2 %all-to-all-done.2 = bf16[128,12,384]{2,1,0:T(8,128)(2,1)} async-done(((bf16[128,12,384]{2,1,0:T(8,128)(2,1)}), bf16[128,12,384]{2,1,0:T(8,128)(2,1)}, u32[]{:S(2)}, u32[]{:S(2)}) %all-to-all-start.2) | async-done | bytes 1179680 | tf_op jit(solution)/shard_map/all_to_all | solution.py:219
  304.5 2.3 reshape.211
  306.7 1.9 gather_fusion
  308.8 0.6 fusion.73
  310.2 0.8 copy.90
  (86 shorter events, 6.8 us)
Async XLA Ops:
  0.0 195.5 %copy-start = (bf16[1,384,1536]{2,1,0:T(8,128)(2,1)S(1)}, bf16[1,384,1536]{2,1,0:T(8,128)(2,1)}, u32[]{:S(2)}) copy-start(bf16[1,384,1536]{2,1,0:T(8,128)(2,1)} %param.17) | copy-start | bytes 3538948
  1.9 17.3 %copy-start.9 = (bf16[128,1,128]{2,0,1:T(8,128)(2,1)S(1)}, bf16[128,1,128]{2,0,1:T(8,128)(2,1)}, u32[]{:S(2)}) copy-start(bf16[128,1,128]{2,0,1:T(8,128)(2,1)} %param.12) | copy-start | bytes 98308
  1.9 21.7 %copy-start.5 = (bf16[128,512]{1,0:T(8,128)(2,1)S(1)}, bf16[128,512]{1,0:T(8,128)(2,1)}, u32[]{:S(2)}) copy-start(bf16[128,512]{1,0:T(8,128)(2,1)} %param.11) | copy-start | bytes 393220
  1.9 21.8 %copy-start.6 = (bf16[128,384]{1,0:T(8,128)(2,1)S(1)}, bf16[128,384]{1,0:T(8,128)(2,1)}, u32[]{:S(2)}) copy-start(bf16[128,384]{1,0:T(8,128)(2,1)} %param.10) | copy-start | bytes 294916
  1.9 44.1 %all-to-all-start = ((bf16[64,12,512]{2,1,0:T(8,128)(2,1)}), bf16[64,12,512]{2,1,0:T(8,128)(2,1)S(1)}, u32[]{:S(2)}, u32[]{:S(2)}) async-start(bf16[64,12,512]{2,1,0:T(8,128)(2,1)} %broadcast_in_dim.21), calls=%async_computation | async-start | bytes 2097152 | tf_op jit(solution)/shard_map/all_to_all | solution.py:34
  19.2 11.1 %copy-start.13 = (f32[8]{0:T(128)S(1)}, f32[8]{0:T(128)}, u32[]{:S(2)}) copy-start(f32[8]{0:T(128)} %param.13) | copy-start | bytes 100
  19.3 9.3 %copy-start.3 = (bf16[128,1,128]{0,2,1:T(8,128)(2,1)}, bf16[128,1,128]{0,2,1:T(8,128)(2,1)S(1)}, u32[]{:S(2)}) copy-start(bf16[128,1,128]{0,2,1:T(8,128)(2,1)S(1)} %copy.69) | copy-start | bytes 98308
  19.3 9.3 %collective-permute-start = (bf16[128,1,128]{0,2,1:T(8,128)(2,1)S(1)}, bf16[128,1,128]{0,2,1:T(8,128)(2,1)S(1)}, u32[]{:S(2)}, u32[]{:S(2)}) collective-permute-start(bf16[128,1,128]{0,2,1:T(8,128)(2,1)S(1)} %copy.69), channel_id=1, source_target_pairs={{0,4},{4,8},{8,12},{12,16},{16,20},{20,24},{24,28},{28,32},{32,36}... | collective-permute-start | bytes 98312 | tf_op jit(solution)/shard_map/ppermute | solution.py:19
  23.8 69.4 %copy-start.1 = (bf16[128,384]{0,1:T(8,128)(2,1)}, bf16[128,384]{0,1:T(8,128)(2,1)S(1)}, u32[]{:S(2)}) copy-start(bf16[128,384]{0,1:T(8,128)(2,1)S(1)} %copy.68) | copy-start | bytes 294916
  28.6 0.6 copy-start.7
  30.4 21.9 %copy-start.4 = (bf16[128,1,128]{0,2,1:T(8,128)(2,1)S(1)}, bf16[128,1,128]{0,2,1:T(8,128)(2,1)}, u32[]{:S(2)}) copy-start(bf16[128,1,128]{0,2,1:T(8,128)(2,1)} %copy-done.3) | copy-start | bytes 98308
  30.4 21.9 %copy-start.8 = (bf16[128,1,128]{0,2,1:T(8,128)(2,1)S(1)}, bf16[128,1,128]{0,2,1:T(8,128)(2,1)}, u32[]{:S(2)}) copy-start(bf16[128,1,128]{0,2,1:T(8,128)(2,1)} %copy-done.7) | copy-start | bytes 98308
  46.5 7.4 %collective-permute-start.1 = (bf16[64,12,512]{2,0,1:T(8,128)(2,1)S(1)}, bf16[64,12,512]{2,0,1:T(8,128)(2,1)S(1)}, u32[]{:S(2)}, u32[]{:S(2)}) collective-permute-start(bf16[64,12,512]{2,0,1:T(8,128)(2,1)S(1)} %copy.74), channel_id=1, source_target_pairs={{0,4},{4,0},{1,5},{5,1},{2,6},{6,2},{3,7},{7,3},{8,12},{12,8},{9,1... | collective-permute-start | bytes 2359304 | tf_op jit(solution)/shard_map/ppermute | solution.py:28
  54.6 7.3 %copy-start.10 = (s32[128,4]{0,1:T(4,128)S(1)}, s32[128,4]{0,1:T(4,128)}, u32[]{:S(2)}) copy-start(s32[128,4]{0,1:T(4,128)} %param.18) | copy-start | bytes 6148
  55.5 14.9 %collective-permute-start.3 = (bf16[128,1920]{0,1:T(8,128)(2,1)}, bf16[128,1920]{0,1:T(8,128)(2,1)S(1)}, u32[]{:S(2)}, u32[]{:S(2)}) collective-permute-start(bf16[128,1920]{0,1:T(8,128)(2,1)} %pad_maximum_fusion.3), channel_id=1, source_target_pairs={{0,3},{1,0},{2,1},{3,2},{4,7},{5,4},{6,5},{7,6},{8,11},{9,8},{10,9... | collective-permute-start | bytes 1474568 | tf_op jit(solution)/shard_map/ppermute | solution.py:128
  59.9 15.9 %collective-permute-start.2 = (bf16[128,1920]{0,1:T(8,128)(2,1)}, bf16[128,1920]{0,1:T(8,128)(2,1)}, u32[]{:S(2)}, u32[]{:S(2)}) collective-permute-start(bf16[128,1920]{0,1:T(8,128)(2,1)} %pad_maximum_fusion.3), channel_id=1, source_target_pairs={{0,1},{1,2},{2,3},{3,0},{4,5},{5,6},{6,7},{7,4},{8,9},{9,10},{10,1... | collective-permute-start | bytes 1474568 | tf_op jit(solution)/shard_map/ppermute | solution.py:127
  70.6 14.6 %collective-permute-start.5 = (bf16[64,1920]{0,1:T(8,128)(2,1)S(1)}, bf16[64,1920]{0,1:T(8,128)(2,1)}, u32[]{:S(2)}, u32[]{:S(2)}) collective-permute-start(bf16[64,1920]{0,1:T(8,128)(2,1)S(1)} %slice.145), channel_id=1, source_target_pairs={{0,3},{1,0},{2,1},{3,2},{4,7},{5,4},{6,5},{7,6},{8,11},{9,8},{10,9... | collective-permute-start | bytes 737288 | tf_op jit(solution)/shard_map/ppermute | solution.py:133
  75.8 14.7 %collective-permute-start.4 = (bf16[64,1920]{0,1:T(8,128)(2,1)}, bf16[64,1920]{0,1:T(8,128)(2,1)}, u32[]{:S(2)}, u32[]{:S(2)}) collective-permute-start(bf16[64,1920]{0,1:T(8,128)(2,1)} %bitcast.116), channel_id=1, source_target_pairs={{0,1},{1,2},{2,3},{3,0},{4,5},{5,6},{6,7},{7,4},{8,9},{9,10},{10,1... | collective-permute-start | bytes 737288 | tf_op jit(solution)/shard_map/ppermute | solution.py:132
  92.1 1.2 copy-start.12
  99.7 5.9 %collective-permute-start.6 = (bf16[64,12,384]{2,0,1:T(8,128)(2,1)S(1)}, bf16[64,12,384]{2,0,1:T(8,128)(2,1)S(1)}, u32[]{:S(2)}, u32[]{:S(2)}) collective-permute-start(bf16[64,12,384]{2,0,1:T(8,128)(2,1)S(1)} %copy.81), channel_id=1, source_target_pairs={{0,4},{4,0},{1,5},{5,1},{2,6},{6,2},{3,7},{7,3},{8,12},{12,8},{9,1... | collective-permute-start | bytes 1769480 | tf_op jit(solution)/shard_map/ppermute | solution.py:28
  148.9 27.4 %collective-permute-start.7 = (bf16[1536,384]{1,0:T(8,128)(2,1)S(1)}, bf16[1536,384]{1,0:T(8,128)(2,1)S(1)}, u32[]{:S(2)}, u32[]{:S(2)}) collective-permute-start(bf16[1536,384]{1,0:T(8,128)(2,1)S(1)} %reshape_reshape.7), channel_id=1, source_target_pairs={{0,1},{1,2},{2,3},{3,0},{4,5},{5,6},{6,7},{7,4},{8,9},{9,10},{10,1... | collective-permute-start | bytes 3538952 | tf_op jit(solution)/shard_map/ppermute | solution.py:174
  150.8 27.5 %collective-permute-start.8 = (bf16[1536,384]{1,0:T(8,128)(2,1)S(1)}, bf16[1536,384]{1,0:T(8,128)(2,1)S(1)}, u32[]{:S(2)}, u32[]{:S(2)}) collective-permute-start(bf16[1536,384]{1,0:T(8,128)(2,1)S(1)} %reshape_reshape.7), channel_id=1, source_target_pairs={{0,3},{1,0},{2,1},{3,2},{4,7},{5,4},{6,5},{7,6},{8,11},{9,8},{10,9... | collective-permute-start | bytes 3538952 | tf_op jit(solution)/shard_map/ppermute | solution.py:175
  176.3 13.9 %collective-permute-start.9 = (bf16[768,384]{1,0:T(8,128)(2,1)S(1)}, bf16[768,384]{1,0:T(8,128)(2,1)S(1)}, u32[]{:S(2)}, u32[]{:S(2)}) collective-permute-start(bf16[768,384]{1,0:T(8,128)(2,1)S(1)} %slice.152), channel_id=1, source_target_pairs={{0,1},{1,2},{2,3},{3,0},{4,5},{5,6},{6,7},{7,4},{8,9},{9,10},{10,1... | collective-permute-start | bytes 1769480 | tf_op jit(solution)/shard_map/ppermute | solution.py:176
  178.3 12.9 %collective-permute-start.10 = (bf16[768,384]{1,0:T(8,128)(2,1)S(1)}, bf16[768,384]{1,0:T(8,128)(2,1)S(1)}, u32[]{:S(2)}, u32[]{:S(2)}) collective-permute-start(bf16[768,384]{1,0:T(8,128)(2,1)S(1)} %slice.153), channel_id=1, source_target_pairs={{0,3},{1,0},{2,1},{3,2},{4,7},{5,4},{6,5},{7,6},{8,11},{9,8},{10,9... | collective-permute-start | bytes 1769480 | tf_op jit(solution)/shard_map/ppermute | solution.py:177
  196.5 13.8 %collective-permute-start.11 = (bf16[768,384]{1,0:T(8,128)(2,1)S(1)}, bf16[768,384]{1,0:T(8,128)(2,1)S(1)}, u32[]{:S(2)}, u32[]{:S(2)}) collective-permute-start(bf16[768,384]{1,0:T(8,128)(2,1)S(1)} %get-tuple-element.13), channel_id=1, source_target_pairs={{0,1},{1,2},{2,3},{3,0},{4,5},{5,6},{6,7},{7,4},{8,9},{9,10},{10,1... | collective-permute-start | bytes 1769480 | tf_op jit(solution)/shard_map/ppermute | solution.py:201
  198.4 14.1 %collective-permute-start.13 = (bf16[768,384]{1,0:T(8,128)(2,1)S(1)}, bf16[768,384]{1,0:T(8,128)(2,1)S(1)}, u32[]{:S(2)}, u32[]{:S(2)}) collective-permute-start(bf16[768,384]{1,0:T(8,128)(2,1)S(1)} %get-tuple-element.14), channel_id=1, source_target_pairs={{0,3},{1,0},{2,1},{3,2},{4,7},{5,4},{6,5},{7,6},{8,11},{9,8},{10,9... | collective-permute-start | bytes 1769480 | tf_op jit(solution)/shard_map/ppermute | solution.py:202
  210.6 24.9 %collective-permute-start.12 = (bf16[1536,384]{1,0:T(8,128)(2,1)S(1)}, bf16[1536,384]{1,0:T(8,128)(2,1)S(1)}, u32[]{:S(2)}, u32[]{:S(2)}) collective-permute-start(bf16[1536,384]{1,0:T(8,128)(2,1)S(1)} %pad_maximum_fusion.1), channel_id=1, source_target_pairs={{0,1},{1,2},{2,3},{3,0},{4,5},{5,6},{6,7},{7,4},{8,9},{9,10},{10,1... | collective-permute-start | bytes 3538952 | tf_op jit(solution)/shard_map/ppermute | solution.py:211
  212.9 23.8 %collective-permute-start.14 = (bf16[1536,384]{1,0:T(8,128)(2,1)S(1)}, bf16[1536,384]{1,0:T(8,128)(2,1)S(1)}, u32[]{:S(2)}, u32[]{:S(2)}) collective-permute-start(bf16[1536,384]{1,0:T(8,128)(2,1)S(1)} %pad_maximum_fusion.2), channel_id=1, source_target_pairs={{0,3},{1,0},{2,1},{3,2},{4,7},{5,4},{6,5},{7,6},{8,11},{9,8},{10,9... | collective-permute-start | bytes 3538952 | tf_op jit(solution)/shard_map/ppermute | solution.py:212
  238.4 25.2 %copy-start.11 = (f32[128,4]{0,1:T(4,128)S(1)}, f32[128,4]{0,1:T(4,128)}, u32[]{:S(2)}) copy-start(f32[128,4]{0,1:T(4,128)} %param.19) | copy-start | bytes 6148
  238.4 66.1 %all-to-all-start.2 = ((bf16[128,12,384]{2,1,0:T(8,128)(2,1)}), bf16[128,12,384]{2,1,0:T(8,128)(2,1)}, u32[]{:S(2)}, u32[]{:S(2)}) async-start(bf16[128,12,384]{2,1,0:T(8,128)(2,1)} %reshape.210), calls=%async_computation.2 | async-start | bytes 3145728 | tf_op jit(solution)/shard_map/all_to_all | solution.py:219
  308.8 1.3 copy-start.2
  308.8 1.3 copy-start.14

commit v9 on v6

--- a/solution.py
+++ b/solution.py
@@ -37,9 +37,9 @@
 
 def to_experts(outbox):
     parts = outbox.reshape((lax.axis_size("yz"), 2) + outbox.shape[1:])
-    first = lax.axis_index("core") == 0
-    mine = jnp.where(first, parts[:, 0], parts[:, 1])
-    theirs = jnp.where(first, parts[:, 1], parts[:, 0])
+    core = lax.axis_index("core")
+    mine = lax.dynamic_index_in_dim(parts, core, 1, keepdims=False)
+    theirs = lax.dynamic_index_in_dim(parts, 1 - core, 1, keepdims=False)
     staged = by_core(mine, other_core(theirs))
     return lax.all_to_all(staged, "yz", 0, 0, tiled=True).reshape(outbox.shape)
 

time: 305 us -> 305 us (level)
  no operation moved by 1% of the time
where the time goes in v9:
time: 305 us; the launch traced here: 303 us
  waiting for transfers between devices  124 us (41%)
  starting transfers between devices  96.5 us (32%)
  blocking collectives  36.1 us (12%)
  local copies, waits for them, and re-layouts  26.9 us (9%)
  matrix products  14 us (5%)
  other arithmetic  4.53 us (1%)
    all_to_all x1, waiting for transfers between devices, body(): lax.all_to_all(result, CTX, 0, 0, tiled=True).reshape(-1, quarter_w)  40.3 us
    all_to_all x1, blocking collectives, to_experts(): return lax.all_to_all(staged, 'yz', 0, 0, tiled=True).reshape(outbox.shape)  36.1 us
    all_to_all x1, starting transfers between devices, body(): lax.all_to_all(result, CTX, 0, 0, tiled=True).reshape(-1, quarter_w)  24.9 us
    ppermute x1, waiting for transfers between devices, body(): from_behind = lax.ppermute(arrived, 'tp', ahead)  17.6 us
    ppermute x1, waiting for transfers between devices, body(): got_behind = lax.ppermute(for_ahead, 'tp', ahead)  17.4 us
    all_to_all x1, starting transfers between devices, gathered_columns(): mine = lax.all_to_all(spread, 'yz', 0, 0, tiled=True)  17.3 us
    all_to_all x1, waiting for transfers between devices, gathered_columns(): mine = lax.all_to_all(spread, 'yz', 0, 0, tiled=True)  17.2 us
    ppermute x2, starting transfers between devices, other_core(): return lax.ppermute(value, 'core', [(0, 1), (1, 0)])  9.66 us
  transfers between devices with their start and end apart: 17, of which 13 were waited for; matrix products, arithmetic and copies ran while one was open for 4% of the time, Pallas kernels for 0%

profile of v9, /device:TPU:1, one launch (start us, length us, event | category | flops | bytes accessed | tf_op | source)
XLA Modules:
  0.0 302.7 jit_solution(14978101984494247266)
XLA Ops:
  0.0 1.9 broadcast_in_dim.21
  1.9 17.3 %all-to-all-start = ((bf16[64,12,512]{2,1,0:T(8,128)(2,1)}), bf16[64,12,512]{2,1,0:T(8,128)(2,1)S(1)}, u32[]{:S(2)}, u32[]{:S(2)}) async-start(bf16[64,12,512]{2,1,0:T(8,128)(2,1)} %broadcast_in_dim.21), calls=%async_computation | async-start | bytes 2097152 | tf_op jit(solution)/shard_map/all_to_all | solution.py:34
  19.3 4.0 %collective-permute-start = (bf16[128,1,128]{0,2,1:T(8,128)(2,1)S(1)}, bf16[128,1,128]{0,2,1:T(8,128)(2,1)S(1)}, u32[]{:S(2)}, u32[]{:S(2)}) collective-permute-start(bf16[128,1,128]{0,2,1:T(8,128)(2,1)S(1)} %copy.74), channel_id=1, source_target_pairs={{0,4},{4,8},{8,12},{12,16},{16,20},{20,24},{24,28},{28,32},{32,36}... | collective-permute-start | bytes 98312 | tf_op jit(solution)/shard_map/ppermute | solution.py:19
  23.7 4.8 %collective-permute-done = bf16[128,1,128]{0,2,1:T(8,128)(2,1)S(1)} collective-permute-done((bf16[128,1,128]{0,2,1:T(8,128)(2,1)S(1)}, bf16[128,1,128]{0,2,1:T(8,128)(2,1)S(1)}, u32[]{:S(2)}, u32[]{:S(2)}) %collective-permute-start) | collective-permute-done | bytes 32800 | tf_op jit(solution)/shard_map/ppermute | solution.py:19
  28.9 17.2 %all-to-all-done = bf16[64,12,512]{2,1,0:T(8,128)(2,1)S(1)} async-done(((bf16[64,12,512]{2,1,0:T(8,128)(2,1)}), bf16[64,12,512]{2,1,0:T(8,128)(2,1)S(1)}, u32[]{:S(2)}, u32[]{:S(2)}) %all-to-all-start) | async-done | bytes 786464 | tf_op jit(solution)/shard_map/all_to_all | solution.py:34
  46.0 0.4 copy.78
  46.4 5.5 %collective-permute-start.1 = (bf16[64,12,512]{2,0,1:T(8,128)(2,1)S(1)}, bf16[64,12,512]{2,0,1:T(8,128)(2,1)S(1)}, u32[]{:S(2)}, u32[]{:S(2)}) collective-permute-start(bf16[64,12,512]{2,0,1:T(8,128)(2,1)S(1)} %copy.78), channel_id=1, source_target_pairs={{0,4},{4,0},{1,5},{5,1},{2,6},{6,2},{3,7},{7,3},{8,12},{12,8},{9,1... | collective-permute-start | bytes 2359304 | tf_op jit(solution)/shard_map/ppermute | solution.py:28
  52.7 1.2 collective-permute-done.1
  53.9 0.5 fusion.8
  54.9 1.3 reshape.205
  56.2 2.1 convolution_convert_fusion.4
  58.4 3.1 %collective-permute-start.2 = (bf16[128,1920]{1,0:T(8,128)(2,1)S(1)}, bf16[128,1920]{1,0:T(8,128)(2,1)S(1)}, u32[]{:S(2)}, u32[]{:S(2)}) collective-permute-start(bf16[128,1920]{1,0:T(8,128)(2,1)S(1)} %pad_maximum_fusion.4), channel_id=1, source_target_pairs={{0,1},{1,2},{2,3},{3,0},{4,5},{5,6},{6,7},{7,4},{8,9},{9,10},{10,1... | collective-permute-start | bytes 1474568 | tf_op jit(solution)/shard_map/ppermute | solution.py:125
  61.5 3.4 %collective-permute-start.3 = (bf16[128,1920]{1,0:T(8,128)(2,1)S(1)}, bf16[128,1920]{1,0:T(8,128)(2,1)S(1)}, u32[]{:S(2)}, u32[]{:S(2)}) collective-permute-start(bf16[128,1920]{1,0:T(8,128)(2,1)S(1)} %pad_maximum_fusion.4), channel_id=1, source_target_pairs={{0,3},{1,0},{2,1},{3,2},{4,7},{5,4},{6,5},{7,6},{8,11},{9,8},{10,9... | collective-permute-start | bytes 1474568 | tf_op jit(solution)/shard_map/ppermute | solution.py:126
  65.5 8.4 %collective-permute-done.2 = bf16[128,1920]{1,0:T(8,128)(2,1)S(1)} collective-permute-done((bf16[128,1920]{1,0:T(8,128)(2,1)S(1)}, bf16[128,1920]{1,0:T(8,128)(2,1)S(1)}, u32[]{:S(2)}, u32[]{:S(2)}) %collective-permute-start.2) | collective-permute-done | bytes 491552 | tf_op jit(solution)/shard_map/ppermute | solution.py:125
  73.9 0.7 slice.134
  74.6 1.9 collective-permute-start.4
  76.8 4.6 %collective-permute-start.5 = (bf16[64,1920]{1,0:T(8,128)(2,1)S(1)}, bf16[64,1920]{1,0:T(8,128)(2,1)S(1)}, u32[]{:S(2)}, u32[]{:S(2)}) collective-permute-start(bf16[64,1920]{1,0:T(8,128)(2,1)S(1)} %slice.135), channel_id=1, source_target_pairs={{0,3},{1,0},{2,1},{3,2},{4,7},{5,4},{6,5},{7,6},{8,11},{9,8},{10,9... | collective-permute-start | bytes 737288 | tf_op jit(solution)/shard_map/ppermute | solution.py:131
  81.4 2.9 collective-permute-done.4
  84.3 1.0 constant_dynamic-update-slice_fusion.1
  85.7 0.5 copy-done.7
  86.5 3.5 %scatter_custom_fusion = bf16[1536,384]{1,0:T(8,128)(2,1)} fusion(s32[512]{0:T(512)S(1)} %bitcast.126, bf16[512,384]{1,0:T(8,128)(2,1)S(1)} %reshape.227, bf16[]{:T(256)} %constant.101.clone.1), kind=kCustom, calls=%fused_computation.42 | custom fusion | bytes 1179650 | tf_op jit(solution)/shard_map/scatter | solution.py:169
  90.0 2.2 reshape_reshape.6
  92.5 4.1 %collective-permute-start.6 = (bf16[64,12,384]{2,0,1:T(8,128)(2,1)S(1)}, bf16[64,12,384]{2,0,1:T(8,128)(2,1)S(1)}, u32[]{:S(2)}, u32[]{:S(2)}) collective-permute-start(bf16[64,12,384]{2,0,1:T(8,128)(2,1)S(1)} %bitcast.122), channel_id=1, source_target_pairs={{0,4},{4,0},{1,5},{5,1},{2,6},{6,2},{3,7},{7,3},{8,12},{12,8},{9,1... | collective-permute-start | bytes 1769480 | tf_op jit(solution)/shard_map/ppermute | solution.py:28
  96.6 1.6 collective-permute-done.6
  98.6 1.2 copy.85
  99.8 36.1 %all_to_all.15 = bf16[64,2,12,384]{3,1,2,0:T(2,128)(2,1)S(1)} all-to-all(bf16[64,2,12,384]{3,1,2,0:T(2,128)(2,1)S(1)} %copy.85), channel_id=1, replica_groups=mesh['yz'=64,'core'=2,'tp'=4] {'yz'}, dimensions={0} | all-to-all | bytes 2359296 | tf_op jit(solution)/shard_map/all_to_all | solution.py:44
  135.9 1.4 copy.86
  137.3 2.3 reshape_reshape.7
  139.6 2.6 collective-permute-start.7
  142.2 4.6 %collective-permute-start.8 = (bf16[1536,384]{1,0:T(8,128)(2,1)S(1)}, bf16[1536,384]{1,0:T(8,128)(2,1)S(1)}, u32[]{:S(2)}, u32[]{:S(2)}) collective-permute-start(bf16[1536,384]{1,0:T(8,128)(2,1)S(1)} %reshape_reshape.7), channel_id=1, source_target_pairs={{0,3},{1,0},{2,1},{3,2},{4,7},{5,4},{6,5},{7,6},{8,11},{9,8},{10,9... | collective-permute-start | bytes 3538952 | tf_op jit(solution)/shard_map/ppermute | solution.py:173
  146.9 1.9 fusion.70
  148.7 0.9 fusion.30
  149.6 0.9 fusion.24
  150.5 17.6 %collective-permute-done.7 = bf16[1536,384]{1,0:T(8,128)(2,1)S(1)} collective-permute-done((bf16[1536,384]{1,0:T(8,128)(2,1)S(1)}, bf16[1536,384]{1,0:T(8,128)(2,1)S(1)}, u32[]{:S(2)}, u32[]{:S(2)}) %collective-permute-start.7) | collective-permute-done | bytes 1179680 | tf_op jit(solution)/shard_map/ppermute | solution.py:172
  168.1 1.9 collective-permute-start.9
  170.1 4.6 %collective-permute-start.10 = (bf16[768,384]{1,0:T(8,128)(2,1)S(1)}, bf16[768,384]{1,0:T(8,128)(2,1)S(1)}, u32[]{:S(2)}, u32[]{:S(2)}) collective-permute-start(bf16[768,384]{1,0:T(8,128)(2,1)S(1)} %slice.141), channel_id=1, source_target_pairs={{0,3},{1,0},{2,1},{3,2},{4,7},{5,4},{6,5},{7,6},{8,11},{9,8},{10,9... | collective-permute-start | bytes 1769480 | tf_op jit(solution)/shard_map/ppermute | solution.py:175
  174.7 0.9 convolution_add_fusion.3
  175.6 0.9 convolution_add_fusion.1
  176.6 5.8 %collective-permute-done.9 = bf16[768,384]{1,0:T(8,128)(2,1)S(1)} collective-permute-done((bf16[768,384]{1,0:T(8,128)(2,1)S(1)}, bf16[768,384]{1,0:T(8,128)(2,1)S(1)}, u32[]{:S(2)}, u32[]{:S(2)}) %collective-permute-start.9) | collective-permute-done | bytes 589856 | tf_op jit(solution)/shard_map/ppermute | solution.py:174
  182.4 0.9 collective-permute-done.10
  183.4 0.9 fusion.20
  184.3 0.9 fusion.26
  185.2 1.0 fusion
  186.2 1.4 fusion.5
  187.6 0.9 convolution_convert_fusion.1
  188.6 2.0 collective-permute-start.11
  190.6 5.4 %collective-permute-start.13 = (bf16[768,384]{1,0:T(8,128)(2,1)S(1)}, bf16[768,384]{1,0:T(8,128)(2,1)S(1)}, u32[]{:S(2)}, u32[]{:S(2)}) collective-permute-start(bf16[768,384]{1,0:T(8,128)(2,1)S(1)} %get-tuple-element.18), channel_id=1, source_target_pairs={{0,3},{1,0},{2,1},{3,2},{4,7},{5,4},{6,5},{7,6},{8,11},{9,8},{10,9... | collective-permute-start | bytes 1769480 | tf_op jit(solution)/shard_map/ppermute | solution.py:200
  196.1 0.9 convolution_convert_fusion.2
  196.9 0.9 convolution_convert_fusion
  198.0 4.7 %collective-permute-done.11 = bf16[768,384]{1,0:T(8,128)(2,1)S(1)} collective-permute-done((bf16[768,384]{1,0:T(8,128)(2,1)S(1)}, bf16[768,384]{1,0:T(8,128)(2,1)S(1)}, u32[]{:S(2)}, u32[]{:S(2)}) %collective-permute-start.11) | collective-permute-done | bytes 589856 | tf_op jit(solution)/shard_map/ppermute | solution.py:199
  203.0 1.9 collective-permute-start.12
  205.2 4.6 %collective-permute-start.14 = (bf16[1536,384]{1,0:T(8,128)(2,1)S(1)}, bf16[1536,384]{1,0:T(8,128)(2,1)S(1)}, u32[]{:S(2)}, u32[]{:S(2)}) collective-permute-start(bf16[1536,384]{1,0:T(8,128)(2,1)S(1)} %pad_maximum_fusion.3), channel_id=1, source_target_pairs={{0,3},{1,0},{2,1},{3,2},{4,7},{5,4},{6,5},{7,6},{8,11},{9,8},{10,9... | collective-permute-start | bytes 3538952 | tf_op jit(solution)/shard_map/ppermute | solution.py:210
  209.8 0.9 fusion.6
  210.7 17.4 %collective-permute-done.12 = bf16[1536,384]{1,0:T(8,128)(2,1)S(1)} collective-permute-done((bf16[1536,384]{1,0:T(8,128)(2,1)S(1)}, bf16[1536,384]{1,0:T(8,128)(2,1)S(1)}, u32[]{:S(2)}, u32[]{:S(2)}) %collective-permute-start.12) | collective-permute-done | bytes 1179680 | tf_op jit(solution)/shard_map/ppermute | solution.py:209
  228.1 1.2 collective-permute-done.14
  229.3 0.4 add_convert_fusion
  229.7 1.3 reshape.208
  231.0 24.9 %all-to-all-start.2 = ((bf16[128,12,384]{2,1,0:T(8,128)(2,1)}), bf16[128,12,384]{2,1,0:T(8,128)(2,1)}, u32[]{:S(2)}, u32[]{:S(2)}) async-start(bf16[128,12,384]{2,1,0:T(8,128)(2,1)} %reshape.208), calls=%async_computation.2 | async-start | bytes 3145728 | tf_op jit(solution)/shard_map/all_to_all | solution.py:217
  256.0 0.5 slice_bitcast_fusion.3
  256.5 40.3 %all-to-all-done.2 = bf16[128,12,384]{2,1,0:T(8,128)(2,1)} async-done(((bf16[128,12,384]{2,1,0:T(8,128)(2,1)}), bf16[128,12,384]{2,1,0:T(8,128)(2,1)}, u32[]{:S(2)}, u32[]{:S(2)}) %all-to-all-start.2) | async-done | bytes 1179680 | tf_op jit(solution)/shard_map/all_to_all | solution.py:217
  296.8 2.3 reshape.209
  299.0 1.9 gather_fusion
  301.1 0.6 fusion.72
  301.9 0.8 fusion.46
  (72 shorter events, 5.5 us)
Async XLA Ops:
  0.0 187.6 %copy-start = (bf16[1,384,1536]{2,1,0:T(8,128)(2,1)S(1)}, bf16[1,384,1536]{2,1,0:T(8,128)(2,1)}, u32[]{:S(2)}) copy-start(bf16[1,384,1536]{2,1,0:T(8,128)(2,1)} %param.17) | copy-start | bytes 3538948
  1.9 17.3 %copy-start.4 = (bf16[128,1,128]{2,0,1:T(8,128)(2,1)S(1)}, bf16[128,1,128]{2,0,1:T(8,128)(2,1)}, u32[]{:S(2)}) copy-start(bf16[128,1,128]{2,0,1:T(8,128)(2,1)} %param.12) | copy-start | bytes 98308
  1.9 21.6 %copy-start.3 = (bf16[128,512]{1,0:T(8,128)(2,1)S(1)}, bf16[128,512]{1,0:T(8,128)(2,1)}, u32[]{:S(2)}) copy-start(bf16[128,512]{1,0:T(8,128)(2,1)} %param.11) | copy-start | bytes 393220
  1.9 44.1 %all-to-all-start = ((bf16[64,12,512]{2,1,0:T(8,128)(2,1)}), bf16[64,12,512]{2,1,0:T(8,128)(2,1)S(1)}, u32[]{:S(2)}, u32[]{:S(2)}) async-start(bf16[64,12,512]{2,1,0:T(8,128)(2,1)} %broadcast_in_dim.21), calls=%async_computation | async-start | bytes 2097152 | tf_op jit(solution)/shard_map/all_to_all | solution.py:34
  19.3 9.2 %collective-permute-start = (bf16[128,1,128]{0,2,1:T(8,128)(2,1)S(1)}, bf16[128,1,128]{0,2,1:T(8,128)(2,1)S(1)}, u32[]{:S(2)}, u32[]{:S(2)}) collective-permute-start(bf16[128,1,128]{0,2,1:T(8,128)(2,1)S(1)} %copy.74), channel_id=1, source_target_pairs={{0,4},{4,8},{8,12},{12,16},{16,20},{20,24},{24,28},{28,32},{32,36}... | collective-permute-start | bytes 98312 | tf_op jit(solution)/shard_map/ppermute | solution.py:19
  28.8 23.1 %copy-start.9 = (f32[8]{0:T(128)S(1)}, f32[8]{0:T(128)}, u32[]{:S(2)}) copy-start(f32[8]{0:T(128)} %param.13) | copy-start | bytes 100
  46.4 7.4 %collective-permute-start.1 = (bf16[64,12,512]{2,0,1:T(8,128)(2,1)S(1)}, bf16[64,12,512]{2,0,1:T(8,128)(2,1)S(1)}, u32[]{:S(2)}, u32[]{:S(2)}) collective-permute-start(bf16[64,12,512]{2,0,1:T(8,128)(2,1)S(1)} %copy.78), channel_id=1, source_target_pairs={{0,4},{4,0},{1,5},{5,1},{2,6},{6,2},{3,7},{7,3},{8,12},{12,8},{9,1... | collective-permute-start | bytes 2359304 | tf_op jit(solution)/shard_map/ppermute | solution.py:28
  56.2 2.1 copy-start.1
  56.2 8.7 %copy-start.5 = (s32[128,4]{0,1:T(4,128)S(1)}, s32[128,4]{0,1:T(4,128)}, u32[]{:S(2)}) copy-start(s32[128,4]{0,1:T(4,128)} %param.18) | copy-start | bytes 6148
  58.4 15.5 %collective-permute-start.2 = (bf16[128,1920]{1,0:T(8,128)(2,1)S(1)}, bf16[128,1920]{1,0:T(8,128)(2,1)S(1)}, u32[]{:S(2)}, u32[]{:S(2)}) collective-permute-start(bf16[128,1920]{1,0:T(8,128)(2,1)S(1)} %pad_maximum_fusion.4), channel_id=1, source_target_pairs={{0,1},{1,2},{2,3},{3,0},{4,5},{5,6},{6,7},{7,4},{8,9},{9,10},{10,1... | collective-permute-start | bytes 1474568 | tf_op jit(solution)/shard_map/ppermute | solution.py:125
  61.5 15.2 %collective-permute-start.3 = (bf16[128,1920]{1,0:T(8,128)(2,1)S(1)}, bf16[128,1920]{1,0:T(8,128)(2,1)S(1)}, u32[]{:S(2)}, u32[]{:S(2)}) collective-permute-start(bf16[128,1920]{1,0:T(8,128)(2,1)S(1)} %pad_maximum_fusion.4), channel_id=1, source_target_pairs={{0,3},{1,0},{2,1},{3,2},{4,7},{5,4},{6,5},{7,6},{8,11},{9,8},{10,9... | collective-permute-start | bytes 1474568 | tf_op jit(solution)/shard_map/ppermute | solution.py:126
  74.6 9.7 %collective-permute-start.4 = (bf16[64,1920]{1,0:T(8,128)(2,1)}, bf16[64,1920]{1,0:T(8,128)(2,1)}, u32[]{:S(2)}, u32[]{:S(2)}) collective-permute-start(bf16[64,1920]{1,0:T(8,128)(2,1)} %slice.134), channel_id=1, source_target_pairs={{0,1},{1,2},{2,3},{3,0},{4,5},{5,6},{6,7},{7,4},{8,9},{9,10},{10,1... | collective-permute-start | bytes 737288 | tf_op jit(solution)/shard_map/ppermute | solution.py:130
  76.8 8.5 %collective-permute-start.5 = (bf16[64,1920]{1,0:T(8,128)(2,1)S(1)}, bf16[64,1920]{1,0:T(8,128)(2,1)S(1)}, u32[]{:S(2)}, u32[]{:S(2)}) collective-permute-start(bf16[64,1920]{1,0:T(8,128)(2,1)S(1)} %slice.135), channel_id=1, source_target_pairs={{0,3},{1,0},{2,1},{3,2},{4,7},{5,4},{6,5},{7,6},{8,11},{9,8},{10,9... | collective-permute-start | bytes 737288 | tf_op jit(solution)/shard_map/ppermute | solution.py:131
  85.5 0.7 copy-start.7
  92.5 5.8 %collective-permute-start.6 = (bf16[64,12,384]{2,0,1:T(8,128)(2,1)S(1)}, bf16[64,12,384]{2,0,1:T(8,128)(2,1)S(1)}, u32[]{:S(2)}, u32[]{:S(2)}) collective-permute-start(bf16[64,12,384]{2,0,1:T(8,128)(2,1)S(1)} %bitcast.122), channel_id=1, source_target_pairs={{0,4},{4,0},{1,5},{5,1},{2,6},{6,2},{3,7},{7,3},{8,12},{12,8},{9,1... | collective-permute-start | bytes 1769480 | tf_op jit(solution)/shard_map/ppermute | solution.py:28
  139.6 28.5 %collective-permute-start.7 = (bf16[1536,384]{1,0:T(8,128)(2,1)S(1)}, bf16[1536,384]{1,0:T(8,128)(2,1)S(1)}, u32[]{:S(2)}, u32[]{:S(2)}) collective-permute-start(bf16[1536,384]{1,0:T(8,128)(2,1)S(1)} %reshape_reshape.7), channel_id=1, source_target_pairs={{0,1},{1,2},{2,3},{3,0},{4,5},{5,6},{6,7},{7,4},{8,9},{9,10},{10,1... | collective-permute-start | bytes 3538952 | tf_op jit(solution)/shard_map/ppermute | solution.py:172
  142.2 27.8 %collective-permute-start.8 = (bf16[1536,384]{1,0:T(8,128)(2,1)S(1)}, bf16[1536,384]{1,0:T(8,128)(2,1)S(1)}, u32[]{:S(2)}, u32[]{:S(2)}) collective-permute-start(bf16[1536,384]{1,0:T(8,128)(2,1)S(1)} %reshape_reshape.7), channel_id=1, source_target_pairs={{0,3},{1,0},{2,1},{3,2},{4,7},{5,4},{6,5},{7,6},{8,11},{9,8},{10,9... | collective-permute-start | bytes 3538952 | tf_op jit(solution)/shard_map/ppermute | solution.py:173
  168.1 14.2 %collective-permute-start.9 = (bf16[768,384]{1,0:T(8,128)(2,1)S(1)}, bf16[768,384]{1,0:T(8,128)(2,1)S(1)}, u32[]{:S(2)}, u32[]{:S(2)}) collective-permute-start(bf16[768,384]{1,0:T(8,128)(2,1)S(1)} %slice.140), channel_id=1, source_target_pairs={{0,1},{1,2},{2,3},{3,0},{4,5},{5,6},{6,7},{7,4},{8,9},{9,10},{10,1... | collective-permute-start | bytes 1769480 | tf_op jit(solution)/shard_map/ppermute | solution.py:174
  170.1 13.2 %collective-permute-start.10 = (bf16[768,384]{1,0:T(8,128)(2,1)S(1)}, bf16[768,384]{1,0:T(8,128)(2,1)S(1)}, u32[]{:S(2)}, u32[]{:S(2)}) collective-permute-start(bf16[768,384]{1,0:T(8,128)(2,1)S(1)} %slice.141), channel_id=1, source_target_pairs={{0,3},{1,0},{2,1},{3,2},{4,7},{5,4},{6,5},{7,6},{8,11},{9,8},{10,9... | collective-permute-start | bytes 1769480 | tf_op jit(solution)/shard_map/ppermute | solution.py:175
  188.6 14.1 %collective-permute-start.11 = (bf16[768,384]{1,0:T(8,128)(2,1)S(1)}, bf16[768,384]{1,0:T(8,128)(2,1)S(1)}, u32[]{:S(2)}, u32[]{:S(2)}) collective-permute-start(bf16[768,384]{1,0:T(8,128)(2,1)S(1)} %get-tuple-element.17), channel_id=1, source_target_pairs={{0,1},{1,2},{2,3},{3,0},{4,5},{5,6},{6,7},{7,4},{8,9},{9,10},{10,1... | collective-permute-start | bytes 1769480 | tf_op jit(solution)/shard_map/ppermute | solution.py:199
  190.6 14.3 %collective-permute-start.13 = (bf16[768,384]{1,0:T(8,128)(2,1)S(1)}, bf16[768,384]{1,0:T(8,128)(2,1)S(1)}, u32[]{:S(2)}, u32[]{:S(2)}) collective-permute-start(bf16[768,384]{1,0:T(8,128)(2,1)S(1)} %get-tuple-element.18), channel_id=1, source_target_pairs={{0,3},{1,0},{2,1},{3,2},{4,7},{5,4},{6,5},{7,6},{8,11},{9,8},{10,9... | collective-permute-start | bytes 1769480 | tf_op jit(solution)/shard_map/ppermute | solution.py:200
  203.0 25.1 %collective-permute-start.12 = (bf16[1536,384]{1,0:T(8,128)(2,1)S(1)}, bf16[1536,384]{1,0:T(8,128)(2,1)S(1)}, u32[]{:S(2)}, u32[]{:S(2)}) collective-permute-start(bf16[1536,384]{1,0:T(8,128)(2,1)S(1)} %pad_maximum_fusion.2), channel_id=1, source_target_pairs={{0,1},{1,2},{2,3},{3,0},{4,5},{5,6},{6,7},{7,4},{8,9},{9,10},{10,1... | collective-permute-start | bytes 3538952 | tf_op jit(solution)/shard_map/ppermute | solution.py:209
  205.2 24.1 %collective-permute-start.14 = (bf16[1536,384]{1,0:T(8,128)(2,1)S(1)}, bf16[1536,384]{1,0:T(8,128)(2,1)S(1)}, u32[]{:S(2)}, u32[]{:S(2)}) collective-permute-start(bf16[1536,384]{1,0:T(8,128)(2,1)S(1)} %pad_maximum_fusion.3), channel_id=1, source_target_pairs={{0,3},{1,0},{2,1},{3,2},{4,7},{5,4},{6,5},{7,6},{8,11},{9,8},{10,9... | collective-permute-start | bytes 3538952 | tf_op jit(solution)/shard_map/ppermute | solution.py:210
  231.0 24.9 %copy-start.6 = (f32[128,4]{0,1:T(4,128)S(1)}, f32[128,4]{0,1:T(4,128)}, u32[]{:S(2)}) copy-start(f32[128,4]{0,1:T(4,128)} %param.19) | copy-start | bytes 6148
  231.0 65.7 %all-to-all-start.2 = ((bf16[128,12,384]{2,1,0:T(8,128)(2,1)}), bf16[128,12,384]{2,1,0:T(8,128)(2,1)}, u32[]{:S(2)}, u32[]{:S(2)}) async-start(bf16[128,12,384]{2,1,0:T(8,128)(2,1)} %reshape.208), calls=%async_computation.2 | async-start | bytes 3145728 | tf_op jit(solution)/shard_map/all_to_all | solution.py:217
  301.0 0.9 copy-start.2
  301.0 0.9 copy-start.8
